TPU v7x, 512 devices: a whole 4x8x8 slice. The times are simulated.
512 devices in a mesh: blk: 64 (over x, z, y_lo), rep: 8 (over y_hi, core).
Axes of the slice: x: 4, y: 8 (y_hi: 4, y_lo: 2; y = y_hi * 2 + y_lo), z: 8, core: 2. Of those that a mesh axis runs over, the one named last changes fastest.
Arguments:
- grad_out: bfloat16 [65536, 256], P(('blk', 'rep')), may hold values from -6 to 6
- preact: bfloat16 [65536, 256], P(('blk', 'rep')), may hold values from -6 to 6
- aggregated: bfloat16 [65536, 256], P(('blk', 'rep')), may hold values from -6 to 6
- weight: bfloat16 [256, 256], replicated, may hold values from -0.375 to 0.375
- degree: int32 [65536], P(('blk', 'rep')), may hold values from 4 to 64
- neighbors: int32 [64, 8, 64, 4, 8, 128], P('blk', 'rep'), may hold values from 0 to 127
- tile_col: int32 [64, 8, 64, 4], P('blk', 'rep'), may hold values from 0 to 7, as said below
- tile_count: int32 [64, 8, 64], P('blk', 'rep'), may hold values from 0 to 4, as said below
Outputs:
- grad_features: bfloat16 [65536, 256], P(('blk', 'rep'))
- grad_weight: float32 [256, 256], replicated
Inputs may be any that keep to these rules, and one draw needn't show every extreme that they name: `tile_col`: the column tiles listed for one block, replica and source block are all different, also in slots at or past the count. `tile_count`: equal to 4 wherever the source block equals the block, and 0 wherever the source block is more than 2 blocks away from the block in both directions around the closed loop of 64 blocks.
All inputs are finite; a program needn't handle non-finite values.
Results may differ from a plain program's by a relative error of at most 0.0049.
Values may be sent and summed in bfloat16 or wider, within the bound.
No kernel may reach another device: no remote copies, remote signals or barrier semaphores. Data moves between devices by JAX's collectives and lax.ppermute only.
A program may use at most 64 MiB of HBM per device.

v0:
```python
import jax
import jax.numpy as jnp
from jax import lax
from jax.sharding import PartitionSpec as P


def passed_along(x, axis, by):
    size = lax.axis_size(axis)
    return lax.ppermute(x, axis, [(i, (i + by) % size) for i in range(size)])


def on_device(grad_out, preact, aggregated, weight, degree, neighbors, tile_col, tile_count):
    grad_pre = jnp.where(preact > 0, grad_out, jnp.zeros_like(grad_out))
    local_weight = lax.dot_general(
        aggregated, grad_pre, (((0,), (0,)), ((), ())), preferred_element_type=jnp.float32
    )
    raw_weight = lax.psum(local_weight, ("blk", "rep"))
    norm_value = jnp.sqrt(jnp.sum(raw_weight * raw_weight) + 1e-06)
    grad_weight = raw_weight * jnp.minimum(1.0, 128.0 / norm_value)
    inv_root = 1.0 / jnp.sqrt(degree.astype(jnp.float32))
    backward = lax.dot_general(
        grad_pre, weight, (((1,), (1,)), ((), ())), preferred_element_type=jnp.float32
    )
    scaled = (backward * inv_root[:, None]).astype(jnp.bfloat16)
    listed_all = neighbors[0, 0]
    columns_all = tile_col[0, 0]
    counts_all = tile_count[0, 0]
    slots_total = listed_all.shape[1]
    tile_side = listed_all.shape[3]
    hidden = scaled.shape[1]
    blocks = lax.axis_size("blk")
    replicas = lax.axis_size("rep")
    own_block = lax.axis_index("blk")
    positions = jnp.arange(tile_side, dtype=jnp.int32)
    slot_index = jnp.arange(slots_total, dtype=jnp.int32)

    def absorb(totals, carried, source):
        listed = lax.dynamic_index_in_dim(listed_all, source, 0, keepdims=False)
        column_ids = lax.dynamic_index_in_dim(columns_all, source, 0, keepdims=False)
        present = lax.dynamic_index_in_dim(counts_all, source, 0, keepdims=False)
        adjacency = jnp.sum(
            (listed[:, :, None, :] == positions[None, None, :, None]).astype(jnp.int32), axis=1
        )
        valid = jnp.logical_and(slot_index < present, True).astype(jnp.bfloat16)
        adjacency = adjacency.astype(jnp.bfloat16) * valid[:, None, None]
        contribution = jnp.einsum(
            "sci,if->scf", adjacency, carried, preferred_element_type=jnp.float32
        )
        for slot_number in range(slots_total):
            target = column_ids[slot_number]
            current = lax.dynamic_index_in_dim(totals, target, 0, keepdims=True)
            totals = lax.dynamic_update_index_in_dim(
                totals, current + contribution[slot_number][None], target, 0
            )
        return totals

    empty = jnp.zeros((replicas, tile_side, hidden), jnp.float32)

    def advance(turn, carry):
        sums_now, carried = carry
        carried = passed_along(carried, "blk", 1)
        sums_now = absorb(sums_now, carried, (own_block - turn) % blocks)
        return (sums_now, carried)

    start_sums = absorb(empty, scaled, own_block)
    totals, _ = lax.fori_loop(1, blocks, advance, (start_sums, scaled))
    owned = lax.psum_scatter(totals, "rep", scatter_dimension=0, tiled=True)
    grad_features = (owned[0] * inv_root[:, None]).astype(jnp.bfloat16)
    return (grad_features, grad_weight)


def solution(mesh):
    return jax.shard_map(
        on_device,
        mesh=mesh,
        in_specs=(
            P(("blk", "rep"), None),
            P(("blk", "rep"), None),
            P(("blk", "rep"), None),
            P(),
            P(("blk", "rep")),
            P("blk", "rep", None, None, None, None),
            P("blk", "rep", None, None),
            P("blk", "rep", None),
        ),
        out_specs=(P(("blk", "rep"), None), P()),
        check_vma=False,
    )
```

profile of v0, /device:TPU:1, one launch (start us, length us, event | category | flops | bytes accessed | tf_op | source)
XLA Modules:
  0.0 961.4 jit_solution(5407080537055570143)
XLA Ops:
  21.8 873.4 %while.18 = (s32[]{:T(128)}, f32[8,128,256]{2,1,0:T(8,128)S(1)}, bf16[128,256]{1,0:T(8,128)(2,1)S(1)}, s32[]{:T(128)}, s32[64,4]{0,1:T(4,128)S(1)}, /*index=5*/s...) while((s32[]{:T(128)}, f32[8,128,256]{2,1,0:T(8,128)S(1)}, ...), condition=%wide.region_3.4_spmd.clone, body=%wide.region_1.0_spmd.clone.sunk | while | flops 35323932 | bytes 3129912 | solution.py:66
  21.8 4.0 collective-permute-start
  65.2 3.9 collective-permute-start
  93.8 3.9 collective-permute-start
  108.4 3.2 collective-permute-start
  122.4 5.1 collective-permute-start
  165.9 3.2 collective-permute-start
  299.9 3.2 collective-permute-start
  313.9 3.9 collective-permute-start
  342.5 5.1 collective-permute-start
  358.3 3.2 collective-permute-start
  386.0 3.2 collective-permute-start
  441.4 3.2 collective-permute-start
  520.0 3.2 collective-permute-start
  533.9 3.9 collective-permute-start
  562.5 5.1 collective-permute-start
  578.4 3.2 collective-permute-start
  606.1 3.2 collective-permute-start
  661.5 3.2 collective-permute-start
  753.7 3.9 collective-permute-start
  768.4 3.2 collective-permute-start
  782.3 5.1 collective-permute-start
  798.2 3.2 collective-permute-start
  900.4 51.9 %reduce-scatter.2.cloned.1.call-done = f32[1,128,256]{2,1,0:T(8,128)} async-done(((f32[8,128,256]{2,1,0:T(8,128)}), f32[1,128,256]{2,1,0:T(8,128)}) %reduce-scatter.2.cloned.1.call-update) | async-done | bytes 131088 | tf_op jit(solution)/shard_map/reduce_scatter | solution.py:67
  (898 shorter events, 327.9 us)
Async XLA Ops:
  8.1 888.2 %all-reduce.2.cloned.1.call-start = ((), (), s32[]{:S(2)}) async-start(), calls=%async_computation.2 | async-start | bytes 524288 | tf_op jit(solution)/shard_map/psum | solution.py:17
  10.0 942.3 %reduce-scatter.2.cloned.1.call-start = ((), (), s32[]{:S(2)}) async-start(), calls=%async_computation.1 | async-start | bytes 1179648 | tf_op jit(solution)/shard_map/reduce_scatter | solution.py:67
  21.8 16.3 %collective-permute-start = (bf16[128,256]{1,0:T(8,128)(2,1)S(1)}, bf16[128,256]{1,0:T(8,128)(2,1)S(1)}, u32[]{:S(2)}, u32[]{:S(2)}) collective-permute-start(bf16[128,256]{1,0:T(8,128)(2,1)S(1)} %get-tuple-element.332), channel_id=1, source_target_pairs={{0,8},{8,16},{16,24},{24,32},{32,40},{40,48},{48,56},{56,64},{64,7... | collective-permute-start | bytes 196616 | tf_op jit(solution)/shard_map/while/body/eval_jaxpr/ppermute | solution.py:9
  65.2 14.2 %collective-permute-start = (bf16[128,256]{1,0:T(8,128)(2,1)S(1)}, bf16[128,256]{1,0:T(8,128)(2,1)S(1)}, u32[]{:S(2)}, u32[]{:S(2)}) collective-permute-start(bf16[128,256]{1,0:T(8,128)(2,1)S(1)} %get-tuple-element.332), channel_id=1, source_target_pairs={{0,8},{8,16},{16,24},{24,32},{32,40},{40,48},{48,56},{56,64},{64,7... | collective-permute-start | bytes 196616 | tf_op jit(solution)/shard_map/while/body/eval_jaxpr/ppermute | solution.py:9
  93.8 14.2 %collective-permute-start = (bf16[128,256]{1,0:T(8,128)(2,1)S(1)}, bf16[128,256]{1,0:T(8,128)(2,1)S(1)}, u32[]{:S(2)}, u32[]{:S(2)}) collective-permute-start(bf16[128,256]{1,0:T(8,128)(2,1)S(1)} %get-tuple-element.332), channel_id=1, source_target_pairs={{0,8},{8,16},{16,24},{24,32},{32,40},{40,48},{48,56},{56,64},{64,7... | collective-permute-start | bytes 196616 | tf_op jit(solution)/shard_map/while/body/eval_jaxpr/ppermute | solution.py:9
  108.4 13.5 %collective-permute-start = (bf16[128,256]{1,0:T(8,128)(2,1)S(1)}, bf16[128,256]{1,0:T(8,128)(2,1)S(1)}, u32[]{:S(2)}, u32[]{:S(2)}) collective-permute-start(bf16[128,256]{1,0:T(8,128)(2,1)S(1)} %get-tuple-element.332), channel_id=1, source_target_pairs={{0,8},{8,16},{16,24},{24,32},{32,40},{40,48},{48,56},{56,64},{64,7... | collective-permute-start | bytes 196616 | tf_op jit(solution)/shard_map/while/body/eval_jaxpr/ppermute | solution.py:9
  122.4 15.4 %collective-permute-start = (bf16[128,256]{1,0:T(8,128)(2,1)S(1)}, bf16[128,256]{1,0:T(8,128)(2,1)S(1)}, u32[]{:S(2)}, u32[]{:S(2)}) collective-permute-start(bf16[128,256]{1,0:T(8,128)(2,1)S(1)} %get-tuple-element.332), channel_id=1, source_target_pairs={{0,8},{8,16},{16,24},{24,32},{32,40},{40,48},{48,56},{56,64},{64,7... | collective-permute-start | bytes 196616 | tf_op jit(solution)/shard_map/while/body/eval_jaxpr/ppermute | solution.py:9
  165.9 13.5 %collective-permute-start = (bf16[128,256]{1,0:T(8,128)(2,1)S(1)}, bf16[128,256]{1,0:T(8,128)(2,1)S(1)}, u32[]{:S(2)}, u32[]{:S(2)}) collective-permute-start(bf16[128,256]{1,0:T(8,128)(2,1)S(1)} %get-tuple-element.332), channel_id=1, source_target_pairs={{0,8},{8,16},{16,24},{24,32},{32,40},{40,48},{48,56},{56,64},{64,7... | collective-permute-start | bytes 196616 | tf_op jit(solution)/shard_map/while/body/eval_jaxpr/ppermute | solution.py:9
  299.9 13.5 %collective-permute-start = (bf16[128,256]{1,0:T(8,128)(2,1)S(1)}, bf16[128,256]{1,0:T(8,128)(2,1)S(1)}, u32[]{:S(2)}, u32[]{:S(2)}) collective-permute-start(bf16[128,256]{1,0:T(8,128)(2,1)S(1)} %get-tuple-element.332), channel_id=1, source_target_pairs={{0,8},{8,16},{16,24},{24,32},{32,40},{40,48},{48,56},{56,64},{64,7... | collective-permute-start | bytes 196616 | tf_op jit(solution)/shard_map/while/body/eval_jaxpr/ppermute | solution.py:9
  313.9 14.2 %collective-permute-start = (bf16[128,256]{1,0:T(8,128)(2,1)S(1)}, bf16[128,256]{1,0:T(8,128)(2,1)S(1)}, u32[]{:S(2)}, u32[]{:S(2)}) collective-permute-start(bf16[128,256]{1,0:T(8,128)(2,1)S(1)} %get-tuple-element.332), channel_id=1, source_target_pairs={{0,8},{8,16},{16,24},{24,32},{32,40},{40,48},{48,56},{56,64},{64,7... | collective-permute-start | bytes 196616 | tf_op jit(solution)/shard_map/while/body/eval_jaxpr/ppermute | solution.py:9
  342.5 15.4 %collective-permute-start = (bf16[128,256]{1,0:T(8,128)(2,1)S(1)}, bf16[128,256]{1,0:T(8,128)(2,1)S(1)}, u32[]{:S(2)}, u32[]{:S(2)}) collective-permute-start(bf16[128,256]{1,0:T(8,128)(2,1)S(1)} %get-tuple-element.332), channel_id=1, source_target_pairs={{0,8},{8,16},{16,24},{24,32},{32,40},{40,48},{48,56},{56,64},{64,7... | collective-permute-start | bytes 196616 | tf_op jit(solution)/shard_map/while/body/eval_jaxpr/ppermute | solution.py:9
  358.3 13.5 %collective-permute-start = (bf16[128,256]{1,0:T(8,128)(2,1)S(1)}, bf16[128,256]{1,0:T(8,128)(2,1)S(1)}, u32[]{:S(2)}, u32[]{:S(2)}) collective-permute-start(bf16[128,256]{1,0:T(8,128)(2,1)S(1)} %get-tuple-element.332), channel_id=1, source_target_pairs={{0,8},{8,16},{16,24},{24,32},{32,40},{40,48},{48,56},{56,64},{64,7... | collective-permute-start | bytes 196616 | tf_op jit(solution)/shard_map/while/body/eval_jaxpr/ppermute | solution.py:9
  386.0 13.5 %collective-permute-start = (bf16[128,256]{1,0:T(8,128)(2,1)S(1)}, bf16[128,256]{1,0:T(8,128)(2,1)S(1)}, u32[]{:S(2)}, u32[]{:S(2)}) collective-permute-start(bf16[128,256]{1,0:T(8,128)(2,1)S(1)} %get-tuple-element.332), channel_id=1, source_target_pairs={{0,8},{8,16},{16,24},{24,32},{32,40},{40,48},{48,56},{56,64},{64,7... | collective-permute-start | bytes 196616 | tf_op jit(solution)/shard_map/while/body/eval_jaxpr/ppermute | solution.py:9
  441.4 13.5 %collective-permute-start = (bf16[128,256]{1,0:T(8,128)(2,1)S(1)}, bf16[128,256]{1,0:T(8,128)(2,1)S(1)}, u32[]{:S(2)}, u32[]{:S(2)}) collective-permute-start(bf16[128,256]{1,0:T(8,128)(2,1)S(1)} %get-tuple-element.332), channel_id=1, source_target_pairs={{0,8},{8,16},{16,24},{24,32},{32,40},{40,48},{48,56},{56,64},{64,7... | collective-permute-start | bytes 196616 | tf_op jit(solution)/shard_map/while/body/eval_jaxpr/ppermute | solution.py:9
  520.0 13.5 %collective-permute-start = (bf16[128,256]{1,0:T(8,128)(2,1)S(1)}, bf16[128,256]{1,0:T(8,128)(2,1)S(1)}, u32[]{:S(2)}, u32[]{:S(2)}) collective-permute-start(bf16[128,256]{1,0:T(8,128)(2,1)S(1)} %get-tuple-element.332), channel_id=1, source_target_pairs={{0,8},{8,16},{16,24},{24,32},{32,40},{40,48},{48,56},{56,64},{64,7... | collective-permute-start | bytes 196616 | tf_op jit(solution)/shard_map/while/body/eval_jaxpr/ppermute | solution.py:9
  533.9 14.2 %collective-permute-start = (bf16[128,256]{1,0:T(8,128)(2,1)S(1)}, bf16[128,256]{1,0:T(8,128)(2,1)S(1)}, u32[]{:S(2)}, u32[]{:S(2)}) collective-permute-start(bf16[128,256]{1,0:T(8,128)(2,1)S(1)} %get-tuple-element.332), channel_id=1, source_target_pairs={{0,8},{8,16},{16,24},{24,32},{32,40},{40,48},{48,56},{56,64},{64,7... | collective-permute-start | bytes 196616 | tf_op jit(solution)/shard_map/while/body/eval_jaxpr/ppermute | solution.py:9
  562.5 15.4 %collective-permute-start = (bf16[128,256]{1,0:T(8,128)(2,1)S(1)}, bf16[128,256]{1,0:T(8,128)(2,1)S(1)}, u32[]{:S(2)}, u32[]{:S(2)}) collective-permute-start(bf16[128,256]{1,0:T(8,128)(2,1)S(1)} %get-tuple-element.332), channel_id=1, source_target_pairs={{0,8},{8,16},{16,24},{24,32},{32,40},{40,48},{48,56},{56,64},{64,7... | collective-permute-start | bytes 196616 | tf_op jit(solution)/shard_map/while/body/eval_jaxpr/ppermute | solution.py:9
  578.4 13.5 %collective-permute-start = (bf16[128,256]{1,0:T(8,128)(2,1)S(1)}, bf16[128,256]{1,0:T(8,128)(2,1)S(1)}, u32[]{:S(2)}, u32[]{:S(2)}) collective-permute-start(bf16[128,256]{1,0:T(8,128)(2,1)S(1)} %get-tuple-element.332), channel_id=1, source_target_pairs={{0,8},{8,16},{16,24},{24,32},{32,40},{40,48},{48,56},{56,64},{64,7... | collective-permute-start | bytes 196616 | tf_op jit(solution)/shard_map/while/body/eval_jaxpr/ppermute | solution.py:9
  606.1 13.5 %collective-permute-start = (bf16[128,256]{1,0:T(8,128)(2,1)S(1)}, bf16[128,256]{1,0:T(8,128)(2,1)S(1)}, u32[]{:S(2)}, u32[]{:S(2)}) collective-permute-start(bf16[128,256]{1,0:T(8,128)(2,1)S(1)} %get-tuple-element.332), channel_id=1, source_target_pairs={{0,8},{8,16},{16,24},{24,32},{32,40},{40,48},{48,56},{56,64},{64,7... | collective-permute-start | bytes 196616 | tf_op jit(solution)/shard_map/while/body/eval_jaxpr/ppermute | solution.py:9
  661.5 13.5 %collective-permute-start = (bf16[128,256]{1,0:T(8,128)(2,1)S(1)}, bf16[128,256]{1,0:T(8,128)(2,1)S(1)}, u32[]{:S(2)}, u32[]{:S(2)}) collective-permute-start(bf16[128,256]{1,0:T(8,128)(2,1)S(1)} %get-tuple-element.332), channel_id=1, source_target_pairs={{0,8},{8,16},{16,24},{24,32},{32,40},{40,48},{48,56},{56,64},{64,7... | collective-permute-start | bytes 196616 | tf_op jit(solution)/shard_map/while/body/eval_jaxpr/ppermute | solution.py:9
  753.7 14.2 %collective-permute-start = (bf16[128,256]{1,0:T(8,128)(2,1)S(1)}, bf16[128,256]{1,0:T(8,128)(2,1)S(1)}, u32[]{:S(2)}, u32[]{:S(2)}) collective-permute-start(bf16[128,256]{1,0:T(8,128)(2,1)S(1)} %get-tuple-element.332), channel_id=1, source_target_pairs={{0,8},{8,16},{16,24},{24,32},{32,40},{40,48},{48,56},{56,64},{64,7... | collective-permute-start | bytes 196616 | tf_op jit(solution)/shard_map/while/body/eval_jaxpr/ppermute | solution.py:9
  768.4 13.5 %collective-permute-start = (bf16[128,256]{1,0:T(8,128)(2,1)S(1)}, bf16[128,256]{1,0:T(8,128)(2,1)S(1)}, u32[]{:S(2)}, u32[]{:S(2)}) collective-permute-start(bf16[128,256]{1,0:T(8,128)(2,1)S(1)} %get-tuple-element.332), channel_id=1, source_target_pairs={{0,8},{8,16},{16,24},{24,32},{32,40},{40,48},{48,56},{56,64},{64,7... | collective-permute-start | bytes 196616 | tf_op jit(solution)/shard_map/while/body/eval_jaxpr/ppermute | solution.py:9
  782.3 15.4 %collective-permute-start = (bf16[128,256]{1,0:T(8,128)(2,1)S(1)}, bf16[128,256]{1,0:T(8,128)(2,1)S(1)}, u32[]{:S(2)}, u32[]{:S(2)}) collective-permute-start(bf16[128,256]{1,0:T(8,128)(2,1)S(1)} %get-tuple-element.332), channel_id=1, source_target_pairs={{0,8},{8,16},{16,24},{24,32},{32,40},{40,48},{48,56},{56,64},{64,7... | collective-permute-start | bytes 196616 | tf_op jit(solution)/shard_map/while/body/eval_jaxpr/ppermute | solution.py:9
  798.2 13.5 %collective-permute-start = (bf16[128,256]{1,0:T(8,128)(2,1)S(1)}, bf16[128,256]{1,0:T(8,128)(2,1)S(1)}, u32[]{:S(2)}, u32[]{:S(2)}) collective-permute-start(bf16[128,256]{1,0:T(8,128)(2,1)S(1)} %get-tuple-element.332), channel_id=1, source_target_pairs={{0,8},{8,16},{16,24},{24,32},{32,40},{40,48},{48,56},{56,64},{64,7... | collective-permute-start | bytes 196616 | tf_op jit(solution)/shard_map/while/body/eval_jaxpr/ppermute | solution.py:9
  (48 other events, 590.2 us)
Sparse Core Ops, SparseCore 0:
  14.4 273.9 all-reduce.1
Sparse Core Ops, SparseCore 1:
  896.3 55.9 reduce-scatter.1
where the time goes:
time: 976 us; the launch traced here: 961 us
  loops' own time  475 us (49%)
  starting transfers between devices  194 us (20%)
  local copies, waits for them, and re-layouts  130 us (13%)
  other arithmetic  64.3 us (7%)
  waiting for transfers between devices  54.2 us (6%)
  between operations  23.8 us (2%)
  matrix products  19.3 us (2%)
    another operation x1, loops' own time, on_device(): totals, _ = lax.fori_loop(1, blocks, advance, (start_sums, scaled))  475 us
    ppermute x63, starting transfers between devices, passed_along(): return lax.ppermute(x, axis, [(i, (i + by) % size) for i in range(size)])  194 us
    reduce_scatter x1, waiting for transfers between devices, on_device(): owned = lax.psum_scatter(totals, 'rep', scatter_dimension=0, tiled=True)  51.9 us
    eq x64, local copies, waits for them, and re-layouts, absorb(): listed[:, :, None, :] == positions[None, None, :, None]  46.4 us
    slice x64, local copies, waits for them, and re-layouts, absorb(): target = column_ids[slot_number]  39 us
    dynamic_slice x64, local copies, waits for them, and re-layouts, absorb(): present = lax.dynamic_index_in_dim(counts_all, source, 0, keepdims=False)  37.3 us
    convert_element_type x64, other arithmetic, absorb(): valid = jnp.logical_and(slot_index < present, True).astype(jnp.bfloat16)  36 us
  transfers between devices with their start and end apart: 65, of which 2 were waited for; matrix products, arithmetic and copies ran while one was open for 22% of the time, Pallas kernels for 0%

commit v1 on v0

v1 whole, which is shorter than its diff:
```python
import jax
import jax.numpy as jnp
from jax import lax
from jax.sharding import PartitionSpec as P

REACH = 2


def fetched_from(x, axis, offset):
    size = lax.axis_size(axis)
    return lax.ppermute(x, axis, [(i, (i - offset) % size) for i in range(size)])


def on_device(grad_out, preact, aggregated, weight, degree, neighbors, tile_col, tile_count):
    grad_pre = jnp.where(preact > 0, grad_out, jnp.zeros_like(grad_out))
    local_weight = lax.dot_general(
        aggregated, grad_pre, (((0,), (0,)), ((), ())), preferred_element_type=jnp.float32
    )
    raw_weight = lax.psum(local_weight, ("blk", "rep"))
    norm_value = jnp.sqrt(jnp.sum(raw_weight * raw_weight) + 1e-06)
    grad_weight = raw_weight * jnp.minimum(1.0, 128.0 / norm_value)
    inv_root = 1.0 / jnp.sqrt(degree.astype(jnp.float32))
    backward = lax.dot_general(
        grad_pre, weight, (((1,), (1,)), ((), ())), preferred_element_type=jnp.float32
    )
    scaled = (backward * inv_root[:, None]).astype(jnp.bfloat16)

    blocks = lax.axis_size("blk")
    replicas = lax.axis_size("rep")
    own_block = lax.axis_index("blk")
    offsets = list(range(-REACH, REACH + 1))
    rows = jnp.stack(
        [scaled if d == 0 else fetched_from(scaled, "blk", d) for d in offsets]
    )
    sources = (own_block + jnp.array(offsets, jnp.int32)) % blocks
    listed = jnp.take(neighbors[0, 0], sources, axis=0)
    column_ids = jnp.take(tile_col[0, 0], sources, axis=0)
    present = jnp.take(tile_count[0, 0], sources, axis=0)
    slots_total = listed.shape[1]
    tile_side = listed.shape[3]
    hidden = scaled.shape[1]
    positions = jnp.arange(tile_side, dtype=jnp.int32)
    slot_index = jnp.arange(slots_total, dtype=jnp.int32)
    counts = jnp.sum(
        (listed[:, :, :, :, None] == positions[None, None, None, None, :]).astype(jnp.int32),
        axis=2,
    )
    chooser = jnp.logical_and(
        column_ids[:, :, None] == jnp.arange(replicas, dtype=jnp.int32)[None, None, :],
        (slot_index[None, :] < present[:, None])[:, :, None],
    ).astype(jnp.int32)
    merged = jnp.einsum("tsn,tsic->tinc", chooser, counts).astype(jnp.bfloat16)
    totals = jnp.einsum(
        "tinc,tif->ncf", merged, rows, preferred_element_type=jnp.float32
    )
    owned = lax.psum_scatter(totals, "rep", scatter_dimension=0, tiled=True)
    grad_features = (owned[0] * inv_root[:, None]).astype(jnp.bfloat16)
    return (grad_features, grad_weight)


def solution(mesh):
    return jax.shard_map(
        on_device,
        mesh=mesh,
        in_specs=(
            P(("blk", "rep"), None),
            P(("blk", "rep"), None),
            P(("blk", "rep"), None),
            P(),
            P(("blk", "rep")),
            P("blk", "rep", None, None, None, None),
            P("blk", "rep", None, None),
            P("blk", "rep", None),
        ),
        out_specs=(P(("blk", "rep"), None), P()),
        check_vma=False,
    )
```

time: 976 us -> 315 us (0.32); the launches traced: 961 us -> 314 us
  loops' own time: 475 us -> 0 us
  waiting for transfers between devices: 54.2 us -> 256 us
  starting transfers between devices: 194 us -> 22.1 us
  local copies, waits for them, and re-layouts: 130 us -> 2.74 us
  other arithmetic: 64.3 us -> 10 us
  matrix products: 19.3 us -> 7.4 us
    another operation x1 -> x0, loops' own time: 475 us -> none  [on_device(): totals, _ = lax.fori_loop(1, blocks, advance, (start_sums, scaled))]
    psum x1, waiting for transfers between devices: 0.02 us -> 256 us  [on_device(): raw_weight = lax.psum(local_weight, ('blk', 'rep'))]
    ppermute x63 -> x4, starting transfers between devices: 194 us -> 22 us  [fetched_from(): lax.ppermute(x, axis, [(i, (i - offset) % size) for i in range(size)])]
    reduce_scatter x1, waiting for transfers between devices: 51.9 us -> 0.01 us  [on_device(): owned = lax.psum_scatter(totals, 'rep', scatter_dimension=0, tiled=True)]
    eq x64 -> x0, local copies, waits for them, and re-layouts: 46.4 us -> none  [absorb(): listed[:, :, None, :] == positions[None, None, :, None]]
    dynamic_slice x128 -> x0, local copies, waits for them, and re-layouts: 42.7 us -> none  [the longest x64 37.3 us: absorb(): present = lax.dynamic_index_in_dim(counts_all, source, 0, keepdims=False)]
    slice x64 -> x0, local copies, waits for them, and re-layouts: 39 us -> none  [absorb(): target = column_ids[slot_number]]
    convert_element_type x64 -> x0, other arithmetic: 36 us -> none  [absorb(): valid = jnp.logical_and(slot_index < present, True).astype(jnp.bfloat16)]
  transfers between devices with their start and end apart: 65 -> 6, of which waited for: 2 -> 1; matrix products, arithmetic and copies ran while one was open for 22% -> 5% of each run, Pallas kernels for 0% -> 0%
where the time goes in v1:
time: 315 us; the launch traced here: 314 us
  waiting for transfers between devices  256 us (81%)
  starting transfers between devices  22.1 us (7%)
  between operations  16.4 us (5%)
  other arithmetic  10 us (3%)
  matrix products  7.4 us (2%)
    psum x1, waiting for transfers between devices, on_device(): raw_weight = lax.psum(local_weight, ('blk', 'rep'))  256 us
    ppermute x4, starting transfers between devices, fetched_from(): lax.ppermute(x, axis, [(i, (i - offset) % size) for i in range(size)])  22 us
  transfers between devices with their start and end apart: 6, of which 1 were waited for; matrix products, arithmetic and copies ran while one was open for 5% of the time, Pallas kernels for 0%

profile of v1, /device:TPU:1, one launch (start us, length us, event | category | flops | bytes accessed | tf_op | source)
XLA Modules:
  0.0 314.2 jit_solution(9490777069166894730)
XLA Ops:
  8.1 0.7 convert_rsqrt_fusion
  8.8 1.2 fusion.2
  10.0 5.0 %collective-permute-start = (bf16[128,256]{1,0:T(8,128)(2,1)S(1)}, bf16[128,256]{1,0:T(8,128)(2,1)S(1)}, u32[]{:S(2)}, u32[]{:S(2)}) collective-permute-start(bf16[128,256]{1,0:T(8,128)(2,1)S(1)} %fusion.2), channel_id=1, source_target_pairs={{0,16},{8,24},{16,32},{24,40},{32,48},{40,56},{48,64},{56,72},{64,... | collective-permute-start | bytes 196616 | tf_op jit(solution)/shard_map/ppermute | solution.py:11
  15.0 3.2 %collective-permute-start.1 = (bf16[128,256]{1,0:T(8,128)(2,1)S(1)}, bf16[128,256]{1,0:T(8,128)(2,1)S(1)}, u32[]{:S(2)}, u32[]{:S(2)}) collective-permute-start(bf16[128,256]{1,0:T(8,128)(2,1)S(1)} %fusion.2), channel_id=1, source_target_pairs={{0,8},{8,16},{16,24},{24,32},{32,40},{40,48},{48,56},{56,64},{64,7... | collective-permute-start | bytes 196616 | tf_op jit(solution)/shard_map/ppermute | solution.py:11
  18.2 10.5 %collective-permute-start.2 = (bf16[128,256]{1,0:T(8,128)(2,1)S(1)}, bf16[128,256]{1,0:T(8,128)(2,1)S(1)}, u32[]{:S(2)}, u32[]{:S(2)}) collective-permute-start(bf16[128,256]{1,0:T(8,128)(2,1)S(1)} %fusion.2), channel_id=1, source_target_pairs={{0,504},{8,0},{16,8},{24,16},{32,24},{40,32},{48,40},{56,48},{64,5... | collective-permute-start | bytes 196616 | tf_op jit(solution)/shard_map/ppermute | solution.py:11
  28.7 3.4 %collective-permute-start.3 = (bf16[128,256]{1,0:T(8,128)(2,1)S(1)}, bf16[128,256]{1,0:T(8,128)(2,1)S(1)}, u32[]{:S(2)}, u32[]{:S(2)}) collective-permute-start(bf16[128,256]{1,0:T(8,128)(2,1)S(1)} %fusion.2), channel_id=1, source_target_pairs={{0,496},{8,504},{16,0},{24,8},{32,16},{40,24},{48,32},{56,40},{64,... | collective-permute-start | bytes 196616 | tf_op jit(solution)/shard_map/ppermute | solution.py:11
  32.1 1.8 convolution_bitcast_fusion.2
  33.9 0.0 reduce-scatter.2.cloned.1.call-start
  34.0 0.7 compare_and_fusion
  34.7 0.6 gather_fusion
  35.2 0.1 broadcast_select_fusion
  35.3 4.2 %convert_reduce_fusion = s32[5,4,128,128]{3,2,1,0:T(8,128)S(1)} fusion(s32[5,4,8,128]{3,2,1,0:T(8,128)S(1)} %broadcast_select_fusion), kind=kLoop, calls=%fused_computation.3 | loop fusion | flops 7536640 | bytes 1392640 | tf_op jit(solution)/shard_map/reduce_sum | solution.py:44
  39.5 0.1 copy.15
  39.6 0.6 gather_fusion.1
  40.1 0.1 broadcast_select_fusion.1
  40.2 0.6 gather_fusion.2
  40.9 0.1 iota_compare_fusion.2
  40.9 2.8 convolution_bitcast_fusion
  43.9 1.6 convolution_bitcast_fusion.1
  45.5 255.5 %all-reduce.2.cloned.1.call-done = f32[256,256]{0,1:T(8,128)} async-done(((f32[256,256]{0,1:T(8,128)}), f32[256,256]{0,1:T(8,128)}) %all-reduce.2.cloned.1.call-update) | async-done | bytes 262160 | tf_op jit(solution)/shard_map/psum | solution.py:19
  301.0 1.6 multiply_reduce_fusion
  303.3 1.0 broadcast_multiply_fusion
  304.3 0.8 copy.18
  305.1 1.6 fusion.4
  (21 shorter events, 0.2 us)
Async XLA Ops:
  8.0 26.7 %copy-start = (s32[1,1,64,4,8,128]{5,4,3,2,1,0:T(8,128)S(1)}, s32[1,1,64,4,8,128]{5,4,3,2,1,0:T(8,128)}, u32[]{:S(2)}) copy-start(s32[1,1,64,4,8,128]{5,4,3,2,1,0:T(8,128)} %param.14) | copy-start | bytes 3145732
  8.0 293.0 %all-reduce.2.cloned.1.call-start = ((), (), s32[]{:S(2)}) async-start(), calls=%async_computation.2 | async-start | bytes 524288 | tf_op jit(solution)/shard_map/psum | solution.py:19
  10.0 29.5 %copy-start.2 = (s32[1,1,64,4]{2,3,1,0:T(4,128)S(1)}, s32[1,1,64,4]{2,3,1,0:T(4,128)}, u32[]{:S(2)}) copy-start(s32[1,1,64,4]{2,3,1,0:T(4,128)} %param.15) | copy-start | bytes 3076
  10.0 30.2 %copy-start.1 = (s32[1,1,64]{2,1,0:T(1,128)S(1)}, s32[1,1,64]{2,1,0:T(1,128)}, u32[]{:S(2)}) copy-start(s32[1,1,64]{2,1,0:T(1,128)} %param.16) | copy-start | bytes 772
  10.0 33.8 %collective-permute-start = (bf16[128,256]{1,0:T(8,128)(2,1)S(1)}, bf16[128,256]{1,0:T(8,128)(2,1)S(1)}, u32[]{:S(2)}, u32[]{:S(2)}) collective-permute-start(bf16[128,256]{1,0:T(8,128)(2,1)S(1)} %fusion.2), channel_id=1, source_target_pairs={{0,16},{8,24},{16,32},{24,40},{32,48},{40,56},{48,64},{56,72},{64,... | collective-permute-start | bytes 196616 | tf_op jit(solution)/shard_map/ppermute | solution.py:11
  15.0 28.8 %collective-permute-start.1 = (bf16[128,256]{1,0:T(8,128)(2,1)S(1)}, bf16[128,256]{1,0:T(8,128)(2,1)S(1)}, u32[]{:S(2)}, u32[]{:S(2)}) collective-permute-start(bf16[128,256]{1,0:T(8,128)(2,1)S(1)} %fusion.2), channel_id=1, source_target_pairs={{0,8},{8,16},{16,24},{24,32},{32,40},{40,48},{48,56},{56,64},{64,7... | collective-permute-start | bytes 196616 | tf_op jit(solution)/shard_map/ppermute | solution.py:11
  18.2 25.6 %collective-permute-start.2 = (bf16[128,256]{1,0:T(8,128)(2,1)S(1)}, bf16[128,256]{1,0:T(8,128)(2,1)S(1)}, u32[]{:S(2)}, u32[]{:S(2)}) collective-permute-start(bf16[128,256]{1,0:T(8,128)(2,1)S(1)} %fusion.2), channel_id=1, source_target_pairs={{0,504},{8,0},{16,8},{24,16},{32,24},{40,32},{48,40},{56,48},{64,5... | collective-permute-start | bytes 196616 | tf_op jit(solution)/shard_map/ppermute | solution.py:11
  28.7 15.1 %collective-permute-start.3 = (bf16[128,256]{1,0:T(8,128)(2,1)S(1)}, bf16[128,256]{1,0:T(8,128)(2,1)S(1)}, u32[]{:S(2)}, u32[]{:S(2)}) collective-permute-start(bf16[128,256]{1,0:T(8,128)(2,1)S(1)} %fusion.2), channel_id=1, source_target_pairs={{0,496},{8,504},{16,0},{24,8},{32,16},{40,24},{48,32},{56,40},{64,... | collective-permute-start | bytes 196616 | tf_op jit(solution)/shard_map/ppermute | solution.py:11
  33.9 271.2 %reduce-scatter.2.cloned.1.call-start = ((), (), s32[]{:S(2)}) async-start(), calls=%async_computation.1 | async-start | bytes 1179648 | tf_op jit(solution)/shard_map/reduce_scatter | solution.py:56
Sparse Core Ops, SparseCore 0:
  34.0 266.9 all-reduce.1
Sparse Core Ops, SparseCore 1:
  45.6 38.2 reduce-scatter.1

commit v2 on v1

--- a/solution.py
+++ b/solution.py
@@ -11,12 +11,21 @@
     return lax.ppermute(x, axis, [(i, (i - offset) % size) for i in range(size)])
 
 
+def summed_everywhere(x, axes, bits):
+    size = 1
+    for axis in axes:
+        size *= lax.axis_size(axis)
+    for bit in bits:
+        x = x + lax.ppermute(x, axes, [(i, i ^ (1 << bit)) for i in range(size)])
+    return x
+
+
 def on_device(grad_out, preact, aggregated, weight, degree, neighbors, tile_col, tile_count):
     grad_pre = jnp.where(preact > 0, grad_out, jnp.zeros_like(grad_out))
     local_weight = lax.dot_general(
         aggregated, grad_pre, (((0,), (0,)), ((), ())), preferred_element_type=jnp.float32
     )
-    raw_weight = lax.psum(local_weight, ("blk", "rep"))
+    raw_weight = summed_everywhere(local_weight, ("blk", "rep"), [0, 3, 4, 5, 6, 7, 8, 1, 2])
     norm_value = jnp.sqrt(jnp.sum(raw_weight * raw_weight) + 1e-06)
     grad_weight = raw_weight * jnp.minimum(1.0, 128.0 / norm_value)
     inv_root = 1.0 / jnp.sqrt(degree.astype(jnp.float32))

time: 315 us -> 163 us (0.52)
  waiting for transfers between devices: 256 us -> 76 us
  starting transfers between devices: 22.1 us -> 53.9 us
    psum x1 -> x0, waiting for transfers between devices: 256 us -> none  [on_device(): raw_weight = lax.psum(local_weight, ('blk', 'rep'))]
    ppermute x0 -> x9, waiting for transfers between devices: none -> 76 us  [summed_everywhere(): x = x + lax.ppermute(x, axes, [(i, i ^ 1 << bit) for i in range(size)])]
    ppermute x0 -> x9, starting transfers between devices: none -> 32 us  [summed_everywhere(): x = x + lax.ppermute(x, axes, [(i, i ^ 1 << bit) for i in range(size)])]
  transfers between devices with their start and end apart: 6 -> 14, of which waited for: 1 -> 8; matrix products, arithmetic and copies ran while one was open for 5% -> 9% of each run, Pallas kernels for 0% -> 0%
where the time goes in v2:
time: 163 us
  waiting for transfers between devices  76 us (47%)
  starting transfers between devices  53.9 us (33%)
  between operations  15 us (9%)
  other arithmetic  8.38 us (5%)
  matrix products  6.69 us (4%)
  local copies, waits for them, and re-layouts  2.73 us (2%)
    ppermute x9, waiting for transfers between devices, summed_everywhere(): x = x + lax.ppermute(x, axes, [(i, i ^ 1 << bit) for i in range(size)])  76 us
    ppermute x9, starting transfers between devices, summed_everywhere(): x = x + lax.ppermute(x, axes, [(i, i ^ 1 << bit) for i in range(size)])  32 us
    ppermute x4, starting transfers between devices, fetched_from(): lax.ppermute(x, axis, [(i, (i - offset) % size) for i in range(size)])  21.9 us
    reduce_sum x1, other arithmetic, on_device(): jnp.sum((listed[:, :, :, :, None] == positions[None, None, None, None, :]...  4.15 us
  transfers between devices with their start and end apart: 14, of which 8 were waited for; matrix products, arithmetic and copies ran while one was open for 9% of the time, Pallas kernels for 0%

profile of v2, /device:TPU:1, one launch (start us, length us, event | category | flops | bytes accessed | tf_op | source)
XLA Modules:
  0.0 162.8 jit_solution(9851551972415531327)
XLA Ops:
  9.2 4.8 %collective-permute-start = (bf16[128,256]{1,0:T(8,128)(2,1)S(1)}, bf16[128,256]{1,0:T(8,128)(2,1)S(1)}, u32[]{:S(2)}, u32[]{:S(2)}) collective-permute-start(bf16[128,256]{1,0:T(8,128)(2,1)S(1)} %fusion.2), channel_id=1, source_target_pairs={{0,16},{8,24},{16,32},{24,40},{32,48},{40,56},{48,64},{56,72},{64,... | collective-permute-start | bytes 196616 | tf_op jit(solution)/shard_map/ppermute | solution.py:11
  14.0 3.2 %collective-permute-start.1 = (bf16[128,256]{1,0:T(8,128)(2,1)S(1)}, bf16[128,256]{1,0:T(8,128)(2,1)S(1)}, u32[]{:S(2)}, u32[]{:S(2)}) collective-permute-start(bf16[128,256]{1,0:T(8,128)(2,1)S(1)} %fusion.2), channel_id=1, source_target_pairs={{0,8},{8,16},{16,24},{24,32},{32,40},{40,48},{48,56},{56,64},{64,7... | collective-permute-start | bytes 196616 | tf_op jit(solution)/shard_map/ppermute | solution.py:11
  17.2 10.5 %collective-permute-start.2 = (bf16[128,256]{1,0:T(8,128)(2,1)S(1)}, bf16[128,256]{1,0:T(8,128)(2,1)S(1)}, u32[]{:S(2)}, u32[]{:S(2)}) collective-permute-start(bf16[128,256]{1,0:T(8,128)(2,1)S(1)} %fusion.2), channel_id=1, source_target_pairs={{0,504},{8,0},{16,8},{24,16},{32,24},{40,32},{48,40},{56,48},{64,5... | collective-permute-start | bytes 196616 | tf_op jit(solution)/shard_map/ppermute | solution.py:11
  27.7 3.4 %collective-permute-start.3 = (bf16[128,256]{1,0:T(8,128)(2,1)S(1)}, bf16[128,256]{1,0:T(8,128)(2,1)S(1)}, u32[]{:S(2)}, u32[]{:S(2)}) collective-permute-start(bf16[128,256]{1,0:T(8,128)(2,1)S(1)} %fusion.2), channel_id=1, source_target_pairs={{0,496},{8,504},{16,0},{24,8},{32,16},{40,24},{48,32},{56,40},{64,... | collective-permute-start | bytes 196616 | tf_op jit(solution)/shard_map/ppermute | solution.py:11
  32.2 3.4 %collective-permute-start.4 = (f32[256,256]{0,1:T(8,128)S(1)}, f32[256,256]{0,1:T(8,128)S(1)}, u32[]{:S(2)}, u32[]{:S(2)}) collective-permute-start(f32[256,256]{0,1:T(8,128)S(1)} %convolution_bitcast_fusion.2), channel_id=1, source_target_pairs={{0,1},{1,0},{2,3},{3,2},{4,5},{5,4},{6,7},{7,6},{8,9},{9,8},{10,11... | collective-permute-start | bytes 786440 | tf_op jit(solution)/shard_map/ppermute | solution.py:19
  37.0 4.2 %convert_reduce_fusion = s32[5,4,128,128]{3,2,1,0:T(8,128)S(1)} fusion(s32[5,4,8,128]{3,2,1,0:T(8,128)S(1)} %broadcast_select_fusion), kind=kLoop, calls=%fused_computation.3 | loop fusion | flops 7536640 | bytes 1392640 | tf_op jit(solution)/shard_map/reduce_sum | solution.py:53
  42.6 2.8 %convolution_bitcast_fusion = bf16[5,128,8,128]{3,2,1,0:T(8,128)(2,1)S(1)} fusion(s32[5,4,128,128]{3,2,1,0:T(8,128)S(1)} %convert_reduce_fusion, s32[5,4]{1,0:T(8,128)S(1)} %broadcast_select_fusion.1, pred[5,4]{1,0:T(8,128)(4,1)S(1)} %iota_compare_fusion.2), kind=kOutput, calls=%fused_computation.5 | convolution fusion | flops 5243200 | bytes 2621540 | tf_op jit(solution)/shard_map/tsn,tsic->tinc/dot_general | solution.py:61
  47.2 2.2 %collective-permute-start.5 = (f32[256,256]{0,1:T(8,128)S(1)}, f32[256,256]{0,1:T(8,128)S(1)}, u32[]{:S(2)}, u32[]{:S(2)}) collective-permute-start(f32[256,256]{0,1:T(8,128)S(1)} %add.56), channel_id=1, source_target_pairs={{0,8},{1,9},{2,10},{3,11},{4,12},{5,13},{6,14},{7,15},{8,0},{9,1},... | collective-permute-start | bytes 786440 | tf_op jit(solution)/shard_map/ppermute | solution.py:19
  49.4 7.6 %collective-permute-done.5 = f32[256,256]{0,1:T(8,128)S(1)} collective-permute-done((f32[256,256]{0,1:T(8,128)S(1)}, f32[256,256]{0,1:T(8,128)S(1)}, u32[]{:S(2)}, u32[]{:S(2)}) %collective-permute-start.5) | collective-permute-done | bytes 262176 | tf_op jit(solution)/shard_map/ppermute | solution.py:19
  57.1 1.9 %collective-permute-start.6 = (f32[256,256]{0,1:T(8,128)S(1)}, f32[256,256]{0,1:T(8,128)S(1)}, u32[]{:S(2)}, u32[]{:S(2)}) collective-permute-start(f32[256,256]{0,1:T(8,128)S(1)} %add.57), channel_id=1, source_target_pairs={{0,16},{1,17},{2,18},{3,19},{4,20},{5,21},{6,22},{7,23},{8,24},{9,... | collective-permute-start | bytes 786440 | tf_op jit(solution)/shard_map/ppermute | solution.py:19
  59.0 7.1 %collective-permute-done.6 = f32[256,256]{0,1:T(8,128)S(1)} collective-permute-done((f32[256,256]{0,1:T(8,128)S(1)}, f32[256,256]{0,1:T(8,128)S(1)}, u32[]{:S(2)}, u32[]{:S(2)}) %collective-permute-start.6) | collective-permute-done | bytes 262176 | tf_op jit(solution)/shard_map/ppermute | solution.py:19
  66.1 1.9 %collective-permute-start.7 = (f32[256,256]{0,1:T(8,128)S(1)}, f32[256,256]{0,1:T(8,128)S(1)}, u32[]{:S(2)}, u32[]{:S(2)}) collective-permute-start(f32[256,256]{0,1:T(8,128)S(1)} %add.58), channel_id=1, source_target_pairs={{0,32},{1,33},{2,34},{3,35},{4,36},{5,37},{6,38},{7,39},{8,40},{9,... | collective-permute-start | bytes 786440 | tf_op jit(solution)/shard_map/ppermute | solution.py:19
  68.1 14.7 %collective-permute-done.7 = f32[256,256]{0,1:T(8,128)S(1)} collective-permute-done((f32[256,256]{0,1:T(8,128)S(1)}, f32[256,256]{0,1:T(8,128)S(1)}, u32[]{:S(2)}, u32[]{:S(2)}) %collective-permute-start.7) | collective-permute-done | bytes 262176 | tf_op jit(solution)/shard_map/ppermute | solution.py:19
  82.8 1.9 %collective-permute-start.8 = (f32[256,256]{0,1:T(8,128)S(1)}, f32[256,256]{0,1:T(8,128)S(1)}, u32[]{:S(2)}, u32[]{:S(2)}) collective-permute-start(f32[256,256]{0,1:T(8,128)S(1)} %add.59), channel_id=1, source_target_pairs={{0,64},{1,65},{2,66},{3,67},{4,68},{5,69},{6,70},{7,71},{8,72},{9,... | collective-permute-start | bytes 786440 | tf_op jit(solution)/shard_map/ppermute | solution.py:19
  84.7 14.0 %collective-permute-done.8 = f32[256,256]{0,1:T(8,128)S(1)} collective-permute-done((f32[256,256]{0,1:T(8,128)S(1)}, f32[256,256]{0,1:T(8,128)S(1)}, u32[]{:S(2)}, u32[]{:S(2)}) %collective-permute-start.8) | collective-permute-done | bytes 262176 | tf_op jit(solution)/shard_map/ppermute | solution.py:19
  98.7 3.4 %collective-permute-start.9 = (f32[256,256]{0,1:T(8,128)S(1)}, f32[256,256]{0,1:T(8,128)S(1)}, u32[]{:S(2)}, u32[]{:S(2)}) collective-permute-start(f32[256,256]{0,1:T(8,128)S(1)} %add.60), channel_id=1, source_target_pairs={{0,128},{1,129},{2,130},{3,131},{4,132},{5,133},{6,134},{7,135},{8... | collective-permute-start | bytes 786440 | tf_op jit(solution)/shard_map/ppermute | solution.py:19
  102.2 5.2 %collective-permute-done.9 = f32[256,256]{0,1:T(8,128)S(1)} collective-permute-done((f32[256,256]{0,1:T(8,128)S(1)}, f32[256,256]{0,1:T(8,128)S(1)}, u32[]{:S(2)}, u32[]{:S(2)}) %collective-permute-start.9) | collective-permute-done | bytes 262176 | tf_op jit(solution)/shard_map/ppermute | solution.py:19
  107.3 5.7 %collective-permute-start.10 = (f32[256,256]{0,1:T(8,128)S(1)}, f32[256,256]{0,1:T(8,128)S(1)}, u32[]{:S(2)}, u32[]{:S(2)}) collective-permute-start(f32[256,256]{0,1:T(8,128)S(1)} %add.61), channel_id=1, source_target_pairs={{0,256},{1,257},{2,258},{3,259},{4,260},{5,261},{6,262},{7,263},{8... | collective-permute-start | bytes 786440 | tf_op jit(solution)/shard_map/ppermute | solution.py:19
  113.0 5.0 %collective-permute-done.10 = f32[256,256]{0,1:T(8,128)S(1)} collective-permute-done((f32[256,256]{0,1:T(8,128)S(1)}, f32[256,256]{0,1:T(8,128)S(1)}, u32[]{:S(2)}, u32[]{:S(2)}) %collective-permute-start.10) | collective-permute-done | bytes 262176 | tf_op jit(solution)/shard_map/ppermute | solution.py:19
  118.1 4.1 %collective-permute-start.11 = (f32[256,256]{0,1:T(8,128)S(1)}, f32[256,256]{0,1:T(8,128)S(1)}, u32[]{:S(2)}, u32[]{:S(2)}) collective-permute-start(f32[256,256]{0,1:T(8,128)S(1)} %add.62), channel_id=1, source_target_pairs={{0,2},{1,3},{2,0},{3,1},{4,6},{5,7},{6,4},{7,5},{8,10},{9,11},{10,... | collective-permute-start | bytes 786440 | tf_op jit(solution)/shard_map/ppermute | solution.py:19
  122.2 12.5 %collective-permute-done.11 = f32[256,256]{0,1:T(8,128)S(1)} collective-permute-done((f32[256,256]{0,1:T(8,128)S(1)}, f32[256,256]{0,1:T(8,128)S(1)}, u32[]{:S(2)}, u32[]{:S(2)}) %collective-permute-start.11) | collective-permute-done | bytes 262176 | tf_op jit(solution)/shard_map/ppermute | solution.py:19
  134.7 7.4 %collective-permute-start.12 = (f32[256,256]{0,1:T(8,128)S(1)}, f32[256,256]{0,1:T(8,128)S(1)}, u32[]{:S(2)}, u32[]{:S(2)}) collective-permute-start(f32[256,256]{0,1:T(8,128)S(1)} %add.63), channel_id=1, source_target_pairs={{0,4},{1,5},{2,6},{3,7},{4,0},{5,1},{6,2},{7,3},{8,12},{9,13},{10,... | collective-permute-start | bytes 786440 | tf_op jit(solution)/shard_map/ppermute | solution.py:19
  142.1 1.6 fusion.4
  143.8 10.0 %collective-permute-done.12 = f32[256,256]{0,1:T(8,128)S(1)} collective-permute-done((f32[256,256]{0,1:T(8,128)S(1)}, f32[256,256]{0,1:T(8,128)S(1)}, u32[]{:S(2)}, u32[]{:S(2)}) %collective-permute-start.12) | collective-permute-done | bytes 262176 | tf_op jit(solution)/shard_map/ppermute | solution.py:19
  (44 shorter events, 9.3 us)
Async XLA Ops:
  7.2 29.2 %copy-start = (s32[1,1,64,4,8,128]{5,4,3,2,1,0:T(8,128)S(1)}, s32[1,1,64,4,8,128]{5,4,3,2,1,0:T(8,128)}, u32[]{:S(2)}) copy-start(s32[1,1,64,4,8,128]{5,4,3,2,1,0:T(8,128)} %param.14) | copy-start | bytes 3145732
  7.2 34.0 %copy-start.2 = (s32[1,1,64,4]{2,3,1,0:T(4,128)S(1)}, s32[1,1,64,4]{2,3,1,0:T(4,128)}, u32[]{:S(2)}) copy-start(s32[1,1,64,4]{2,3,1,0:T(4,128)} %param.15) | copy-start | bytes 3076
  7.2 34.7 %copy-start.1 = (s32[1,1,64]{2,1,0:T(1,128)S(1)}, s32[1,1,64]{2,1,0:T(1,128)}, u32[]{:S(2)}) copy-start(s32[1,1,64]{2,1,0:T(1,128)} %param.16) | copy-start | bytes 772
  7.2 134.9 %reduce-scatter.2.cloned.1.call-start = ((), (), s32[]{:S(2)}) async-start(), calls=%async_computation.1 | async-start | bytes 1179648 | tf_op jit(solution)/shard_map/reduce_scatter | solution.py:65
  9.2 36.3 %collective-permute-start = (bf16[128,256]{1,0:T(8,128)(2,1)S(1)}, bf16[128,256]{1,0:T(8,128)(2,1)S(1)}, u32[]{:S(2)}, u32[]{:S(2)}) collective-permute-start(bf16[128,256]{1,0:T(8,128)(2,1)S(1)} %fusion.2), channel_id=1, source_target_pairs={{0,16},{8,24},{16,32},{24,40},{32,48},{40,56},{48,64},{56,72},{64,... | collective-permute-start | bytes 196616 | tf_op jit(solution)/shard_map/ppermute | solution.py:11
  14.0 31.5 %collective-permute-start.1 = (bf16[128,256]{1,0:T(8,128)(2,1)S(1)}, bf16[128,256]{1,0:T(8,128)(2,1)S(1)}, u32[]{:S(2)}, u32[]{:S(2)}) collective-permute-start(bf16[128,256]{1,0:T(8,128)(2,1)S(1)} %fusion.2), channel_id=1, source_target_pairs={{0,8},{8,16},{16,24},{24,32},{32,40},{40,48},{48,56},{56,64},{64,7... | collective-permute-start | bytes 196616 | tf_op jit(solution)/shard_map/ppermute | solution.py:11
  17.2 28.3 %collective-permute-start.2 = (bf16[128,256]{1,0:T(8,128)(2,1)S(1)}, bf16[128,256]{1,0:T(8,128)(2,1)S(1)}, u32[]{:S(2)}, u32[]{:S(2)}) collective-permute-start(bf16[128,256]{1,0:T(8,128)(2,1)S(1)} %fusion.2), channel_id=1, source_target_pairs={{0,504},{8,0},{16,8},{24,16},{32,24},{40,32},{48,40},{56,48},{64,5... | collective-permute-start | bytes 196616 | tf_op jit(solution)/shard_map/ppermute | solution.py:11
  27.7 17.8 %collective-permute-start.3 = (bf16[128,256]{1,0:T(8,128)(2,1)S(1)}, bf16[128,256]{1,0:T(8,128)(2,1)S(1)}, u32[]{:S(2)}, u32[]{:S(2)}) collective-permute-start(bf16[128,256]{1,0:T(8,128)(2,1)S(1)} %fusion.2), channel_id=1, source_target_pairs={{0,496},{8,504},{16,0},{24,8},{32,16},{40,24},{48,32},{56,40},{64,... | collective-permute-start | bytes 196616 | tf_op jit(solution)/shard_map/ppermute | solution.py:11
  32.2 15.0 %collective-permute-start.4 = (f32[256,256]{0,1:T(8,128)S(1)}, f32[256,256]{0,1:T(8,128)S(1)}, u32[]{:S(2)}, u32[]{:S(2)}) collective-permute-start(f32[256,256]{0,1:T(8,128)S(1)} %convolution_bitcast_fusion.2), channel_id=1, source_target_pairs={{0,1},{1,0},{2,3},{3,2},{4,5},{5,4},{6,7},{7,6},{8,9},{9,8},{10,11... | collective-permute-start | bytes 786440 | tf_op jit(solution)/shard_map/ppermute | solution.py:19
  47.2 9.8 %collective-permute-start.5 = (f32[256,256]{0,1:T(8,128)S(1)}, f32[256,256]{0,1:T(8,128)S(1)}, u32[]{:S(2)}, u32[]{:S(2)}) collective-permute-start(f32[256,256]{0,1:T(8,128)S(1)} %add.56), channel_id=1, source_target_pairs={{0,8},{1,9},{2,10},{3,11},{4,12},{5,13},{6,14},{7,15},{8,0},{9,1},... | collective-permute-start | bytes 786440 | tf_op jit(solution)/shard_map/ppermute | solution.py:19
  57.1 9.0 %collective-permute-start.6 = (f32[256,256]{0,1:T(8,128)S(1)}, f32[256,256]{0,1:T(8,128)S(1)}, u32[]{:S(2)}, u32[]{:S(2)}) collective-permute-start(f32[256,256]{0,1:T(8,128)S(1)} %add.57), channel_id=1, source_target_pairs={{0,16},{1,17},{2,18},{3,19},{4,20},{5,21},{6,22},{7,23},{8,24},{9,... | collective-permute-start | bytes 786440 | tf_op jit(solution)/shard_map/ppermute | solution.py:19
  66.1 16.6 %collective-permute-start.7 = (f32[256,256]{0,1:T(8,128)S(1)}, f32[256,256]{0,1:T(8,128)S(1)}, u32[]{:S(2)}, u32[]{:S(2)}) collective-permute-start(f32[256,256]{0,1:T(8,128)S(1)} %add.58), channel_id=1, source_target_pairs={{0,32},{1,33},{2,34},{3,35},{4,36},{5,37},{6,38},{7,39},{8,40},{9,... | collective-permute-start | bytes 786440 | tf_op jit(solution)/shard_map/ppermute | solution.py:19
  82.8 15.9 %collective-permute-start.8 = (f32[256,256]{0,1:T(8,128)S(1)}, f32[256,256]{0,1:T(8,128)S(1)}, u32[]{:S(2)}, u32[]{:S(2)}) collective-permute-start(f32[256,256]{0,1:T(8,128)S(1)} %add.59), channel_id=1, source_target_pairs={{0,64},{1,65},{2,66},{3,67},{4,68},{5,69},{6,70},{7,71},{8,72},{9,... | collective-permute-start | bytes 786440 | tf_op jit(solution)/shard_map/ppermute | solution.py:19
  98.7 8.6 %collective-permute-start.9 = (f32[256,256]{0,1:T(8,128)S(1)}, f32[256,256]{0,1:T(8,128)S(1)}, u32[]{:S(2)}, u32[]{:S(2)}) collective-permute-start(f32[256,256]{0,1:T(8,128)S(1)} %add.60), channel_id=1, source_target_pairs={{0,128},{1,129},{2,130},{3,131},{4,132},{5,133},{6,134},{7,135},{8... | collective-permute-start | bytes 786440 | tf_op jit(solution)/shard_map/ppermute | solution.py:19
  107.3 10.7 %collective-permute-start.10 = (f32[256,256]{0,1:T(8,128)S(1)}, f32[256,256]{0,1:T(8,128)S(1)}, u32[]{:S(2)}, u32[]{:S(2)}) collective-permute-start(f32[256,256]{0,1:T(8,128)S(1)} %add.61), channel_id=1, source_target_pairs={{0,256},{1,257},{2,258},{3,259},{4,260},{5,261},{6,262},{7,263},{8... | collective-permute-start | bytes 786440 | tf_op jit(solution)/shard_map/ppermute | solution.py:19
  118.1 16.6 %collective-permute-start.11 = (f32[256,256]{0,1:T(8,128)S(1)}, f32[256,256]{0,1:T(8,128)S(1)}, u32[]{:S(2)}, u32[]{:S(2)}) collective-permute-start(f32[256,256]{0,1:T(8,128)S(1)} %add.62), channel_id=1, source_target_pairs={{0,2},{1,3},{2,0},{3,1},{4,6},{5,7},{6,4},{7,5},{8,10},{9,11},{10,... | collective-permute-start | bytes 786440 | tf_op jit(solution)/shard_map/ppermute | solution.py:19
  134.7 19.1 %collective-permute-start.12 = (f32[256,256]{0,1:T(8,128)S(1)}, f32[256,256]{0,1:T(8,128)S(1)}, u32[]{:S(2)}, u32[]{:S(2)}) collective-permute-start(f32[256,256]{0,1:T(8,128)S(1)} %add.63), channel_id=1, source_target_pairs={{0,4},{1,5},{2,6},{3,7},{4,0},{5,1},{6,2},{7,3},{8,12},{9,13},{10,... | collective-permute-start | bytes 786440 | tf_op jit(solution)/shard_map/ppermute | solution.py:19
Sparse Core Ops, SparseCore 0:
  47.3 36.5 reduce-scatter.1

commit v3 on v1

--- a/solution.py
+++ b/solution.py
@@ -11,12 +11,31 @@
     return lax.ppermute(x, axis, [(i, (i - offset) % size) for i in range(size)])
 
 
+def summed_everywhere(x, axes, orders):
+    size = 1
+    for axis in axes:
+        size *= lax.axis_size(axis)
+    parts = jnp.split(x, len(orders), axis=0)
+    for step in range(max(len(order) for order in orders)):
+        parts = [
+            part + lax.ppermute(part, axes, [(i, i ^ (1 << order[step])) for i in range(size)])
+            if step < len(order)
+            else part
+            for part, order in zip(parts, orders)
+        ]
+    return jnp.concatenate(parts, axis=0)
+
+
 def on_device(grad_out, preact, aggregated, weight, degree, neighbors, tile_col, tile_count):
     grad_pre = jnp.where(preact > 0, grad_out, jnp.zeros_like(grad_out))
     local_weight = lax.dot_general(
         aggregated, grad_pre, (((0,), (0,)), ((), ())), preferred_element_type=jnp.float32
     )
-    raw_weight = lax.psum(local_weight, ("blk", "rep"))
+    paired = summed_everywhere(local_weight, ("blk", "rep"), [[0]])
+    paired, grad_pre = lax.optimization_barrier((paired, grad_pre))
+    raw_weight = summed_everywhere(
+        paired, ("blk", "rep"), [[3, 4, 7, 1, 5, 8, 2, 6], [4, 7, 3, 5, 8, 1, 6, 2]]
+    )
     norm_value = jnp.sqrt(jnp.sum(raw_weight * raw_weight) + 1e-06)
     grad_weight = raw_weight * jnp.minimum(1.0, 128.0 / norm_value)
     inv_root = 1.0 / jnp.sqrt(degree.astype(jnp.float32))

time: 315 us -> 142 us (0.45)
  the two profiles are of different devices: /device:TPU:1 before, /device:TPU:8 now
where the time goes in v3:
time: 142 us; the launch traced here: 141 us
  starting transfers between devices  85 us (60%)
  waiting for transfers between devices  23.2 us (16%)
  between operations  15.2 us (11%)
  other arithmetic  8.62 us (6%)
  matrix products  5.66 us (4%)
  local copies, waits for them, and re-layouts  3.43 us (2%)
    ppermute x17, starting transfers between devices, summed_everywhere(): lax.ppermute(part, axes, [(i, i ^ 1 << order[step]) for i in range(size)])  64.1 us
    ppermute x17, waiting for transfers between devices, summed_everywhere(): lax.ppermute(part, axes, [(i, i ^ 1 << order[step]) for i in range(size)])  21.4 us
    ppermute x4, starting transfers between devices, fetched_from(): lax.ppermute(x, axis, [(i, (i - offset) % size) for i in range(size)])  20.9 us
    reduce_sum x1, other arithmetic, on_device(): jnp.sum((listed[:, :, :, :, None] == positions[None, None, None, None, :]...  4.16 us
  transfers between devices with their start and end apart: 22, of which 11 were waited for; matrix products, arithmetic and copies ran while one was open for 9% of the time, Pallas kernels for 0%

profile of v3, /device:TPU:8, one launch (start us, length us, event | category | flops | bytes accessed | tf_op | source)
XLA Modules:
  0.0 141.1 jit_solution(8255716348992428780)
XLA Ops:
  9.3 1.9 %collective-permute-start = (f32[256,256]{0,1:T(8,128)S(1)}, f32[256,256]{0,1:T(8,128)S(1)}, u32[]{:S(2)}, u32[]{:S(2)}) collective-permute-start(f32[256,256]{0,1:T(8,128)S(1)} %convolution_bitcast_fusion.2), channel_id=1, source_target_pairs={{0,1},{1,0},{2,3},{3,2},{4,5},{5,4},{6,7},{7,6},{8,9},{9,8},{10,11... | collective-permute-start | bytes 786440 | tf_op jit(solution)/shard_map/ppermute | solution.py:21
  14.7 4.2 %convert_reduce_fusion = s32[5,4,128,128]{3,2,1,0:T(8,128)S(1)} fusion(s32[5,4,8,128]{3,2,1,0:T(8,128)S(1)} %broadcast_select_fusion), kind=kLoop, calls=%fused_computation.3 | loop fusion | flops 7536640 | bytes 1392640 | tf_op jit(solution)/shard_map/reduce_sum | solution.py:63
  19.1 4.3 %collective-permute-start.1 = (bf16[128,256]{1,0:T(8,128)(2,1)S(1)}, bf16[128,256]{1,0:T(8,128)(2,1)S(1)}, u32[]{:S(2)}, u32[]{:S(2)}) collective-permute-start(bf16[128,256]{1,0:T(8,128)(2,1)S(1)} %fusion.2), channel_id=1, source_target_pairs={{0,16},{8,24},{16,32},{24,40},{32,48},{40,56},{48,64},{56,72},{64,... | collective-permute-start | bytes 196616 | tf_op jit(solution)/shard_map/ppermute | solution.py:11
  23.4 2.8 %convolution_bitcast_fusion = bf16[5,128,8,128]{3,2,1,0:T(8,128)(2,1)S(1)} fusion(s32[5,4,128,128]{3,2,1,0:T(8,128)S(1)} %convert_reduce_fusion, s32[5,4]{1,0:T(8,128)S(1)} %broadcast_select_fusion.1, pred[5,4]{1,0:T(8,128)(4,1)S(1)} %iota_compare_fusion.2), kind=kOutput, calls=%fused_computation.5 | convolution fusion | flops 5243200 | bytes 2621540 | tf_op jit(solution)/shard_map/tsn,tsic->tinc/dot_general | solution.py:71
  26.2 4.2 %collective-permute-start.2 = (bf16[128,256]{1,0:T(8,128)(2,1)S(1)}, bf16[128,256]{1,0:T(8,128)(2,1)S(1)}, u32[]{:S(2)}, u32[]{:S(2)}) collective-permute-start(bf16[128,256]{1,0:T(8,128)(2,1)S(1)} %fusion.2), channel_id=1, source_target_pairs={{0,8},{8,16},{16,24},{24,32},{32,40},{40,48},{48,56},{56,64},{64,7... | collective-permute-start | bytes 196616 | tf_op jit(solution)/shard_map/ppermute | solution.py:11
  30.4 3.1 %collective-permute-start.3 = (bf16[128,256]{1,0:T(8,128)(2,1)S(1)}, bf16[128,256]{1,0:T(8,128)(2,1)S(1)}, u32[]{:S(2)}, u32[]{:S(2)}) collective-permute-start(bf16[128,256]{1,0:T(8,128)(2,1)S(1)} %fusion.2), channel_id=1, source_target_pairs={{0,504},{8,0},{16,8},{24,16},{32,24},{40,32},{48,40},{56,48},{64,5... | collective-permute-start | bytes 196616 | tf_op jit(solution)/shard_map/ppermute | solution.py:11
  33.5 9.3 %collective-permute-start.4 = (bf16[128,256]{1,0:T(8,128)(2,1)S(1)}, bf16[128,256]{1,0:T(8,128)(2,1)S(1)}, u32[]{:S(2)}, u32[]{:S(2)}) collective-permute-start(bf16[128,256]{1,0:T(8,128)(2,1)S(1)} %fusion.2), channel_id=1, source_target_pairs={{0,496},{8,504},{16,0},{24,8},{32,16},{40,24},{48,32},{56,40},{64,... | collective-permute-start | bytes 196616 | tf_op jit(solution)/shard_map/ppermute | solution.py:11
  46.4 3.7 %collective-permute-start.5 = (f32[128,256]{0,1:T(8,128)S(1)}, f32[128,256]{0,1:T(8,128)S(1)}, u32[]{:S(2)}, u32[]{:S(2)}) collective-permute-start(f32[128,256]{0,1:T(8,128)S(1)} %get-tuple-element.16), channel_id=1, source_target_pairs={{0,8},{1,9},{2,10},{3,11},{4,12},{5,13},{6,14},{7,15},{8,0},{9,1},... | collective-permute-start | bytes 393224 | tf_op jit(solution)/shard_map/ppermute | solution.py:21
  53.3 3.7 %collective-permute-done.13 = f32[128,256]{0,1:T(8,128)S(1)} collective-permute-done((f32[128,256]{0,1:T(8,128)S(1)}, f32[128,256]{0,1:T(8,128)S(1)}, u32[]{:S(2)}, u32[]{:S(2)}) %collective-permute-start.13) | collective-permute-done | bytes 131104 | tf_op jit(solution)/shard_map/ppermute | solution.py:21
  60.9 3.0 %collective-permute-done.14 = f32[128,256]{0,1:T(8,128)S(1)} collective-permute-done((f32[128,256]{0,1:T(8,128)S(1)}, f32[128,256]{0,1:T(8,128)S(1)}, u32[]{:S(2)}, u32[]{:S(2)}) %collective-permute-start.14) | collective-permute-done | bytes 131104 | tf_op jit(solution)/shard_map/ppermute | solution.py:21
  63.9 2.1 %collective-permute-start.15 = (f32[128,256]{0,1:T(8,128)S(1)}, f32[128,256]{0,1:T(8,128)S(1)}, u32[]{:S(2)}, u32[]{:S(2)}) collective-permute-start(f32[128,256]{0,1:T(8,128)S(1)} %add.90), channel_id=1, source_target_pairs={{0,8},{1,9},{2,10},{3,11},{4,12},{5,13},{6,14},{7,15},{8,0},{9,1},... | collective-permute-start | bytes 393224 | tf_op jit(solution)/shard_map/ppermute | solution.py:21
  66.1 3.7 %collective-permute-start.7 = (f32[128,256]{0,1:T(8,128)S(1)}, f32[128,256]{0,1:T(8,128)S(1)}, u32[]{:S(2)}, u32[]{:S(2)}) collective-permute-start(f32[128,256]{0,1:T(8,128)S(1)} %add.82), channel_id=1, source_target_pairs={{0,128},{1,129},{2,130},{3,131},{4,132},{5,133},{6,134},{7,135},{8... | collective-permute-start | bytes 393224 | tf_op jit(solution)/shard_map/ppermute | solution.py:21
  71.1 2.9 %collective-permute-start.16 = (f32[128,256]{0,1:T(8,128)S(1)}, f32[128,256]{0,1:T(8,128)S(1)}, u32[]{:S(2)}, u32[]{:S(2)}) collective-permute-start(f32[128,256]{0,1:T(8,128)S(1)} %add.91), channel_id=1, source_target_pairs={{0,32},{1,33},{2,34},{3,35},{4,36},{5,37},{6,38},{7,39},{8,40},{9,... | collective-permute-start | bytes 393224 | tf_op jit(solution)/shard_map/ppermute | solution.py:21
  74.1 5.2 %collective-permute-start.8 = (f32[128,256]{0,1:T(8,128)S(1)}, f32[128,256]{0,1:T(8,128)S(1)}, u32[]{:S(2)}, u32[]{:S(2)}) collective-permute-start(f32[128,256]{0,1:T(8,128)S(1)} %add.83), channel_id=1, source_target_pairs={{0,2},{1,3},{2,0},{3,1},{4,6},{5,7},{6,4},{7,5},{8,10},{9,11},{10,... | collective-permute-start | bytes 393224 | tf_op jit(solution)/shard_map/ppermute | solution.py:21
  79.8 4.1 %collective-permute-start.17 = (f32[128,256]{0,1:T(8,128)S(1)}, f32[128,256]{0,1:T(8,128)S(1)}, u32[]{:S(2)}, u32[]{:S(2)}) collective-permute-start(f32[128,256]{0,1:T(8,128)S(1)} %add.92), channel_id=1, source_target_pairs={{0,256},{1,257},{2,258},{3,259},{4,260},{5,261},{6,262},{7,263},{8... | collective-permute-start | bytes 393224 | tf_op jit(solution)/shard_map/ppermute | solution.py:21
  84.7 2.9 %collective-permute-start.9 = (f32[128,256]{0,1:T(8,128)S(1)}, f32[128,256]{0,1:T(8,128)S(1)}, u32[]{:S(2)}, u32[]{:S(2)}) collective-permute-start(f32[128,256]{0,1:T(8,128)S(1)} %add.84), channel_id=1, source_target_pairs={{0,32},{1,33},{2,34},{3,35},{4,36},{5,37},{6,38},{7,39},{8,40},{9,... | collective-permute-start | bytes 393224 | tf_op jit(solution)/shard_map/ppermute | solution.py:21
  88.2 5.0 %collective-permute-start.18 = (f32[128,256]{0,1:T(8,128)S(1)}, f32[128,256]{0,1:T(8,128)S(1)}, u32[]{:S(2)}, u32[]{:S(2)}) collective-permute-start(f32[128,256]{0,1:T(8,128)S(1)} %add.93), channel_id=1, source_target_pairs={{0,2},{1,3},{2,0},{3,1},{4,6},{5,7},{6,4},{7,5},{8,10},{9,11},{10,... | collective-permute-start | bytes 393224 | tf_op jit(solution)/shard_map/ppermute | solution.py:21
  93.9 3.1 %collective-permute-start.10 = (f32[128,256]{0,1:T(8,128)S(1)}, f32[128,256]{0,1:T(8,128)S(1)}, u32[]{:S(2)}, u32[]{:S(2)}) collective-permute-start(f32[128,256]{0,1:T(8,128)S(1)} %add.85), channel_id=1, source_target_pairs={{0,256},{1,257},{2,258},{3,259},{4,260},{5,261},{6,262},{7,263},{8... | collective-permute-start | bytes 393224 | tf_op jit(solution)/shard_map/ppermute | solution.py:21
  97.0 7.3 %collective-permute-start.19 = (f32[128,256]{0,1:T(8,128)S(1)}, f32[128,256]{0,1:T(8,128)S(1)}, u32[]{:S(2)}, u32[]{:S(2)}) collective-permute-start(f32[128,256]{0,1:T(8,128)S(1)} %add.94), channel_id=1, source_target_pairs={{0,64},{1,65},{2,66},{3,67},{4,68},{5,69},{6,70},{7,71},{8,72},{9,... | collective-permute-start | bytes 393224 | tf_op jit(solution)/shard_map/ppermute | solution.py:21
  104.4 8.4 %collective-permute-start.11 = (f32[128,256]{0,1:T(8,128)S(1)}, f32[128,256]{0,1:T(8,128)S(1)}, u32[]{:S(2)}, u32[]{:S(2)}) collective-permute-start(f32[128,256]{0,1:T(8,128)S(1)} %add.86), channel_id=1, source_target_pairs={{0,4},{1,5},{2,6},{3,7},{4,0},{5,1},{6,2},{7,3},{8,12},{9,13},{10,... | collective-permute-start | bytes 393224 | tf_op jit(solution)/shard_map/ppermute | solution.py:21
  112.8 3.3 %collective-permute-start.20 = (f32[128,256]{0,1:T(8,128)S(1)}, f32[128,256]{0,1:T(8,128)S(1)}, u32[]{:S(2)}, u32[]{:S(2)}) collective-permute-start(f32[128,256]{0,1:T(8,128)S(1)} %add.95), channel_id=1, source_target_pairs={{0,4},{1,5},{2,6},{3,7},{4,0},{5,1},{6,2},{7,3},{8,12},{9,13},{10,... | collective-permute-start | bytes 393224 | tf_op jit(solution)/shard_map/ppermute | solution.py:21
  116.2 2.7 %collective-permute-done.11 = f32[128,256]{0,1:T(8,128)S(1)} collective-permute-done((f32[128,256]{0,1:T(8,128)S(1)}, f32[128,256]{0,1:T(8,128)S(1)}, u32[]{:S(2)}, u32[]{:S(2)}) %collective-permute-start.11) | collective-permute-done | bytes 131104 | tf_op jit(solution)/shard_map/ppermute | solution.py:21
  118.9 4.7 %collective-permute-start.12 = (f32[128,256]{0,1:T(8,128)S(1)}, f32[128,256]{0,1:T(8,128)S(1)}, u32[]{:S(2)}, u32[]{:S(2)}) collective-permute-start(f32[128,256]{0,1:T(8,128)S(1)} %add.87), channel_id=1, source_target_pairs={{0,64},{1,65},{2,66},{3,67},{4,68},{5,69},{6,70},{7,71},{8,72},{9,... | collective-permute-start | bytes 393224 | tf_op jit(solution)/shard_map/ppermute | solution.py:21
  123.6 6.8 %collective-permute-done.12 = f32[128,256]{0,1:T(8,128)S(1)} collective-permute-done((f32[128,256]{0,1:T(8,128)S(1)}, f32[128,256]{0,1:T(8,128)S(1)}, u32[]{:S(2)}, u32[]{:S(2)}) %collective-permute-start.12) | collective-permute-done | bytes 131104 | tf_op jit(solution)/shard_map/ppermute | solution.py:21
  (72 shorter events, 23.5 us)
Async XLA Ops:
  7.2 6.7 %copy-start.1 = (s32[1,1,64]{2,1,0:T(1,128)S(1)}, s32[1,1,64]{2,1,0:T(1,128)}, u32[]{:S(2)}) copy-start(s32[1,1,64]{2,1,0:T(1,128)} %param.16) | copy-start | bytes 772
  7.2 7.5 %copy-start.3 = (s32[128]{0:T(128)S(1)}, s32[128]{0:T(128)}, u32[]{:S(2)}) copy-start(s32[128]{0:T(128)} %param.13) | copy-start | bytes 1540
  7.2 125.5 %reduce-scatter.2.cloned.1.call-start = ((), (), s32[]{:S(2)}) async-start(), calls=%async_computation.1 | async-start | bytes 1179648 | tf_op jit(solution)/shard_map/reduce_scatter | solution.py:75
  9.3 9.6 %collective-permute-start = (f32[256,256]{0,1:T(8,128)S(1)}, f32[256,256]{0,1:T(8,128)S(1)}, u32[]{:S(2)}, u32[]{:S(2)}) collective-permute-start(f32[256,256]{0,1:T(8,128)S(1)} %convolution_bitcast_fusion.2), channel_id=1, source_target_pairs={{0,1},{1,0},{2,3},{3,2},{4,5},{5,4},{6,7},{7,6},{8,9},{9,8},{10,11... | collective-permute-start | bytes 786440 | tf_op jit(solution)/shard_map/ppermute | solution.py:21
  19.1 23.8 %collective-permute-start.1 = (bf16[128,256]{1,0:T(8,128)(2,1)S(1)}, bf16[128,256]{1,0:T(8,128)(2,1)S(1)}, u32[]{:S(2)}, u32[]{:S(2)}) collective-permute-start(bf16[128,256]{1,0:T(8,128)(2,1)S(1)} %fusion.2), channel_id=1, source_target_pairs={{0,16},{8,24},{16,32},{24,40},{32,48},{40,56},{48,64},{56,72},{64,... | collective-permute-start | bytes 196616 | tf_op jit(solution)/shard_map/ppermute | solution.py:11
  26.2 16.7 %collective-permute-start.2 = (bf16[128,256]{1,0:T(8,128)(2,1)S(1)}, bf16[128,256]{1,0:T(8,128)(2,1)S(1)}, u32[]{:S(2)}, u32[]{:S(2)}) collective-permute-start(bf16[128,256]{1,0:T(8,128)(2,1)S(1)} %fusion.2), channel_id=1, source_target_pairs={{0,8},{8,16},{16,24},{24,32},{32,40},{40,48},{48,56},{56,64},{64,7... | collective-permute-start | bytes 196616 | tf_op jit(solution)/shard_map/ppermute | solution.py:11
  30.4 12.5 %collective-permute-start.3 = (bf16[128,256]{1,0:T(8,128)(2,1)S(1)}, bf16[128,256]{1,0:T(8,128)(2,1)S(1)}, u32[]{:S(2)}, u32[]{:S(2)}) collective-permute-start(bf16[128,256]{1,0:T(8,128)(2,1)S(1)} %fusion.2), channel_id=1, source_target_pairs={{0,504},{8,0},{16,8},{24,16},{32,24},{40,32},{48,40},{56,48},{64,5... | collective-permute-start | bytes 196616 | tf_op jit(solution)/shard_map/ppermute | solution.py:11
  33.5 11.2 %collective-permute-start.4 = (bf16[128,256]{1,0:T(8,128)(2,1)S(1)}, bf16[128,256]{1,0:T(8,128)(2,1)S(1)}, u32[]{:S(2)}, u32[]{:S(2)}) collective-permute-start(bf16[128,256]{1,0:T(8,128)(2,1)S(1)} %fusion.2), channel_id=1, source_target_pairs={{0,496},{8,504},{16,0},{24,8},{32,16},{40,24},{48,32},{56,40},{64,... | collective-permute-start | bytes 196616 | tf_op jit(solution)/shard_map/ppermute | solution.py:11
  46.4 6.9 %collective-permute-start.5 = (f32[128,256]{0,1:T(8,128)S(1)}, f32[128,256]{0,1:T(8,128)S(1)}, u32[]{:S(2)}, u32[]{:S(2)}) collective-permute-start(f32[128,256]{0,1:T(8,128)S(1)} %get-tuple-element.16), channel_id=1, source_target_pairs={{0,8},{1,9},{2,10},{3,11},{4,12},{5,13},{6,14},{7,15},{8,0},{9,1},... | collective-permute-start | bytes 393224 | tf_op jit(solution)/shard_map/ppermute | solution.py:21
  50.1 6.9 %collective-permute-start.13 = (f32[128,256]{0,1:T(8,128)S(1)}, f32[128,256]{0,1:T(8,128)S(1)}, u32[]{:S(2)}, u32[]{:S(2)}) collective-permute-start(f32[128,256]{0,1:T(8,128)S(1)} %get-tuple-element.17), channel_id=1, source_target_pairs={{0,16},{1,17},{2,18},{3,19},{4,20},{5,21},{6,22},{7,23},{8,24},{9,... | collective-permute-start | bytes 393224 | tf_op jit(solution)/shard_map/ppermute | solution.py:21
  57.0 6.9 %collective-permute-start.14 = (f32[128,256]{0,1:T(8,128)S(1)}, f32[128,256]{0,1:T(8,128)S(1)}, u32[]{:S(2)}, u32[]{:S(2)}) collective-permute-start(f32[128,256]{0,1:T(8,128)S(1)} %get-tuple-element.15), channel_id=1, source_target_pairs={{0,128},{1,129},{2,130},{3,131},{4,132},{5,133},{6,134},{7,135},{8... | collective-permute-start | bytes 393224 | tf_op jit(solution)/shard_map/ppermute | solution.py:21
  59.0 7.1 %collective-permute-start.6 = (f32[128,256]{0,1:T(8,128)S(1)}, f32[128,256]{0,1:T(8,128)S(1)}, u32[]{:S(2)}, u32[]{:S(2)}) collective-permute-start(f32[128,256]{0,1:T(8,128)S(1)} %get-tuple-element.14), channel_id=1, source_target_pairs={{0,16},{1,17},{2,18},{3,19},{4,20},{5,21},{6,22},{7,23},{8,24},{9,... | collective-permute-start | bytes 393224 | tf_op jit(solution)/shard_map/ppermute | solution.py:21
  63.9 7.2 %collective-permute-start.15 = (f32[128,256]{0,1:T(8,128)S(1)}, f32[128,256]{0,1:T(8,128)S(1)}, u32[]{:S(2)}, u32[]{:S(2)}) collective-permute-start(f32[128,256]{0,1:T(8,128)S(1)} %add.90), channel_id=1, source_target_pairs={{0,8},{1,9},{2,10},{3,11},{4,12},{5,13},{6,14},{7,15},{8,0},{9,1},... | collective-permute-start | bytes 393224 | tf_op jit(solution)/shard_map/ppermute | solution.py:21
  66.1 8.0 %collective-permute-start.7 = (f32[128,256]{0,1:T(8,128)S(1)}, f32[128,256]{0,1:T(8,128)S(1)}, u32[]{:S(2)}, u32[]{:S(2)}) collective-permute-start(f32[128,256]{0,1:T(8,128)S(1)} %add.82), channel_id=1, source_target_pairs={{0,128},{1,129},{2,130},{3,131},{4,132},{5,133},{6,134},{7,135},{8... | collective-permute-start | bytes 393224 | tf_op jit(solution)/shard_map/ppermute | solution.py:21
  71.1 8.6 %collective-permute-start.16 = (f32[128,256]{0,1:T(8,128)S(1)}, f32[128,256]{0,1:T(8,128)S(1)}, u32[]{:S(2)}, u32[]{:S(2)}) collective-permute-start(f32[128,256]{0,1:T(8,128)S(1)} %add.91), channel_id=1, source_target_pairs={{0,32},{1,33},{2,34},{3,35},{4,36},{5,37},{6,38},{7,39},{8,40},{9,... | collective-permute-start | bytes 393224 | tf_op jit(solution)/shard_map/ppermute | solution.py:21
  74.1 10.5 %collective-permute-start.8 = (f32[128,256]{0,1:T(8,128)S(1)}, f32[128,256]{0,1:T(8,128)S(1)}, u32[]{:S(2)}, u32[]{:S(2)}) collective-permute-start(f32[128,256]{0,1:T(8,128)S(1)} %add.83), channel_id=1, source_target_pairs={{0,2},{1,3},{2,0},{3,1},{4,6},{5,7},{6,4},{7,5},{8,10},{9,11},{10,... | collective-permute-start | bytes 393224 | tf_op jit(solution)/shard_map/ppermute | solution.py:21
  79.8 8.4 %collective-permute-start.17 = (f32[128,256]{0,1:T(8,128)S(1)}, f32[128,256]{0,1:T(8,128)S(1)}, u32[]{:S(2)}, u32[]{:S(2)}) collective-permute-start(f32[128,256]{0,1:T(8,128)S(1)} %add.92), channel_id=1, source_target_pairs={{0,256},{1,257},{2,258},{3,259},{4,260},{5,261},{6,262},{7,263},{8... | collective-permute-start | bytes 393224 | tf_op jit(solution)/shard_map/ppermute | solution.py:21
  84.7 9.2 %collective-permute-start.9 = (f32[128,256]{0,1:T(8,128)S(1)}, f32[128,256]{0,1:T(8,128)S(1)}, u32[]{:S(2)}, u32[]{:S(2)}) collective-permute-start(f32[128,256]{0,1:T(8,128)S(1)} %add.84), channel_id=1, source_target_pairs={{0,32},{1,33},{2,34},{3,35},{4,36},{5,37},{6,38},{7,39},{8,40},{9,... | collective-permute-start | bytes 393224 | tf_op jit(solution)/shard_map/ppermute | solution.py:21
  88.2 8.9 %collective-permute-start.18 = (f32[128,256]{0,1:T(8,128)S(1)}, f32[128,256]{0,1:T(8,128)S(1)}, u32[]{:S(2)}, u32[]{:S(2)}) collective-permute-start(f32[128,256]{0,1:T(8,128)S(1)} %add.93), channel_id=1, source_target_pairs={{0,2},{1,3},{2,0},{3,1},{4,6},{5,7},{6,4},{7,5},{8,10},{9,11},{10,... | collective-permute-start | bytes 393224 | tf_op jit(solution)/shard_map/ppermute | solution.py:21
  93.9 10.5 %collective-permute-start.10 = (f32[128,256]{0,1:T(8,128)S(1)}, f32[128,256]{0,1:T(8,128)S(1)}, u32[]{:S(2)}, u32[]{:S(2)}) collective-permute-start(f32[128,256]{0,1:T(8,128)S(1)} %add.85), channel_id=1, source_target_pairs={{0,256},{1,257},{2,258},{3,259},{4,260},{5,261},{6,262},{7,263},{8... | collective-permute-start | bytes 393224 | tf_op jit(solution)/shard_map/ppermute | solution.py:21
  97.0 15.8 %collective-permute-start.19 = (f32[128,256]{0,1:T(8,128)S(1)}, f32[128,256]{0,1:T(8,128)S(1)}, u32[]{:S(2)}, u32[]{:S(2)}) collective-permute-start(f32[128,256]{0,1:T(8,128)S(1)} %add.94), channel_id=1, source_target_pairs={{0,64},{1,65},{2,66},{3,67},{4,68},{5,69},{6,70},{7,71},{8,72},{9,... | collective-permute-start | bytes 393224 | tf_op jit(solution)/shard_map/ppermute | solution.py:21
  104.4 14.5 %collective-permute-start.11 = (f32[128,256]{0,1:T(8,128)S(1)}, f32[128,256]{0,1:T(8,128)S(1)}, u32[]{:S(2)}, u32[]{:S(2)}) collective-permute-start(f32[128,256]{0,1:T(8,128)S(1)} %add.86), channel_id=1, source_target_pairs={{0,4},{1,5},{2,6},{3,7},{4,0},{5,1},{6,2},{7,3},{8,12},{9,13},{10,... | collective-permute-start | bytes 393224 | tf_op jit(solution)/shard_map/ppermute | solution.py:21
  112.8 10.8 %collective-permute-start.20 = (f32[128,256]{0,1:T(8,128)S(1)}, f32[128,256]{0,1:T(8,128)S(1)}, u32[]{:S(2)}, u32[]{:S(2)}) collective-permute-start(f32[128,256]{0,1:T(8,128)S(1)} %add.95), channel_id=1, source_target_pairs={{0,4},{1,5},{2,6},{3,7},{4,0},{5,1},{6,2},{7,3},{8,12},{9,13},{10,... | collective-permute-start | bytes 393224 | tf_op jit(solution)/shard_map/ppermute | solution.py:21
  118.9 11.5 %collective-permute-start.12 = (f32[128,256]{0,1:T(8,128)S(1)}, f32[128,256]{0,1:T(8,128)S(1)}, u32[]{:S(2)}, u32[]{:S(2)}) collective-permute-start(f32[128,256]{0,1:T(8,128)S(1)} %add.87), channel_id=1, source_target_pairs={{0,64},{1,65},{2,66},{3,67},{4,68},{5,69},{6,70},{7,71},{8,72},{9,... | collective-permute-start | bytes 393224 | tf_op jit(solution)/shard_map/ppermute | solution.py:21
  (2 other events, 10.4 us)
Sparse Core Ops, SparseCore 0:
  46.5 40.7 reduce-scatter.1

commit v4 on v3

--- a/solution.py
+++ b/solution.py
@@ -18,7 +18,7 @@
     parts = jnp.split(x, len(orders), axis=0)
     for step in range(max(len(order) for order in orders)):
         parts = [
-            part + lax.ppermute(part, axes, [(i, i ^ (1 << order[step])) for i in range(size)])
+            part + lax.ppermute(part, axes, [(i, i ^ order[step]) for i in range(size)])
             if step < len(order)
             else part
             for part, order in zip(parts, orders)
@@ -31,10 +31,13 @@
     local_weight = lax.dot_general(
         aggregated, grad_pre, (((0,), (0,)), ((), ())), preferred_element_type=jnp.float32
     )
-    paired = summed_everywhere(local_weight, ("blk", "rep"), [[0]])
+    y1, y2, y3 = 1 << 3, 1 << 1, (1 << 1) | (1 << 2) | (1 << 3)
+    z1, z2, z3 = 1 << 4, 1 << 5, (1 << 4) | (1 << 5) | (1 << 6)
+    x1, x2 = 1 << 7, (1 << 7) | (1 << 8)
+    paired = summed_everywhere(local_weight, ("blk", "rep"), [[1]])
     paired, grad_pre = lax.optimization_barrier((paired, grad_pre))
     raw_weight = summed_everywhere(
-        paired, ("blk", "rep"), [[3, 4, 7, 1, 5, 8, 2, 6], [4, 7, 3, 5, 8, 1, 6, 2]]
+        paired, ("blk", "rep"), [[y1, z1, x1, y2, z2, x2, y3, z3], [z1, x1, y1, z2, x2, y2, z3, y3]]
     )
     norm_value = jnp.sqrt(jnp.sum(raw_weight * raw_weight) + 1e-06)
     grad_weight = raw_weight * jnp.minimum(1.0, 128.0 / norm_value)

time: 142 us -> 135 us (0.951)
  the two profiles are of different devices: /device:TPU:8 before, /device:TPU:16 now
where the time goes in v4:
time: 135 us; the launch traced here: 134 us
  starting transfers between devices  75.6 us (56%)
  waiting for transfers between devices  25.4 us (19%)
  between operations  15.2 us (11%)
  other arithmetic  8.62 us (6%)
  matrix products  5.66 us (4%)
  local copies, waits for them, and re-layouts  3.43 us (3%)
    ppermute x17, starting transfers between devices, summed_everywhere(): lax.ppermute(part, axes, [(i, i ^ order[step]) for i in range(size)])  53.7 us
    ppermute x17, waiting for transfers between devices, summed_everywhere(): lax.ppermute(part, axes, [(i, i ^ order[step]) for i in range(size)])  23.2 us
    ppermute x4, starting transfers between devices, fetched_from(): lax.ppermute(x, axis, [(i, (i - offset) % size) for i in range(size)])  21.9 us
    reduce_sum x1, other arithmetic, on_device(): jnp.sum((listed[:, :, :, :, None] == positions[None, None, None, None, :]...  4.16 us
    dot_general x1, matrix products, on_device(): merged = jnp.einsum('tsn,tsic->tinc', chooser, counts).astype(jnp.bfloat16)  2.81 us
  transfers between devices with their start and end apart: 22, of which 13 were waited for; matrix products, arithmetic and copies ran while one was open for 9% of the time, Pallas kernels for 0%

profile of v4, /device:TPU:16, one launch (start us, length us, event | category | flops | bytes accessed | tf_op | source)
XLA Modules:
  0.0 133.9 jit_solution(3747196768517453668)
XLA Ops:
  14.7 4.2 %convert_reduce_fusion = s32[5,4,128,128]{3,2,1,0:T(8,128)S(1)} fusion(s32[5,4,8,128]{3,2,1,0:T(8,128)S(1)} %broadcast_select_fusion), kind=kLoop, calls=%fused_computation.3 | loop fusion | flops 7536640 | bytes 1392640 | tf_op jit(solution)/shard_map/reduce_sum | solution.py:66
  19.1 4.3 %collective-permute-start.1 = (bf16[128,256]{1,0:T(8,128)(2,1)S(1)}, bf16[128,256]{1,0:T(8,128)(2,1)S(1)}, u32[]{:S(2)}, u32[]{:S(2)}) collective-permute-start(bf16[128,256]{1,0:T(8,128)(2,1)S(1)} %fusion.2), channel_id=1, source_target_pairs={{0,16},{8,24},{16,32},{24,40},{32,48},{40,56},{48,64},{56,72},{64,... | collective-permute-start | bytes 196616 | tf_op jit(solution)/shard_map/ppermute | solution.py:11
  23.4 2.8 %convolution_bitcast_fusion = bf16[5,128,8,128]{3,2,1,0:T(8,128)(2,1)S(1)} fusion(s32[5,4,128,128]{3,2,1,0:T(8,128)S(1)} %convert_reduce_fusion, s32[5,4]{1,0:T(8,128)S(1)} %broadcast_select_fusion.1, pred[5,4]{1,0:T(8,128)(4,1)S(1)} %iota_compare_fusion.2), kind=kOutput, calls=%fused_computation.5 | convolution fusion | flops 5243200 | bytes 2621540 | tf_op jit(solution)/shard_map/tsn,tsic->tinc/dot_general | solution.py:74
  26.2 3.5 %collective-permute-start.2 = (bf16[128,256]{1,0:T(8,128)(2,1)S(1)}, bf16[128,256]{1,0:T(8,128)(2,1)S(1)}, u32[]{:S(2)}, u32[]{:S(2)}) collective-permute-start(bf16[128,256]{1,0:T(8,128)(2,1)S(1)} %fusion.2), channel_id=1, source_target_pairs={{0,8},{8,16},{16,24},{24,32},{32,40},{40,48},{48,56},{56,64},{64,7... | collective-permute-start | bytes 196616 | tf_op jit(solution)/shard_map/ppermute | solution.py:11
  29.7 10.2 %collective-permute-start.3 = (bf16[128,256]{1,0:T(8,128)(2,1)S(1)}, bf16[128,256]{1,0:T(8,128)(2,1)S(1)}, u32[]{:S(2)}, u32[]{:S(2)}) collective-permute-start(bf16[128,256]{1,0:T(8,128)(2,1)S(1)} %fusion.2), channel_id=1, source_target_pairs={{0,504},{8,0},{16,8},{24,16},{32,24},{40,32},{48,40},{56,48},{64,5... | collective-permute-start | bytes 196616 | tf_op jit(solution)/shard_map/ppermute | solution.py:11
  39.9 3.9 %collective-permute-start.4 = (bf16[128,256]{1,0:T(8,128)(2,1)S(1)}, bf16[128,256]{1,0:T(8,128)(2,1)S(1)}, u32[]{:S(2)}, u32[]{:S(2)}) collective-permute-start(bf16[128,256]{1,0:T(8,128)(2,1)S(1)} %fusion.2), channel_id=1, source_target_pairs={{0,496},{8,504},{16,0},{24,8},{32,16},{40,24},{48,32},{56,40},{64,... | collective-permute-start | bytes 196616 | tf_op jit(solution)/shard_map/ppermute | solution.py:11
  43.9 2.1 %collective-permute-done.4 = bf16[128,256]{1,0:T(8,128)(2,1)S(1)} collective-permute-done((bf16[128,256]{1,0:T(8,128)(2,1)S(1)}, bf16[128,256]{1,0:T(8,128)(2,1)S(1)}, u32[]{:S(2)}, u32[]{:S(2)}) %collective-permute-start.4) | collective-permute-done | bytes 65568 | tf_op jit(solution)/shard_map/ppermute | solution.py:11
  47.8 2.1 %collective-permute-start.5 = (f32[128,256]{0,1:T(8,128)S(1)}, f32[128,256]{0,1:T(8,128)S(1)}, u32[]{:S(2)}, u32[]{:S(2)}) collective-permute-start(f32[128,256]{0,1:T(8,128)S(1)} %get-tuple-element.16), channel_id=1, source_target_pairs={{0,8},{1,9},{2,10},{3,11},{4,12},{5,13},{6,14},{7,15},{8,0},{9,1},... | collective-permute-start | bytes 393224 | tf_op jit(solution)/shard_map/ppermute | solution.py:21
  51.8 2.8 %collective-permute-done.5 = f32[128,256]{0,1:T(8,128)S(1)} collective-permute-done((f32[128,256]{0,1:T(8,128)S(1)}, f32[128,256]{0,1:T(8,128)S(1)}, u32[]{:S(2)}, u32[]{:S(2)}) %collective-permute-start.5) | collective-permute-done | bytes 131104 | tf_op jit(solution)/shard_map/ppermute | solution.py:21
  54.6 2.1 %collective-permute-done.13 = f32[128,256]{0,1:T(8,128)S(1)} collective-permute-done((f32[128,256]{0,1:T(8,128)S(1)}, f32[128,256]{0,1:T(8,128)S(1)}, u32[]{:S(2)}, u32[]{:S(2)}) %collective-permute-start.13) | collective-permute-done | bytes 131104 | tf_op jit(solution)/shard_map/ppermute | solution.py:21
  60.6 3.0 %collective-permute-done.14 = f32[128,256]{0,1:T(8,128)S(1)} collective-permute-done((f32[128,256]{0,1:T(8,128)S(1)}, f32[128,256]{0,1:T(8,128)S(1)}, u32[]{:S(2)}, u32[]{:S(2)}) %collective-permute-start.14) | collective-permute-done | bytes 131104 | tf_op jit(solution)/shard_map/ppermute | solution.py:21
  63.7 3.7 %collective-permute-start.15 = (f32[128,256]{0,1:T(8,128)S(1)}, f32[128,256]{0,1:T(8,128)S(1)}, u32[]{:S(2)}, u32[]{:S(2)}) collective-permute-start(f32[128,256]{0,1:T(8,128)S(1)} %add.90), channel_id=1, source_target_pairs={{0,8},{1,9},{2,10},{3,11},{4,12},{5,13},{6,14},{7,15},{8,0},{9,1},... | collective-permute-start | bytes 393224 | tf_op jit(solution)/shard_map/ppermute | solution.py:21
  67.4 2.1 %collective-permute-start.7 = (f32[128,256]{0,1:T(8,128)S(1)}, f32[128,256]{0,1:T(8,128)S(1)}, u32[]{:S(2)}, u32[]{:S(2)}) collective-permute-start(f32[128,256]{0,1:T(8,128)S(1)} %add.82), channel_id=1, source_target_pairs={{0,128},{1,129},{2,130},{3,131},{4,132},{5,133},{6,134},{7,135},{8... | collective-permute-start | bytes 393224 | tf_op jit(solution)/shard_map/ppermute | solution.py:21
  70.9 2.9 %collective-permute-start.16 = (f32[128,256]{0,1:T(8,128)S(1)}, f32[128,256]{0,1:T(8,128)S(1)}, u32[]{:S(2)}, u32[]{:S(2)}) collective-permute-start(f32[128,256]{0,1:T(8,128)S(1)} %add.91), channel_id=1, source_target_pairs={{0,32},{1,33},{2,34},{3,35},{4,36},{5,37},{6,38},{7,39},{8,40},{9,... | collective-permute-start | bytes 393224 | tf_op jit(solution)/shard_map/ppermute | solution.py:21
  74.3 2.2 %collective-permute-start.8 = (f32[128,256]{0,1:T(8,128)S(1)}, f32[128,256]{0,1:T(8,128)S(1)}, u32[]{:S(2)}, u32[]{:S(2)}) collective-permute-start(f32[128,256]{0,1:T(8,128)S(1)} %add.83), channel_id=1, source_target_pairs={{0,2},{1,3},{2,0},{3,1},{4,6},{5,7},{6,4},{7,5},{8,10},{9,11},{10,... | collective-permute-start | bytes 393224 | tf_op jit(solution)/shard_map/ppermute | solution.py:21
  76.6 3.3 %collective-permute-done.16 = f32[128,256]{0,1:T(8,128)S(1)} collective-permute-done((f32[128,256]{0,1:T(8,128)S(1)}, f32[128,256]{0,1:T(8,128)S(1)}, u32[]{:S(2)}, u32[]{:S(2)}) %collective-permute-start.16) | collective-permute-done | bytes 131104 | tf_op jit(solution)/shard_map/ppermute | solution.py:21
  79.9 3.3 %collective-permute-start.17 = (f32[128,256]{0,1:T(8,128)S(1)}, f32[128,256]{0,1:T(8,128)S(1)}, u32[]{:S(2)}, u32[]{:S(2)}) collective-permute-start(f32[128,256]{0,1:T(8,128)S(1)} %add.92), channel_id=1, source_target_pairs={{0,384},{1,385},{2,386},{3,387},{4,388},{5,389},{6,390},{7,391},{8... | collective-permute-start | bytes 393224 | tf_op jit(solution)/shard_map/ppermute | solution.py:21
  83.8 2.3 %collective-permute-start.9 = (f32[128,256]{0,1:T(8,128)S(1)}, f32[128,256]{0,1:T(8,128)S(1)}, u32[]{:S(2)}, u32[]{:S(2)}) collective-permute-start(f32[128,256]{0,1:T(8,128)S(1)} %add.84), channel_id=1, source_target_pairs={{0,32},{1,33},{2,34},{3,35},{4,36},{5,37},{6,38},{7,39},{8,40},{9,... | collective-permute-start | bytes 393224 | tf_op jit(solution)/shard_map/ppermute | solution.py:21
  88.0 3.4 %collective-permute-start.18 = (f32[128,256]{0,1:T(8,128)S(1)}, f32[128,256]{0,1:T(8,128)S(1)}, u32[]{:S(2)}, u32[]{:S(2)}) collective-permute-start(f32[128,256]{0,1:T(8,128)S(1)} %add.93), channel_id=1, source_target_pairs={{0,2},{1,3},{2,0},{3,1},{4,6},{5,7},{6,4},{7,5},{8,10},{9,11},{10,... | collective-permute-start | bytes 393224 | tf_op jit(solution)/shard_map/ppermute | solution.py:21
  95.9 5.3 %collective-permute-start.19 = (f32[128,256]{0,1:T(8,128)S(1)}, f32[128,256]{0,1:T(8,128)S(1)}, u32[]{:S(2)}, u32[]{:S(2)}) collective-permute-start(f32[128,256]{0,1:T(8,128)S(1)} %add.94), channel_id=1, source_target_pairs={{0,112},{1,113},{2,114},{3,115},{4,116},{5,117},{6,118},{7,119},{8... | collective-permute-start | bytes 393224 | tf_op jit(solution)/shard_map/ppermute | solution.py:21
  101.2 7.2 %collective-permute-start.11 = (f32[128,256]{0,1:T(8,128)S(1)}, f32[128,256]{0,1:T(8,128)S(1)}, u32[]{:S(2)}, u32[]{:S(2)}) collective-permute-start(f32[128,256]{0,1:T(8,128)S(1)} %add.86), channel_id=1, source_target_pairs={{0,14},{1,15},{2,12},{3,13},{4,10},{5,11},{6,8},{7,9},{8,6},{9,7},... | collective-permute-start | bytes 393224 | tf_op jit(solution)/shard_map/ppermute | solution.py:21
  108.5 5.2 %collective-permute-start.20 = (f32[128,256]{0,1:T(8,128)S(1)}, f32[128,256]{0,1:T(8,128)S(1)}, u32[]{:S(2)}, u32[]{:S(2)}) collective-permute-start(f32[128,256]{0,1:T(8,128)S(1)} %add.95), channel_id=1, source_target_pairs={{0,14},{1,15},{2,12},{3,13},{4,10},{5,11},{6,8},{7,9},{8,6},{9,7},... | collective-permute-start | bytes 393224 | tf_op jit(solution)/shard_map/ppermute | solution.py:21
  113.7 4.2 %collective-permute-start.12 = (f32[128,256]{0,1:T(8,128)S(1)}, f32[128,256]{0,1:T(8,128)S(1)}, u32[]{:S(2)}, u32[]{:S(2)}) collective-permute-start(f32[128,256]{0,1:T(8,128)S(1)} %add.87), channel_id=1, source_target_pairs={{0,112},{1,113},{2,114},{3,115},{4,116},{5,117},{6,118},{7,119},{8... | collective-permute-start | bytes 393224 | tf_op jit(solution)/shard_map/ppermute | solution.py:21
  118.5 4.7 %collective-permute-done.12 = f32[128,256]{0,1:T(8,128)S(1)} collective-permute-done((f32[128,256]{0,1:T(8,128)S(1)}, f32[128,256]{0,1:T(8,128)S(1)}, u32[]{:S(2)}, u32[]{:S(2)}) %collective-permute-start.12) | collective-permute-done | bytes 131104 | tf_op jit(solution)/shard_map/ppermute | solution.py:21
  (72 shorter events, 27.6 us)
Async XLA Ops:
  7.2 6.7 %copy-start.1 = (s32[1,1,64]{2,1,0:T(1,128)S(1)}, s32[1,1,64]{2,1,0:T(1,128)}, u32[]{:S(2)}) copy-start(s32[1,1,64]{2,1,0:T(1,128)} %param.16) | copy-start | bytes 772
  7.2 7.5 %copy-start.3 = (s32[128]{0:T(128)S(1)}, s32[128]{0:T(128)}, u32[]{:S(2)}) copy-start(s32[128]{0:T(128)} %param.13) | copy-start | bytes 1540
  7.2 118.2 %reduce-scatter.2.cloned.1.call-start = ((), (), s32[]{:S(2)}) async-start(), calls=%async_computation.1 | async-start | bytes 1179648 | tf_op jit(solution)/shard_map/reduce_scatter | solution.py:78
  9.3 9.6 %collective-permute-start = (f32[256,256]{0,1:T(8,128)S(1)}, f32[256,256]{0,1:T(8,128)S(1)}, u32[]{:S(2)}, u32[]{:S(2)}) collective-permute-start(f32[256,256]{0,1:T(8,128)S(1)} %convolution_bitcast_fusion.2), channel_id=1, source_target_pairs={{0,1},{1,0},{2,3},{3,2},{4,5},{5,4},{6,7},{7,6},{8,9},{9,8},{10,11... | collective-permute-start | bytes 786440 | tf_op jit(solution)/shard_map/ppermute | solution.py:21
  19.1 24.8 %collective-permute-start.1 = (bf16[128,256]{1,0:T(8,128)(2,1)S(1)}, bf16[128,256]{1,0:T(8,128)(2,1)S(1)}, u32[]{:S(2)}, u32[]{:S(2)}) collective-permute-start(bf16[128,256]{1,0:T(8,128)(2,1)S(1)} %fusion.2), channel_id=1, source_target_pairs={{0,16},{8,24},{16,32},{24,40},{32,48},{40,56},{48,64},{56,72},{64,... | collective-permute-start | bytes 196616 | tf_op jit(solution)/shard_map/ppermute | solution.py:11
  26.2 17.7 %collective-permute-start.2 = (bf16[128,256]{1,0:T(8,128)(2,1)S(1)}, bf16[128,256]{1,0:T(8,128)(2,1)S(1)}, u32[]{:S(2)}, u32[]{:S(2)}) collective-permute-start(bf16[128,256]{1,0:T(8,128)(2,1)S(1)} %fusion.2), channel_id=1, source_target_pairs={{0,8},{8,16},{16,24},{24,32},{32,40},{40,48},{48,56},{56,64},{64,7... | collective-permute-start | bytes 196616 | tf_op jit(solution)/shard_map/ppermute | solution.py:11
  29.7 14.2 %collective-permute-start.3 = (bf16[128,256]{1,0:T(8,128)(2,1)S(1)}, bf16[128,256]{1,0:T(8,128)(2,1)S(1)}, u32[]{:S(2)}, u32[]{:S(2)}) collective-permute-start(bf16[128,256]{1,0:T(8,128)(2,1)S(1)} %fusion.2), channel_id=1, source_target_pairs={{0,504},{8,0},{16,8},{24,16},{32,24},{40,32},{48,40},{56,48},{64,5... | collective-permute-start | bytes 196616 | tf_op jit(solution)/shard_map/ppermute | solution.py:11
  39.9 6.2 %collective-permute-start.4 = (bf16[128,256]{1,0:T(8,128)(2,1)S(1)}, bf16[128,256]{1,0:T(8,128)(2,1)S(1)}, u32[]{:S(2)}, u32[]{:S(2)}) collective-permute-start(bf16[128,256]{1,0:T(8,128)(2,1)S(1)} %fusion.2), channel_id=1, source_target_pairs={{0,496},{8,504},{16,0},{24,8},{32,16},{40,24},{48,32},{56,40},{64,... | collective-permute-start | bytes 196616 | tf_op jit(solution)/shard_map/ppermute | solution.py:11
  47.8 6.9 %collective-permute-start.5 = (f32[128,256]{0,1:T(8,128)S(1)}, f32[128,256]{0,1:T(8,128)S(1)}, u32[]{:S(2)}, u32[]{:S(2)}) collective-permute-start(f32[128,256]{0,1:T(8,128)S(1)} %get-tuple-element.16), channel_id=1, source_target_pairs={{0,8},{1,9},{2,10},{3,11},{4,12},{5,13},{6,14},{7,15},{8,0},{9,1},... | collective-permute-start | bytes 393224 | tf_op jit(solution)/shard_map/ppermute | solution.py:21
  49.9 6.9 %collective-permute-start.13 = (f32[128,256]{0,1:T(8,128)S(1)}, f32[128,256]{0,1:T(8,128)S(1)}, u32[]{:S(2)}, u32[]{:S(2)}) collective-permute-start(f32[128,256]{0,1:T(8,128)S(1)} %get-tuple-element.17), channel_id=1, source_target_pairs={{0,16},{1,17},{2,18},{3,19},{4,20},{5,21},{6,22},{7,23},{8,24},{9,... | collective-permute-start | bytes 393224 | tf_op jit(solution)/shard_map/ppermute | solution.py:21
  56.8 6.9 %collective-permute-start.14 = (f32[128,256]{0,1:T(8,128)S(1)}, f32[128,256]{0,1:T(8,128)S(1)}, u32[]{:S(2)}, u32[]{:S(2)}) collective-permute-start(f32[128,256]{0,1:T(8,128)S(1)} %get-tuple-element.15), channel_id=1, source_target_pairs={{0,128},{1,129},{2,130},{3,131},{4,132},{5,133},{6,134},{7,135},{8... | collective-permute-start | bytes 393224 | tf_op jit(solution)/shard_map/ppermute | solution.py:21
  58.7 8.7 %collective-permute-start.6 = (f32[128,256]{0,1:T(8,128)S(1)}, f32[128,256]{0,1:T(8,128)S(1)}, u32[]{:S(2)}, u32[]{:S(2)}) collective-permute-start(f32[128,256]{0,1:T(8,128)S(1)} %get-tuple-element.14), channel_id=1, source_target_pairs={{0,16},{1,17},{2,18},{3,19},{4,20},{5,21},{6,22},{7,23},{8,24},{9,... | collective-permute-start | bytes 393224 | tf_op jit(solution)/shard_map/ppermute | solution.py:21
  63.7 7.2 %collective-permute-start.15 = (f32[128,256]{0,1:T(8,128)S(1)}, f32[128,256]{0,1:T(8,128)S(1)}, u32[]{:S(2)}, u32[]{:S(2)}) collective-permute-start(f32[128,256]{0,1:T(8,128)S(1)} %add.90), channel_id=1, source_target_pairs={{0,8},{1,9},{2,10},{3,11},{4,12},{5,13},{6,14},{7,15},{8,0},{9,1},... | collective-permute-start | bytes 393224 | tf_op jit(solution)/shard_map/ppermute | solution.py:21
  67.4 6.9 %collective-permute-start.7 = (f32[128,256]{0,1:T(8,128)S(1)}, f32[128,256]{0,1:T(8,128)S(1)}, u32[]{:S(2)}, u32[]{:S(2)}) collective-permute-start(f32[128,256]{0,1:T(8,128)S(1)} %add.82), channel_id=1, source_target_pairs={{0,128},{1,129},{2,130},{3,131},{4,132},{5,133},{6,134},{7,135},{8... | collective-permute-start | bytes 393224 | tf_op jit(solution)/shard_map/ppermute | solution.py:21
  70.9 9.0 %collective-permute-start.16 = (f32[128,256]{0,1:T(8,128)S(1)}, f32[128,256]{0,1:T(8,128)S(1)}, u32[]{:S(2)}, u32[]{:S(2)}) collective-permute-start(f32[128,256]{0,1:T(8,128)S(1)} %add.91), channel_id=1, source_target_pairs={{0,32},{1,33},{2,34},{3,35},{4,36},{5,37},{6,38},{7,39},{8,40},{9,... | collective-permute-start | bytes 393224 | tf_op jit(solution)/shard_map/ppermute | solution.py:21
  74.3 9.5 %collective-permute-start.8 = (f32[128,256]{0,1:T(8,128)S(1)}, f32[128,256]{0,1:T(8,128)S(1)}, u32[]{:S(2)}, u32[]{:S(2)}) collective-permute-start(f32[128,256]{0,1:T(8,128)S(1)} %add.83), channel_id=1, source_target_pairs={{0,2},{1,3},{2,0},{3,1},{4,6},{5,7},{6,4},{7,5},{8,10},{9,11},{10,... | collective-permute-start | bytes 393224 | tf_op jit(solution)/shard_map/ppermute | solution.py:21
  79.9 8.1 %collective-permute-start.17 = (f32[128,256]{0,1:T(8,128)S(1)}, f32[128,256]{0,1:T(8,128)S(1)}, u32[]{:S(2)}, u32[]{:S(2)}) collective-permute-start(f32[128,256]{0,1:T(8,128)S(1)} %add.92), channel_id=1, source_target_pairs={{0,384},{1,385},{2,386},{3,387},{4,388},{5,389},{6,390},{7,391},{8... | collective-permute-start | bytes 393224 | tf_op jit(solution)/shard_map/ppermute | solution.py:21
  83.8 9.2 %collective-permute-start.9 = (f32[128,256]{0,1:T(8,128)S(1)}, f32[128,256]{0,1:T(8,128)S(1)}, u32[]{:S(2)}, u32[]{:S(2)}) collective-permute-start(f32[128,256]{0,1:T(8,128)S(1)} %add.84), channel_id=1, source_target_pairs={{0,32},{1,33},{2,34},{3,35},{4,36},{5,37},{6,38},{7,39},{8,40},{9,... | collective-permute-start | bytes 393224 | tf_op jit(solution)/shard_map/ppermute | solution.py:21
  88.0 7.8 %collective-permute-start.18 = (f32[128,256]{0,1:T(8,128)S(1)}, f32[128,256]{0,1:T(8,128)S(1)}, u32[]{:S(2)}, u32[]{:S(2)}) collective-permute-start(f32[128,256]{0,1:T(8,128)S(1)} %add.93), channel_id=1, source_target_pairs={{0,2},{1,3},{2,0},{3,1},{4,6},{5,7},{6,4},{7,5},{8,10},{9,11},{10,... | collective-permute-start | bytes 393224 | tf_op jit(solution)/shard_map/ppermute | solution.py:21
  93.0 8.2 %collective-permute-start.10 = (f32[128,256]{0,1:T(8,128)S(1)}, f32[128,256]{0,1:T(8,128)S(1)}, u32[]{:S(2)}, u32[]{:S(2)}) collective-permute-start(f32[128,256]{0,1:T(8,128)S(1)} %add.85), channel_id=1, source_target_pairs={{0,384},{1,385},{2,386},{3,387},{4,388},{5,389},{6,390},{7,391},{8... | collective-permute-start | bytes 393224 | tf_op jit(solution)/shard_map/ppermute | solution.py:21
  95.9 12.6 %collective-permute-start.19 = (f32[128,256]{0,1:T(8,128)S(1)}, f32[128,256]{0,1:T(8,128)S(1)}, u32[]{:S(2)}, u32[]{:S(2)}) collective-permute-start(f32[128,256]{0,1:T(8,128)S(1)} %add.94), channel_id=1, source_target_pairs={{0,112},{1,113},{2,114},{3,115},{4,116},{5,117},{6,118},{7,119},{8... | collective-permute-start | bytes 393224 | tf_op jit(solution)/shard_map/ppermute | solution.py:21
  101.2 12.5 %collective-permute-start.11 = (f32[128,256]{0,1:T(8,128)S(1)}, f32[128,256]{0,1:T(8,128)S(1)}, u32[]{:S(2)}, u32[]{:S(2)}) collective-permute-start(f32[128,256]{0,1:T(8,128)S(1)} %add.86), channel_id=1, source_target_pairs={{0,14},{1,15},{2,12},{3,13},{4,10},{5,11},{6,8},{7,9},{8,6},{9,7},... | collective-permute-start | bytes 393224 | tf_op jit(solution)/shard_map/ppermute | solution.py:21
  108.5 10.0 %collective-permute-start.20 = (f32[128,256]{0,1:T(8,128)S(1)}, f32[128,256]{0,1:T(8,128)S(1)}, u32[]{:S(2)}, u32[]{:S(2)}) collective-permute-start(f32[128,256]{0,1:T(8,128)S(1)} %add.95), channel_id=1, source_target_pairs={{0,14},{1,15},{2,12},{3,13},{4,10},{5,11},{6,8},{7,9},{8,6},{9,7},... | collective-permute-start | bytes 393224 | tf_op jit(solution)/shard_map/ppermute | solution.py:21
  113.7 9.5 %collective-permute-start.12 = (f32[128,256]{0,1:T(8,128)S(1)}, f32[128,256]{0,1:T(8,128)S(1)}, u32[]{:S(2)}, u32[]{:S(2)}) collective-permute-start(f32[128,256]{0,1:T(8,128)S(1)} %add.87), channel_id=1, source_target_pairs={{0,112},{1,113},{2,114},{3,115},{4,116},{5,117},{6,118},{7,119},{8... | collective-permute-start | bytes 393224 | tf_op jit(solution)/shard_map/ppermute | solution.py:21
  (2 other events, 10.4 us)
Sparse Core Ops, SparseCore 0:
  47.9 37.3 reduce-scatter.1

commit v5 on v4

--- a/solution.py
+++ b/solution.py
@@ -36,16 +36,18 @@
     x1, x2 = 1 << 7, (1 << 7) | (1 << 8)
     paired = summed_everywhere(local_weight, ("blk", "rep"), [[1]])
     paired, grad_pre = lax.optimization_barrier((paired, grad_pre))
-    raw_weight = summed_everywhere(
-        paired, ("blk", "rep"), [[y1, z1, x1, y2, z2, x2, y3, z3], [z1, x1, y1, z2, x2, y2, z3, y3]]
-    )
-    norm_value = jnp.sqrt(jnp.sum(raw_weight * raw_weight) + 1e-06)
-    grad_weight = raw_weight * jnp.minimum(1.0, 128.0 / norm_value)
+    early = summed_everywhere(paired, ("blk", "rep"), [[y1, z1, x1], [z1, x1, y1]])
     inv_root = 1.0 / jnp.sqrt(degree.astype(jnp.float32))
     backward = lax.dot_general(
         grad_pre, weight, (((1,), (1,)), ((), ())), preferred_element_type=jnp.float32
     )
     scaled = (backward * inv_root[:, None]).astype(jnp.bfloat16)
+    early, scaled = lax.optimization_barrier((early, scaled))
+    raw_weight = summed_everywhere(
+        early, ("blk", "rep"), [[y2, z2, x2, y3, z3], [z2, x2, y2, z3, y3]]
+    )
+    norm_value = jnp.sqrt(jnp.sum(raw_weight * raw_weight) + 1e-06)
+    grad_weight = raw_weight * jnp.minimum(1.0, 128.0 / norm_value)
 
     blocks = lax.axis_size("blk")
     replicas = lax.axis_size("rep")

time: 135 us -> 142 us (1.052)
  the two profiles are of different devices: /device:TPU:16 before, /device:TPU:6 now
where the time goes in v5:
time: 142 us; the launch traced here: 141 us
  starting transfers between devices  78.6 us (55%)
  waiting for transfers between devices  29.3 us (21%)
  between operations  15.2 us (11%)
  other arithmetic  8.65 us (6%)
  matrix products  5.65 us (4%)
  local copies, waits for them, and re-layouts  3.46 us (2%)
    ppermute x17, starting transfers between devices, summed_everywhere(): lax.ppermute(part, axes, [(i, i ^ order[step]) for i in range(size)])  58.9 us
    ppermute x17, waiting for transfers between devices, summed_everywhere(): lax.ppermute(part, axes, [(i, i ^ order[step]) for i in range(size)])  27.4 us
    ppermute x4, starting transfers between devices, fetched_from(): lax.ppermute(x, axis, [(i, (i - offset) % size) for i in range(size)])  19.6 us
    reduce_sum x1, other arithmetic, on_device(): jnp.sum((listed[:, :, :, :, None] == positions[None, None, None, None, :]...  4.16 us
  transfers between devices with their start and end apart: 22, of which 14 were waited for; matrix products, arithmetic and copies ran while one was open for 9% of the time, Pallas kernels for 0%

profile of v5, /device:TPU:6, one launch (start us, length us, event | category | flops | bytes accessed | tf_op | source)
XLA Modules:
  0.0 140.7 jit_solution(8691819899733835505)
XLA Ops:
  14.6 4.2 %convert_reduce_fusion = s32[5,4,128,128]{3,2,1,0:T(8,128)S(1)} fusion(s32[5,4,8,128]{3,2,1,0:T(8,128)S(1)} %broadcast_select_fusion), kind=kLoop, calls=%fused_computation.3 | loop fusion | flops 7536640 | bytes 1392640 | tf_op jit(solution)/shard_map/reduce_sum | solution.py:68
  18.8 3.5 %collective-permute-start.1 = (f32[128,256]{0,1:T(8,128)S(1)}, f32[128,256]{0,1:T(8,128)S(1)}, u32[]{:S(2)}, u32[]{:S(2)}) collective-permute-start(f32[128,256]{0,1:T(8,128)S(1)} %get-tuple-element.24), channel_id=1, source_target_pairs={{0,8},{1,9},{2,10},{3,11},{4,12},{5,13},{6,14},{7,15},{8,0},{9,1},... | collective-permute-start | bytes 393224 | tf_op jit(solution)/shard_map/ppermute | solution.py:21
  22.3 4.3 %collective-permute-start.4 = (f32[128,256]{0,1:T(8,128)S(1)}, f32[128,256]{0,1:T(8,128)S(1)}, u32[]{:S(2)}, u32[]{:S(2)}) collective-permute-start(f32[128,256]{0,1:T(8,128)S(1)} %get-tuple-element.25), channel_id=1, source_target_pairs={{0,16},{1,17},{2,18},{3,19},{4,20},{5,21},{6,22},{7,23},{8,24},{9,... | collective-permute-start | bytes 393224 | tf_op jit(solution)/shard_map/ppermute | solution.py:21
  26.7 3.8 %collective-permute-done.4 = f32[128,256]{0,1:T(8,128)S(1)} collective-permute-done((f32[128,256]{0,1:T(8,128)S(1)}, f32[128,256]{0,1:T(8,128)S(1)}, u32[]{:S(2)}, u32[]{:S(2)}) %collective-permute-start.4) | collective-permute-done | bytes 131104 | tf_op jit(solution)/shard_map/ppermute | solution.py:21
  30.5 2.7 %collective-permute-start.5 = (f32[128,256]{0,1:T(8,128)S(1)}, f32[128,256]{0,1:T(8,128)S(1)}, u32[]{:S(2)}, u32[]{:S(2)}) collective-permute-start(f32[128,256]{0,1:T(8,128)S(1)} %get-tuple-element.23), channel_id=1, source_target_pairs={{0,128},{1,129},{2,130},{3,131},{4,132},{5,133},{6,134},{7,135},{8... | collective-permute-start | bytes 393224 | tf_op jit(solution)/shard_map/ppermute | solution.py:21
  33.3 3.6 %collective-permute-start.2 = (f32[128,256]{0,1:T(8,128)S(1)}, f32[128,256]{0,1:T(8,128)S(1)}, u32[]{:S(2)}, u32[]{:S(2)}) collective-permute-start(f32[128,256]{0,1:T(8,128)S(1)} %get-tuple-element.22), channel_id=1, source_target_pairs={{0,16},{1,17},{2,18},{3,19},{4,20},{5,21},{6,22},{7,23},{8,24},{9,... | collective-permute-start | bytes 393224 | tf_op jit(solution)/shard_map/ppermute | solution.py:21
  40.1 3.1 %collective-permute-start.3 = (f32[128,256]{0,1:T(8,128)S(1)}, f32[128,256]{0,1:T(8,128)S(1)}, u32[]{:S(2)}, u32[]{:S(2)}) collective-permute-start(f32[128,256]{0,1:T(8,128)S(1)} %add.82), channel_id=1, source_target_pairs={{0,128},{1,129},{2,130},{3,131},{4,132},{5,133},{6,134},{7,135},{8... | collective-permute-start | bytes 393224 | tf_op jit(solution)/shard_map/ppermute | solution.py:21
  44.4 2.6 %collective-permute-done.3 = f32[128,256]{0,1:T(8,128)S(1)} collective-permute-done((f32[128,256]{0,1:T(8,128)S(1)}, f32[128,256]{0,1:T(8,128)S(1)}, u32[]{:S(2)}, u32[]{:S(2)}) %collective-permute-start.3) | collective-permute-done | bytes 131104 | tf_op jit(solution)/shard_map/ppermute | solution.py:21
  47.0 3.6 %collective-permute-start.7 = (bf16[128,256]{1,0:T(8,128)(2,1)S(1)}, bf16[128,256]{1,0:T(8,128)(2,1)S(1)}, u32[]{:S(2)}, u32[]{:S(2)}) collective-permute-start(bf16[128,256]{1,0:T(8,128)(2,1)S(1)} %fusion.2), channel_id=1, source_target_pairs={{0,16},{8,24},{16,32},{24,40},{32,48},{40,56},{48,64},{56,72},{64,... | collective-permute-start | bytes 196616 | tf_op jit(solution)/shard_map/ppermute | solution.py:11
  50.7 2.8 %convolution_bitcast_fusion = bf16[5,128,8,128]{3,2,1,0:T(8,128)(2,1)S(1)} fusion(s32[5,4,128,128]{3,2,1,0:T(8,128)S(1)} %convert_reduce_fusion, s32[5,4]{1,0:T(8,128)S(1)} %broadcast_select_fusion.1, pred[5,4]{1,0:T(8,128)(4,1)S(1)} %iota_compare_fusion.2), kind=kOutput, calls=%fused_computation.5 | convolution fusion | flops 5243200 | bytes 2621540 | tf_op jit(solution)/shard_map/tsn,tsic->tinc/dot_general | solution.py:76
  53.5 3.1 %collective-permute-start.8 = (bf16[128,256]{1,0:T(8,128)(2,1)S(1)}, bf16[128,256]{1,0:T(8,128)(2,1)S(1)}, u32[]{:S(2)}, u32[]{:S(2)}) collective-permute-start(bf16[128,256]{1,0:T(8,128)(2,1)S(1)} %fusion.2), channel_id=1, source_target_pairs={{0,8},{8,16},{16,24},{24,32},{32,40},{40,48},{48,56},{56,64},{64,7... | collective-permute-start | bytes 196616 | tf_op jit(solution)/shard_map/ppermute | solution.py:11
  56.7 8.3 %collective-permute-start.9 = (bf16[128,256]{1,0:T(8,128)(2,1)S(1)}, bf16[128,256]{1,0:T(8,128)(2,1)S(1)}, u32[]{:S(2)}, u32[]{:S(2)}) collective-permute-start(bf16[128,256]{1,0:T(8,128)(2,1)S(1)} %fusion.2), channel_id=1, source_target_pairs={{0,504},{8,0},{16,8},{24,16},{32,24},{40,32},{48,40},{56,48},{64,5... | collective-permute-start | bytes 196616 | tf_op jit(solution)/shard_map/ppermute | solution.py:11
  65.0 4.5 %collective-permute-start.10 = (bf16[128,256]{1,0:T(8,128)(2,1)S(1)}, bf16[128,256]{1,0:T(8,128)(2,1)S(1)}, u32[]{:S(2)}, u32[]{:S(2)}) collective-permute-start(bf16[128,256]{1,0:T(8,128)(2,1)S(1)} %fusion.2), channel_id=1, source_target_pairs={{0,496},{8,504},{16,0},{24,8},{32,16},{40,24},{48,32},{56,40},{64,... | collective-permute-start | bytes 196616 | tf_op jit(solution)/shard_map/ppermute | solution.py:11
  73.1 4.5 %collective-permute-start.11 = (f32[128,256]{0,1:T(8,128)S(1)}, f32[128,256]{0,1:T(8,128)S(1)}, u32[]{:S(2)}, u32[]{:S(2)}) collective-permute-start(f32[128,256]{0,1:T(8,128)S(1)} %get-tuple-element.20), channel_id=1, source_target_pairs={{0,2},{1,3},{2,0},{3,1},{4,6},{5,7},{6,4},{7,5},{8,10},{9,11},{10,... | collective-permute-start | bytes 393224 | tf_op jit(solution)/shard_map/ppermute | solution.py:21
  77.6 2.7 %collective-permute-start.16 = (f32[128,256]{0,1:T(8,128)S(1)}, f32[128,256]{0,1:T(8,128)S(1)}, u32[]{:S(2)}, u32[]{:S(2)}) collective-permute-start(f32[128,256]{0,1:T(8,128)S(1)} %get-tuple-element.21), channel_id=1, source_target_pairs={{0,32},{1,33},{2,34},{3,35},{4,36},{5,37},{6,38},{7,39},{8,40},{9,... | collective-permute-start | bytes 393224 | tf_op jit(solution)/shard_map/ppermute | solution.py:21
  81.6 5.1 %collective-permute-done.16 = f32[128,256]{0,1:T(8,128)S(1)} collective-permute-done((f32[128,256]{0,1:T(8,128)S(1)}, f32[128,256]{0,1:T(8,128)S(1)}, u32[]{:S(2)}, u32[]{:S(2)}) %collective-permute-start.16) | collective-permute-done | bytes 131104 | tf_op jit(solution)/shard_map/ppermute | solution.py:21
  86.8 3.6 %collective-permute-start.17 = (f32[128,256]{0,1:T(8,128)S(1)}, f32[128,256]{0,1:T(8,128)S(1)}, u32[]{:S(2)}, u32[]{:S(2)}) collective-permute-start(f32[128,256]{0,1:T(8,128)S(1)} %get-tuple-element.19), channel_id=1, source_target_pairs={{0,384},{1,385},{2,386},{3,387},{4,388},{5,389},{6,390},{7,391},{8... | collective-permute-start | bytes 393224 | tf_op jit(solution)/shard_map/ppermute | solution.py:21
  92.3 2.5 %collective-permute-done.17 = f32[128,256]{0,1:T(8,128)S(1)} collective-permute-done((f32[128,256]{0,1:T(8,128)S(1)}, f32[128,256]{0,1:T(8,128)S(1)}, u32[]{:S(2)}, u32[]{:S(2)}) %collective-permute-start.17) | collective-permute-done | bytes 131104 | tf_op jit(solution)/shard_map/ppermute | solution.py:21
  98.2 4.0 %collective-permute-start.13 = (f32[128,256]{0,1:T(8,128)S(1)}, f32[128,256]{0,1:T(8,128)S(1)}, u32[]{:S(2)}, u32[]{:S(2)}) collective-permute-start(f32[128,256]{0,1:T(8,128)S(1)} %add.88), channel_id=1, source_target_pairs={{0,384},{1,385},{2,386},{3,387},{4,388},{5,389},{6,390},{7,391},{8... | collective-permute-start | bytes 393224 | tf_op jit(solution)/shard_map/ppermute | solution.py:21
  104.4 4.7 %collective-permute-start.19 = (f32[128,256]{0,1:T(8,128)S(1)}, f32[128,256]{0,1:T(8,128)S(1)}, u32[]{:S(2)}, u32[]{:S(2)}) collective-permute-start(f32[128,256]{0,1:T(8,128)S(1)} %add.94), channel_id=1, source_target_pairs={{0,112},{1,113},{2,114},{3,115},{4,116},{5,117},{6,118},{7,119},{8... | collective-permute-start | bytes 393224 | tf_op jit(solution)/shard_map/ppermute | solution.py:21
  109.1 7.1 %collective-permute-start.14 = (f32[128,256]{0,1:T(8,128)S(1)}, f32[128,256]{0,1:T(8,128)S(1)}, u32[]{:S(2)}, u32[]{:S(2)}) collective-permute-start(f32[128,256]{0,1:T(8,128)S(1)} %add.89), channel_id=1, source_target_pairs={{0,14},{1,15},{2,12},{3,13},{4,10},{5,11},{6,8},{7,9},{8,6},{9,7},... | collective-permute-start | bytes 393224 | tf_op jit(solution)/shard_map/ppermute | solution.py:21
  116.3 2.9 %collective-permute-start.20 = (f32[128,256]{0,1:T(8,128)S(1)}, f32[128,256]{0,1:T(8,128)S(1)}, u32[]{:S(2)}, u32[]{:S(2)}) collective-permute-start(f32[128,256]{0,1:T(8,128)S(1)} %add.95), channel_id=1, source_target_pairs={{0,14},{1,15},{2,12},{3,13},{4,10},{5,11},{6,8},{7,9},{8,6},{9,7},... | collective-permute-start | bytes 393224 | tf_op jit(solution)/shard_map/ppermute | solution.py:21
  120.6 3.7 %collective-permute-start.15 = (f32[128,256]{0,1:T(8,128)S(1)}, f32[128,256]{0,1:T(8,128)S(1)}, u32[]{:S(2)}, u32[]{:S(2)}) collective-permute-start(f32[128,256]{0,1:T(8,128)S(1)} %add.90), channel_id=1, source_target_pairs={{0,112},{1,113},{2,114},{3,115},{4,116},{5,117},{6,118},{7,119},{8... | collective-permute-start | bytes 393224 | tf_op jit(solution)/shard_map/ppermute | solution.py:21
  125.8 4.3 %collective-permute-done.15 = f32[128,256]{0,1:T(8,128)S(1)} collective-permute-done((f32[128,256]{0,1:T(8,128)S(1)}, f32[128,256]{0,1:T(8,128)S(1)}, u32[]{:S(2)}, u32[]{:S(2)}) %collective-permute-start.15) | collective-permute-done | bytes 131104 | tf_op jit(solution)/shard_map/ppermute | solution.py:21
  (73 shorter events, 30.2 us)
Async XLA Ops:
  7.2 125.1 %reduce-scatter.2.cloned.1.call-start = ((), (), s32[]{:S(2)}) async-start(), calls=%async_computation.1 | async-start | bytes 1179648 | tf_op jit(solution)/shard_map/reduce_scatter | solution.py:80
  9.2 9.5 %collective-permute-start = (f32[256,256]{0,1:T(8,128)S(1)}, f32[256,256]{0,1:T(8,128)S(1)}, u32[]{:S(2)}, u32[]{:S(2)}) collective-permute-start(f32[256,256]{0,1:T(8,128)S(1)} %convolution_bitcast_fusion.2), channel_id=1, source_target_pairs={{0,1},{1,0},{2,3},{3,2},{4,5},{5,4},{6,7},{7,6},{8,9},{9,8},{10,11... | collective-permute-start | bytes 786440 | tf_op jit(solution)/shard_map/ppermute | solution.py:21
  18.7 18.2 %copy-start.3 = (s32[128]{0:T(128)S(1)}, s32[128]{0:T(128)}, u32[]{:S(2)}) copy-start(s32[128]{0:T(128)} %param.13) | copy-start | bytes 1540
  18.7 24.5 %copy-start.2 = (bf16[256,256]{1,0:T(8,128)(2,1)S(1)}, bf16[256,256]{1,0:T(8,128)(2,1)}, u32[]{:S(2)}) copy-start(bf16[256,256]{1,0:T(8,128)(2,1)} %param.12) | copy-start | bytes 393220
  18.8 7.9 %collective-permute-start.1 = (f32[128,256]{0,1:T(8,128)S(1)}, f32[128,256]{0,1:T(8,128)S(1)}, u32[]{:S(2)}, u32[]{:S(2)}) collective-permute-start(f32[128,256]{0,1:T(8,128)S(1)} %get-tuple-element.24), channel_id=1, source_target_pairs={{0,8},{1,9},{2,10},{3,11},{4,12},{5,13},{6,14},{7,15},{8,0},{9,1},... | collective-permute-start | bytes 393224 | tf_op jit(solution)/shard_map/ppermute | solution.py:21
  22.3 8.2 %collective-permute-start.4 = (f32[128,256]{0,1:T(8,128)S(1)}, f32[128,256]{0,1:T(8,128)S(1)}, u32[]{:S(2)}, u32[]{:S(2)}) collective-permute-start(f32[128,256]{0,1:T(8,128)S(1)} %get-tuple-element.25), channel_id=1, source_target_pairs={{0,16},{1,17},{2,18},{3,19},{4,20},{5,21},{6,22},{7,23},{8,24},{9,... | collective-permute-start | bytes 393224 | tf_op jit(solution)/shard_map/ppermute | solution.py:21
  30.5 7.0 %collective-permute-start.5 = (f32[128,256]{0,1:T(8,128)S(1)}, f32[128,256]{0,1:T(8,128)S(1)}, u32[]{:S(2)}, u32[]{:S(2)}) collective-permute-start(f32[128,256]{0,1:T(8,128)S(1)} %get-tuple-element.23), channel_id=1, source_target_pairs={{0,128},{1,129},{2,130},{3,131},{4,132},{5,133},{6,134},{7,135},{8... | collective-permute-start | bytes 393224 | tf_op jit(solution)/shard_map/ppermute | solution.py:21
  33.3 6.9 %collective-permute-start.2 = (f32[128,256]{0,1:T(8,128)S(1)}, f32[128,256]{0,1:T(8,128)S(1)}, u32[]{:S(2)}, u32[]{:S(2)}) collective-permute-start(f32[128,256]{0,1:T(8,128)S(1)} %get-tuple-element.22), channel_id=1, source_target_pairs={{0,16},{1,17},{2,18},{3,19},{4,20},{5,21},{6,22},{7,23},{8,24},{9,... | collective-permute-start | bytes 393224 | tf_op jit(solution)/shard_map/ppermute | solution.py:21
  37.5 6.9 %collective-permute-start.6 = (f32[128,256]{0,1:T(8,128)S(1)}, f32[128,256]{0,1:T(8,128)S(1)}, u32[]{:S(2)}, u32[]{:S(2)}) collective-permute-start(f32[128,256]{0,1:T(8,128)S(1)} %add.85), channel_id=1, source_target_pairs={{0,8},{1,9},{2,10},{3,11},{4,12},{5,13},{6,14},{7,15},{8,0},{9,1},... | collective-permute-start | bytes 393224 | tf_op jit(solution)/shard_map/ppermute | solution.py:21
  40.1 6.9 %collective-permute-start.3 = (f32[128,256]{0,1:T(8,128)S(1)}, f32[128,256]{0,1:T(8,128)S(1)}, u32[]{:S(2)}, u32[]{:S(2)}) collective-permute-start(f32[128,256]{0,1:T(8,128)S(1)} %add.82), channel_id=1, source_target_pairs={{0,128},{1,129},{2,130},{3,131},{4,132},{5,133},{6,134},{7,135},{8... | collective-permute-start | bytes 393224 | tf_op jit(solution)/shard_map/ppermute | solution.py:21
  47.0 22.5 %collective-permute-start.7 = (bf16[128,256]{1,0:T(8,128)(2,1)S(1)}, bf16[128,256]{1,0:T(8,128)(2,1)S(1)}, u32[]{:S(2)}, u32[]{:S(2)}) collective-permute-start(bf16[128,256]{1,0:T(8,128)(2,1)S(1)} %fusion.2), channel_id=1, source_target_pairs={{0,16},{8,24},{16,32},{24,40},{32,48},{40,56},{48,64},{56,72},{64,... | collective-permute-start | bytes 196616 | tf_op jit(solution)/shard_map/ppermute | solution.py:11
  53.5 16.0 %collective-permute-start.8 = (bf16[128,256]{1,0:T(8,128)(2,1)S(1)}, bf16[128,256]{1,0:T(8,128)(2,1)S(1)}, u32[]{:S(2)}, u32[]{:S(2)}) collective-permute-start(bf16[128,256]{1,0:T(8,128)(2,1)S(1)} %fusion.2), channel_id=1, source_target_pairs={{0,8},{8,16},{16,24},{24,32},{32,40},{40,48},{48,56},{56,64},{64,7... | collective-permute-start | bytes 196616 | tf_op jit(solution)/shard_map/ppermute | solution.py:11
  56.7 12.9 %collective-permute-start.9 = (bf16[128,256]{1,0:T(8,128)(2,1)S(1)}, bf16[128,256]{1,0:T(8,128)(2,1)S(1)}, u32[]{:S(2)}, u32[]{:S(2)}) collective-permute-start(bf16[128,256]{1,0:T(8,128)(2,1)S(1)} %fusion.2), channel_id=1, source_target_pairs={{0,504},{8,0},{16,8},{24,16},{32,24},{40,32},{48,40},{56,48},{64,5... | collective-permute-start | bytes 196616 | tf_op jit(solution)/shard_map/ppermute | solution.py:11
  65.0 6.4 %collective-permute-start.10 = (bf16[128,256]{1,0:T(8,128)(2,1)S(1)}, bf16[128,256]{1,0:T(8,128)(2,1)S(1)}, u32[]{:S(2)}, u32[]{:S(2)}) collective-permute-start(bf16[128,256]{1,0:T(8,128)(2,1)S(1)} %fusion.2), channel_id=1, source_target_pairs={{0,496},{8,504},{16,0},{24,8},{32,16},{40,24},{48,32},{56,40},{64,... | collective-permute-start | bytes 196616 | tf_op jit(solution)/shard_map/ppermute | solution.py:11
  73.1 8.6 %collective-permute-start.11 = (f32[128,256]{0,1:T(8,128)S(1)}, f32[128,256]{0,1:T(8,128)S(1)}, u32[]{:S(2)}, u32[]{:S(2)}) collective-permute-start(f32[128,256]{0,1:T(8,128)S(1)} %get-tuple-element.20), channel_id=1, source_target_pairs={{0,2},{1,3},{2,0},{3,1},{4,6},{5,7},{6,4},{7,5},{8,10},{9,11},{10,... | collective-permute-start | bytes 393224 | tf_op jit(solution)/shard_map/ppermute | solution.py:21
  77.6 9.2 %collective-permute-start.16 = (f32[128,256]{0,1:T(8,128)S(1)}, f32[128,256]{0,1:T(8,128)S(1)}, u32[]{:S(2)}, u32[]{:S(2)}) collective-permute-start(f32[128,256]{0,1:T(8,128)S(1)} %get-tuple-element.21), channel_id=1, source_target_pairs={{0,32},{1,33},{2,34},{3,35},{4,36},{5,37},{6,38},{7,39},{8,40},{9,... | collective-permute-start | bytes 393224 | tf_op jit(solution)/shard_map/ppermute | solution.py:21
  86.8 8.1 %collective-permute-start.17 = (f32[128,256]{0,1:T(8,128)S(1)}, f32[128,256]{0,1:T(8,128)S(1)}, u32[]{:S(2)}, u32[]{:S(2)}) collective-permute-start(f32[128,256]{0,1:T(8,128)S(1)} %get-tuple-element.19), channel_id=1, source_target_pairs={{0,384},{1,385},{2,386},{3,387},{4,388},{5,389},{6,390},{7,391},{8... | collective-permute-start | bytes 393224 | tf_op jit(solution)/shard_map/ppermute | solution.py:21
  90.4 7.9 %collective-permute-start.12 = (f32[128,256]{0,1:T(8,128)S(1)}, f32[128,256]{0,1:T(8,128)S(1)}, u32[]{:S(2)}, u32[]{:S(2)}) collective-permute-start(f32[128,256]{0,1:T(8,128)S(1)} %get-tuple-element.18), channel_id=1, source_target_pairs={{0,32},{1,33},{2,34},{3,35},{4,36},{5,37},{6,38},{7,39},{8,40},{9,... | collective-permute-start | bytes 393224 | tf_op jit(solution)/shard_map/ppermute | solution.py:21
  94.8 9.5 %collective-permute-start.18 = (f32[128,256]{0,1:T(8,128)S(1)}, f32[128,256]{0,1:T(8,128)S(1)}, u32[]{:S(2)}, u32[]{:S(2)}) collective-permute-start(f32[128,256]{0,1:T(8,128)S(1)} %add.93), channel_id=1, source_target_pairs={{0,2},{1,3},{2,0},{3,1},{4,6},{5,7},{6,4},{7,5},{8,10},{9,11},{10,... | collective-permute-start | bytes 393224 | tf_op jit(solution)/shard_map/ppermute | solution.py:21
  98.2 10.8 %collective-permute-start.13 = (f32[128,256]{0,1:T(8,128)S(1)}, f32[128,256]{0,1:T(8,128)S(1)}, u32[]{:S(2)}, u32[]{:S(2)}) collective-permute-start(f32[128,256]{0,1:T(8,128)S(1)} %add.88), channel_id=1, source_target_pairs={{0,384},{1,385},{2,386},{3,387},{4,388},{5,389},{6,390},{7,391},{8... | collective-permute-start | bytes 393224 | tf_op jit(solution)/shard_map/ppermute | solution.py:21
  104.4 11.9 %collective-permute-start.19 = (f32[128,256]{0,1:T(8,128)S(1)}, f32[128,256]{0,1:T(8,128)S(1)}, u32[]{:S(2)}, u32[]{:S(2)}) collective-permute-start(f32[128,256]{0,1:T(8,128)S(1)} %add.94), channel_id=1, source_target_pairs={{0,112},{1,113},{2,114},{3,115},{4,116},{5,117},{6,118},{7,119},{8... | collective-permute-start | bytes 393224 | tf_op jit(solution)/shard_map/ppermute | solution.py:21
  109.1 11.5 %collective-permute-start.14 = (f32[128,256]{0,1:T(8,128)S(1)}, f32[128,256]{0,1:T(8,128)S(1)}, u32[]{:S(2)}, u32[]{:S(2)}) collective-permute-start(f32[128,256]{0,1:T(8,128)S(1)} %add.89), channel_id=1, source_target_pairs={{0,14},{1,15},{2,12},{3,13},{4,10},{5,11},{6,8},{7,9},{8,6},{9,7},... | collective-permute-start | bytes 393224 | tf_op jit(solution)/shard_map/ppermute | solution.py:21
  116.3 9.5 %collective-permute-start.20 = (f32[128,256]{0,1:T(8,128)S(1)}, f32[128,256]{0,1:T(8,128)S(1)}, u32[]{:S(2)}, u32[]{:S(2)}) collective-permute-start(f32[128,256]{0,1:T(8,128)S(1)} %add.95), channel_id=1, source_target_pairs={{0,14},{1,15},{2,12},{3,13},{4,10},{5,11},{6,8},{7,9},{8,6},{9,7},... | collective-permute-start | bytes 393224 | tf_op jit(solution)/shard_map/ppermute | solution.py:21
  120.6 9.5 %collective-permute-start.15 = (f32[128,256]{0,1:T(8,128)S(1)}, f32[128,256]{0,1:T(8,128)S(1)}, u32[]{:S(2)}, u32[]{:S(2)}) collective-permute-start(f32[128,256]{0,1:T(8,128)S(1)} %add.90), channel_id=1, source_target_pairs={{0,112},{1,113},{2,114},{3,115},{4,116},{5,117},{6,118},{7,119},{8... | collective-permute-start | bytes 393224 | tf_op jit(solution)/shard_map/ppermute | solution.py:21
  (2 other events, 12.2 us)
Sparse Core Ops, SparseCore 0:
  73.1 45.2 reduce-scatter.1

commit v6 on v4

--- a/solution.py
+++ b/solution.py
@@ -34,10 +34,20 @@
     y1, y2, y3 = 1 << 3, 1 << 1, (1 << 1) | (1 << 2) | (1 << 3)
     z1, z2, z3 = 1 << 4, 1 << 5, (1 << 4) | (1 << 5) | (1 << 6)
     x1, x2 = 1 << 7, (1 << 7) | (1 << 8)
-    paired = summed_everywhere(local_weight, ("blk", "rep"), [[1]])
-    paired, grad_pre = lax.optimization_barrier((paired, grad_pre))
-    raw_weight = summed_everywhere(
-        paired, ("blk", "rep"), [[y1, z1, x1, y2, z2, x2, y3, z3], [z1, x1, y1, z2, x2, y2, z3, y3]]
+    devices = lax.axis_size("blk") * lax.axis_size("rep")
+    core = lax.axis_index("rep") % 2
+    rows_half = local_weight.shape[0] // 2
+    lower, upper = local_weight[:rows_half], local_weight[rows_half:]
+    kept = jnp.where(core == 0, lower, upper)
+    given = jnp.where(core == 0, upper, lower)
+    half = kept + lax.ppermute(given, ("blk", "rep"), [(i, i ^ 1) for i in range(devices)])
+    half, grad_pre = lax.optimization_barrier((half, grad_pre))
+    half = summed_everywhere(
+        half, ("blk", "rep"), [[y1, z1, x1, y2, z2, x2, y3, z3], [z1, x1, y1, z2, x2, y2, z3, y3]]
+    )
+    other = lax.ppermute(half, ("blk", "rep"), [(i, i ^ 1) for i in range(devices)])
+    raw_weight = jnp.where(
+        core == 0, jnp.concatenate([half, other]), jnp.concatenate([other, half])
     )
     norm_value = jnp.sqrt(jnp.sum(raw_weight * raw_weight) + 1e-06)
     grad_weight = raw_weight * jnp.minimum(1.0, 128.0 / norm_value)

time: 135 us -> 140 us (1.037)
  the two profiles are of different devices: /device:TPU:16 before, /device:TPU:1 now
where the time goes in v6:
time: 140 us; the launch traced here: 139 us
  starting transfers between devices  86.1 us (62%)
  waiting for transfers between devices  19.9 us (14%)
  between operations  15.3 us (11%)
  other arithmetic  9.06 us (6%)
  matrix products  5.65 us (4%)
  local copies, waits for them, and re-layouts  2.84 us (2%)
    ppermute x16, starting transfers between devices, summed_everywhere(): lax.ppermute(part, axes, [(i, i ^ order[step]) for i in range(size)])  50.2 us
    ppermute x16, waiting for transfers between devices, summed_everywhere(): lax.ppermute(part, axes, [(i, i ^ order[step]) for i in range(size)])  17.4 us
    ppermute x4, starting transfers between devices, fetched_from(): lax.ppermute(x, axis, [(i, (i - offset) % size) for i in range(size)])  15.7 us
    ppermute x1, starting transfers between devices, on_device(): lax.ppermute(half, ('blk', 'rep'), [(i, i ^ 1) for i in range(devices)])  11.3 us
    ppermute x1, starting transfers between devices, on_device(): lax.ppermute(given, ('blk', 'rep'), [(i, i ^ 1) for i in range(devices)])  8.79 us
    reduce_sum x1, other arithmetic, on_device(): jnp.sum((listed[:, :, :, :, None] == positions[None, None, None, None, :]...  4.15 us
    dot_general x1, matrix products, on_device(): merged = jnp.einsum('tsn,tsic->tinc', chooser, counts).astype(jnp.bfloat16)  2.81 us
  transfers between devices with their start and end apart: 23, of which 11 were waited for; matrix products, arithmetic and copies ran while one was open for 9% of the time, Pallas kernels for 0%

profile of v6, /device:TPU:1, one launch (start us, length us, event | category | flops | bytes accessed | tf_op | source)
XLA Modules:
  0.0 138.8 jit_solution(12993303666556133943)
XLA Ops:
  9.3 8.8 %collective-permute-start = (f32[128,256]{0,1:T(8,128)S(1)}, f32[128,256]{0,1:T(8,128)S(1)}, u32[]{:S(2)}, u32[]{:S(2)}) collective-permute-start(f32[128,256]{0,1:T(8,128)S(1)} %slice_select_fusion), channel_id=1, source_target_pairs={{0,1},{1,0},{2,3},{3,2},{4,5},{5,4},{6,7},{7,6},{8,9},{9,8},{10,11... | collective-permute-start | bytes 393224 | tf_op jit(solution)/shard_map/ppermute | solution.py:43
  19.5 4.2 %convert_reduce_fusion = s32[5,4,128,128]{3,2,1,0:T(8,128)S(1)} fusion(s32[5,4,8,128]{3,2,1,0:T(8,128)S(1)} %broadcast_select_fusion), kind=kLoop, calls=%fused_computation.3 | loop fusion | flops 7536640 | bytes 1392640 | tf_op jit(solution)/shard_map/reduce_sum | solution.py:76
  25.3 1.9 %collective-permute-start.1 = (bf16[128,256]{1,0:T(8,128)(2,1)S(1)}, bf16[128,256]{1,0:T(8,128)(2,1)S(1)}, u32[]{:S(2)}, u32[]{:S(2)}) collective-permute-start(bf16[128,256]{1,0:T(8,128)(2,1)S(1)} %fusion.2), channel_id=1, source_target_pairs={{0,16},{8,24},{16,32},{24,40},{32,48},{40,56},{48,64},{56,72},{64,... | collective-permute-start | bytes 196616 | tf_op jit(solution)/shard_map/ppermute | solution.py:11
  27.3 2.8 %convolution_bitcast_fusion = bf16[5,128,8,128]{3,2,1,0:T(8,128)(2,1)S(1)} fusion(s32[5,4,128,128]{3,2,1,0:T(8,128)S(1)} %convert_reduce_fusion, s32[5,4]{1,0:T(8,128)S(1)} %broadcast_select_fusion.1, pred[5,4]{1,0:T(8,128)(4,1)S(1)} %iota_compare_fusion.2), kind=kOutput, calls=%fused_computation.5 | convolution fusion | flops 5243200 | bytes 2621540 | tf_op jit(solution)/shard_map/tsn,tsic->tinc/dot_general | solution.py:84
  30.1 1.9 %collective-permute-start.2 = (bf16[128,256]{1,0:T(8,128)(2,1)S(1)}, bf16[128,256]{1,0:T(8,128)(2,1)S(1)}, u32[]{:S(2)}, u32[]{:S(2)}) collective-permute-start(bf16[128,256]{1,0:T(8,128)(2,1)S(1)} %fusion.2), channel_id=1, source_target_pairs={{0,8},{8,16},{16,24},{24,32},{32,40},{40,48},{48,56},{56,64},{64,7... | collective-permute-start | bytes 196616 | tf_op jit(solution)/shard_map/ppermute | solution.py:11
  32.0 8.5 %collective-permute-start.3 = (bf16[128,256]{1,0:T(8,128)(2,1)S(1)}, bf16[128,256]{1,0:T(8,128)(2,1)S(1)}, u32[]{:S(2)}, u32[]{:S(2)}) collective-permute-start(bf16[128,256]{1,0:T(8,128)(2,1)S(1)} %fusion.2), channel_id=1, source_target_pairs={{0,504},{8,0},{16,8},{24,16},{32,24},{40,32},{48,40},{56,48},{64,5... | collective-permute-start | bytes 196616 | tf_op jit(solution)/shard_map/ppermute | solution.py:11
  40.5 3.4 %collective-permute-start.4 = (bf16[128,256]{1,0:T(8,128)(2,1)S(1)}, bf16[128,256]{1,0:T(8,128)(2,1)S(1)}, u32[]{:S(2)}, u32[]{:S(2)}) collective-permute-start(bf16[128,256]{1,0:T(8,128)(2,1)S(1)} %fusion.2), channel_id=1, source_target_pairs={{0,496},{8,504},{16,0},{24,8},{32,16},{40,24},{48,32},{56,40},{64,... | collective-permute-start | bytes 196616 | tf_op jit(solution)/shard_map/ppermute | solution.py:11
  53.0 2.2 %collective-permute-done.13 = f32[64,256]{0,1:T(8,128)S(1)} collective-permute-done((f32[64,256]{0,1:T(8,128)S(1)}, f32[64,256]{0,1:T(8,128)S(1)}, u32[]{:S(2)}, u32[]{:S(2)}) %collective-permute-start.13) | collective-permute-done | bytes 65568 | tf_op jit(solution)/shard_map/ppermute | solution.py:21
  55.3 1.9 %collective-permute-start.14 = (f32[64,256]{0,1:T(8,128)S(1)}, f32[64,256]{0,1:T(8,128)S(1)}, u32[]{:S(2)}, u32[]{:S(2)}) collective-permute-start(f32[64,256]{0,1:T(8,128)S(1)} %get-tuple-element.15), channel_id=1, source_target_pairs={{0,128},{1,129},{2,130},{3,131},{4,132},{5,133},{6,134},{7,135},{8... | collective-permute-start | bytes 196616 | tf_op jit(solution)/shard_map/ppermute | solution.py:21
  61.0 3.1 %collective-permute-start.15 = (f32[64,256]{0,1:T(8,128)S(1)}, f32[64,256]{0,1:T(8,128)S(1)}, u32[]{:S(2)}, u32[]{:S(2)}) collective-permute-start(f32[64,256]{0,1:T(8,128)S(1)} %add.95), channel_id=1, source_target_pairs={{0,8},{1,9},{2,10},{3,11},{4,12},{5,13},{6,14},{7,15},{8,0},{9,1},... | collective-permute-start | bytes 196616 | tf_op jit(solution)/shard_map/ppermute | solution.py:21
  64.1 2.2 %collective-permute-start.7 = (f32[64,256]{0,1:T(8,128)S(1)}, f32[64,256]{0,1:T(8,128)S(1)}, u32[]{:S(2)}, u32[]{:S(2)}) collective-permute-start(f32[64,256]{0,1:T(8,128)S(1)} %add.87), channel_id=1, source_target_pairs={{0,128},{1,129},{2,130},{3,131},{4,132},{5,133},{6,134},{7,135},{8... | collective-permute-start | bytes 196616 | tf_op jit(solution)/shard_map/ppermute | solution.py:21
  66.3 1.9 %collective-permute-done.15 = f32[64,256]{0,1:T(8,128)S(1)} collective-permute-done((f32[64,256]{0,1:T(8,128)S(1)}, f32[64,256]{0,1:T(8,128)S(1)}, u32[]{:S(2)}, u32[]{:S(2)}) %collective-permute-start.15) | collective-permute-done | bytes 65568 | tf_op jit(solution)/shard_map/ppermute | solution.py:21
  68.3 2.6 %collective-permute-start.16 = (f32[64,256]{0,1:T(8,128)S(1)}, f32[64,256]{0,1:T(8,128)S(1)}, u32[]{:S(2)}, u32[]{:S(2)}) collective-permute-start(f32[64,256]{0,1:T(8,128)S(1)} %add.96), channel_id=1, source_target_pairs={{0,32},{1,33},{2,34},{3,35},{4,36},{5,37},{6,38},{7,39},{8,40},{9,... | collective-permute-start | bytes 196616 | tf_op jit(solution)/shard_map/ppermute | solution.py:21
  70.9 4.2 %collective-permute-start.8 = (f32[64,256]{0,1:T(8,128)S(1)}, f32[64,256]{0,1:T(8,128)S(1)}, u32[]{:S(2)}, u32[]{:S(2)}) collective-permute-start(f32[64,256]{0,1:T(8,128)S(1)} %add.88), channel_id=1, source_target_pairs={{0,2},{1,3},{2,0},{3,1},{4,6},{5,7},{6,4},{7,5},{8,10},{9,11},{10,... | collective-permute-start | bytes 196616 | tf_op jit(solution)/shard_map/ppermute | solution.py:21
  76.0 2.8 %collective-permute-start.17 = (f32[64,256]{0,1:T(8,128)S(1)}, f32[64,256]{0,1:T(8,128)S(1)}, u32[]{:S(2)}, u32[]{:S(2)}) collective-permute-start(f32[64,256]{0,1:T(8,128)S(1)} %add.97), channel_id=1, source_target_pairs={{0,384},{1,385},{2,386},{3,387},{4,388},{5,389},{6,390},{7,391},{8... | collective-permute-start | bytes 196616 | tf_op jit(solution)/shard_map/ppermute | solution.py:21
  80.4 4.5 %collective-permute-start.9 = (f32[64,256]{0,1:T(8,128)S(1)}, f32[64,256]{0,1:T(8,128)S(1)}, u32[]{:S(2)}, u32[]{:S(2)}) collective-permute-start(f32[64,256]{0,1:T(8,128)S(1)} %add.89), channel_id=1, source_target_pairs={{0,32},{1,33},{2,34},{3,35},{4,36},{5,37},{6,38},{7,39},{8,40},{9,... | collective-permute-start | bytes 196616 | tf_op jit(solution)/shard_map/ppermute | solution.py:21
  84.9 2.4 %collective-permute-start.18 = (f32[64,256]{0,1:T(8,128)S(1)}, f32[64,256]{0,1:T(8,128)S(1)}, u32[]{:S(2)}, u32[]{:S(2)}) collective-permute-start(f32[64,256]{0,1:T(8,128)S(1)} %add.98), channel_id=1, source_target_pairs={{0,2},{1,3},{2,0},{3,1},{4,6},{5,7},{6,4},{7,5},{8,10},{9,11},{10,... | collective-permute-start | bytes 196616 | tf_op jit(solution)/shard_map/ppermute | solution.py:21
  88.8 3.9 %collective-permute-start.10 = (f32[64,256]{0,1:T(8,128)S(1)}, f32[64,256]{0,1:T(8,128)S(1)}, u32[]{:S(2)}, u32[]{:S(2)}) collective-permute-start(f32[64,256]{0,1:T(8,128)S(1)} %add.90), channel_id=1, source_target_pairs={{0,384},{1,385},{2,386},{3,387},{4,388},{5,389},{6,390},{7,391},{8... | collective-permute-start | bytes 196616 | tf_op jit(solution)/shard_map/ppermute | solution.py:21
  93.3 3.9 %collective-permute-start.19 = (f32[64,256]{0,1:T(8,128)S(1)}, f32[64,256]{0,1:T(8,128)S(1)}, u32[]{:S(2)}, u32[]{:S(2)}) collective-permute-start(f32[64,256]{0,1:T(8,128)S(1)} %add.99), channel_id=1, source_target_pairs={{0,112},{1,113},{2,114},{3,115},{4,116},{5,117},{6,118},{7,119},{8... | collective-permute-start | bytes 196616 | tf_op jit(solution)/shard_map/ppermute | solution.py:21
  97.2 5.1 %collective-permute-start.11 = (f32[64,256]{0,1:T(8,128)S(1)}, f32[64,256]{0,1:T(8,128)S(1)}, u32[]{:S(2)}, u32[]{:S(2)}) collective-permute-start(f32[64,256]{0,1:T(8,128)S(1)} %add.91), channel_id=1, source_target_pairs={{0,14},{1,15},{2,12},{3,13},{4,10},{5,11},{6,8},{7,9},{8,6},{9,7},... | collective-permute-start | bytes 196616 | tf_op jit(solution)/shard_map/ppermute | solution.py:21
  102.3 4.8 %collective-permute-start.20 = (f32[64,256]{0,1:T(8,128)S(1)}, f32[64,256]{0,1:T(8,128)S(1)}, u32[]{:S(2)}, u32[]{:S(2)}) collective-permute-start(f32[64,256]{0,1:T(8,128)S(1)} %add.100), channel_id=1, source_target_pairs={{0,14},{1,15},{2,12},{3,13},{4,10},{5,11},{6,8},{7,9},{8,6},{9,7},... | collective-permute-start | bytes 196616 | tf_op jit(solution)/shard_map/ppermute | solution.py:21
  107.1 3.3 %collective-permute-start.12 = (f32[64,256]{0,1:T(8,128)S(1)}, f32[64,256]{0,1:T(8,128)S(1)}, u32[]{:S(2)}, u32[]{:S(2)}) collective-permute-start(f32[64,256]{0,1:T(8,128)S(1)} %add.92), channel_id=1, source_target_pairs={{0,112},{1,113},{2,114},{3,115},{4,116},{5,117},{6,118},{7,119},{8... | collective-permute-start | bytes 196616 | tf_op jit(solution)/shard_map/ppermute | solution.py:21
  110.4 5.0 %collective-permute-done.12 = f32[64,256]{0,1:T(8,128)S(1)} collective-permute-done((f32[64,256]{0,1:T(8,128)S(1)}, f32[64,256]{0,1:T(8,128)S(1)}, u32[]{:S(2)}, u32[]{:S(2)}) %collective-permute-start.12) | collective-permute-done | bytes 65568 | tf_op jit(solution)/shard_map/ppermute | solution.py:21
  115.5 11.3 %collective-permute-start.21 = (f32[128,256]{0,1:T(8,128)S(1)}, f32[128,256]{0,1:T(8,128)S(1)}, u32[]{:S(2)}, u32[]{:S(2)}) collective-permute-start(f32[128,256]{0,1:T(8,128)S(1)} %pad_maximum_fusion), channel_id=1, source_target_pairs={{0,1},{1,0},{2,3},{3,2},{4,5},{5,4},{6,7},{7,6},{8,9},{9,8},{10,11... | collective-permute-start | bytes 393224 | tf_op jit(solution)/shard_map/ppermute | solution.py:48
  (78 shorter events, 27.1 us)
Async XLA Ops:
  7.2 123.2 %reduce-scatter.2.cloned.1.call-start = ((), (), s32[]{:S(2)}) async-start(), calls=%async_computation.1 | async-start | bytes 1179648 | tf_op jit(solution)/shard_map/reduce_scatter | solution.py:88
  8.2 16.2 %copy-start.1 = (s32[1,1,64]{2,1,0:T(1,128)S(1)}, s32[1,1,64]{2,1,0:T(1,128)}, u32[]{:S(2)}) copy-start(s32[1,1,64]{2,1,0:T(1,128)} %param.16) | copy-start | bytes 772
  9.3 15.8 %collective-permute-start = (f32[128,256]{0,1:T(8,128)S(1)}, f32[128,256]{0,1:T(8,128)S(1)}, u32[]{:S(2)}, u32[]{:S(2)}) collective-permute-start(f32[128,256]{0,1:T(8,128)S(1)} %slice_select_fusion), channel_id=1, source_target_pairs={{0,1},{1,0},{2,3},{3,2},{4,5},{5,4},{6,7},{7,6},{8,9},{9,8},{10,11... | collective-permute-start | bytes 393224 | tf_op jit(solution)/shard_map/ppermute | solution.py:43
  25.3 18.5 %collective-permute-start.1 = (bf16[128,256]{1,0:T(8,128)(2,1)S(1)}, bf16[128,256]{1,0:T(8,128)(2,1)S(1)}, u32[]{:S(2)}, u32[]{:S(2)}) collective-permute-start(bf16[128,256]{1,0:T(8,128)(2,1)S(1)} %fusion.2), channel_id=1, source_target_pairs={{0,16},{8,24},{16,32},{24,40},{32,48},{40,56},{48,64},{56,72},{64,... | collective-permute-start | bytes 196616 | tf_op jit(solution)/shard_map/ppermute | solution.py:11
  30.1 13.8 %collective-permute-start.2 = (bf16[128,256]{1,0:T(8,128)(2,1)S(1)}, bf16[128,256]{1,0:T(8,128)(2,1)S(1)}, u32[]{:S(2)}, u32[]{:S(2)}) collective-permute-start(bf16[128,256]{1,0:T(8,128)(2,1)S(1)} %fusion.2), channel_id=1, source_target_pairs={{0,8},{8,16},{16,24},{24,32},{32,40},{40,48},{48,56},{56,64},{64,7... | collective-permute-start | bytes 196616 | tf_op jit(solution)/shard_map/ppermute | solution.py:11
  32.0 11.9 %collective-permute-start.3 = (bf16[128,256]{1,0:T(8,128)(2,1)S(1)}, bf16[128,256]{1,0:T(8,128)(2,1)S(1)}, u32[]{:S(2)}, u32[]{:S(2)}) collective-permute-start(bf16[128,256]{1,0:T(8,128)(2,1)S(1)} %fusion.2), channel_id=1, source_target_pairs={{0,504},{8,0},{16,8},{24,16},{32,24},{40,32},{48,40},{56,48},{64,5... | collective-permute-start | bytes 196616 | tf_op jit(solution)/shard_map/ppermute | solution.py:11
  40.5 5.0 %collective-permute-start.4 = (bf16[128,256]{1,0:T(8,128)(2,1)S(1)}, bf16[128,256]{1,0:T(8,128)(2,1)S(1)}, u32[]{:S(2)}, u32[]{:S(2)}) collective-permute-start(bf16[128,256]{1,0:T(8,128)(2,1)S(1)} %fusion.2), channel_id=1, source_target_pairs={{0,496},{8,504},{16,0},{24,8},{32,16},{40,24},{48,32},{56,40},{64,... | collective-permute-start | bytes 196616 | tf_op jit(solution)/shard_map/ppermute | solution.py:11
  47.3 5.7 %collective-permute-start.5 = (f32[64,256]{0,1:T(8,128)S(1)}, f32[64,256]{0,1:T(8,128)S(1)}, u32[]{:S(2)}, u32[]{:S(2)}) collective-permute-start(f32[64,256]{0,1:T(8,128)S(1)} %get-tuple-element.16), channel_id=1, source_target_pairs={{0,8},{1,9},{2,10},{3,11},{4,12},{5,13},{6,14},{7,15},{8,0},{9,1},... | collective-permute-start | bytes 196616 | tf_op jit(solution)/shard_map/ppermute | solution.py:21
  49.2 6.0 %collective-permute-start.13 = (f32[64,256]{0,1:T(8,128)S(1)}, f32[64,256]{0,1:T(8,128)S(1)}, u32[]{:S(2)}, u32[]{:S(2)}) collective-permute-start(f32[64,256]{0,1:T(8,128)S(1)} %get-tuple-element.17), channel_id=1, source_target_pairs={{0,16},{1,17},{2,18},{3,19},{4,20},{5,21},{6,22},{7,23},{8,24},{9,... | collective-permute-start | bytes 196616 | tf_op jit(solution)/shard_map/ppermute | solution.py:21
  55.3 5.7 %collective-permute-start.14 = (f32[64,256]{0,1:T(8,128)S(1)}, f32[64,256]{0,1:T(8,128)S(1)}, u32[]{:S(2)}, u32[]{:S(2)}) collective-permute-start(f32[64,256]{0,1:T(8,128)S(1)} %get-tuple-element.15), channel_id=1, source_target_pairs={{0,128},{1,129},{2,130},{3,131},{4,132},{5,133},{6,134},{7,135},{8... | collective-permute-start | bytes 196616 | tf_op jit(solution)/shard_map/ppermute | solution.py:21
  57.2 6.9 %collective-permute-start.6 = (f32[64,256]{0,1:T(8,128)S(1)}, f32[64,256]{0,1:T(8,128)S(1)}, u32[]{:S(2)}, u32[]{:S(2)}) collective-permute-start(f32[64,256]{0,1:T(8,128)S(1)} %get-tuple-element.14), channel_id=1, source_target_pairs={{0,16},{1,17},{2,18},{3,19},{4,20},{5,21},{6,22},{7,23},{8,24},{9,... | collective-permute-start | bytes 196616 | tf_op jit(solution)/shard_map/ppermute | solution.py:21
  61.0 7.2 %collective-permute-start.15 = (f32[64,256]{0,1:T(8,128)S(1)}, f32[64,256]{0,1:T(8,128)S(1)}, u32[]{:S(2)}, u32[]{:S(2)}) collective-permute-start(f32[64,256]{0,1:T(8,128)S(1)} %add.95), channel_id=1, source_target_pairs={{0,8},{1,9},{2,10},{3,11},{4,12},{5,13},{6,14},{7,15},{8,0},{9,1},... | collective-permute-start | bytes 196616 | tf_op jit(solution)/shard_map/ppermute | solution.py:21
  64.1 6.7 %collective-permute-start.7 = (f32[64,256]{0,1:T(8,128)S(1)}, f32[64,256]{0,1:T(8,128)S(1)}, u32[]{:S(2)}, u32[]{:S(2)}) collective-permute-start(f32[64,256]{0,1:T(8,128)S(1)} %add.87), channel_id=1, source_target_pairs={{0,128},{1,129},{2,130},{3,131},{4,132},{5,133},{6,134},{7,135},{8... | collective-permute-start | bytes 196616 | tf_op jit(solution)/shard_map/ppermute | solution.py:21
  68.3 7.7 %collective-permute-start.16 = (f32[64,256]{0,1:T(8,128)S(1)}, f32[64,256]{0,1:T(8,128)S(1)}, u32[]{:S(2)}, u32[]{:S(2)}) collective-permute-start(f32[64,256]{0,1:T(8,128)S(1)} %add.96), channel_id=1, source_target_pairs={{0,32},{1,33},{2,34},{3,35},{4,36},{5,37},{6,38},{7,39},{8,40},{9,... | collective-permute-start | bytes 196616 | tf_op jit(solution)/shard_map/ppermute | solution.py:21
  70.9 9.5 %collective-permute-start.8 = (f32[64,256]{0,1:T(8,128)S(1)}, f32[64,256]{0,1:T(8,128)S(1)}, u32[]{:S(2)}, u32[]{:S(2)}) collective-permute-start(f32[64,256]{0,1:T(8,128)S(1)} %add.88), channel_id=1, source_target_pairs={{0,2},{1,3},{2,0},{3,1},{4,6},{5,7},{6,4},{7,5},{8,10},{9,11},{10,... | collective-permute-start | bytes 196616 | tf_op jit(solution)/shard_map/ppermute | solution.py:21
  76.0 8.9 %collective-permute-start.17 = (f32[64,256]{0,1:T(8,128)S(1)}, f32[64,256]{0,1:T(8,128)S(1)}, u32[]{:S(2)}, u32[]{:S(2)}) collective-permute-start(f32[64,256]{0,1:T(8,128)S(1)} %add.97), channel_id=1, source_target_pairs={{0,384},{1,385},{2,386},{3,387},{4,388},{5,389},{6,390},{7,391},{8... | collective-permute-start | bytes 196616 | tf_op jit(solution)/shard_map/ppermute | solution.py:21
  80.4 8.4 %collective-permute-start.9 = (f32[64,256]{0,1:T(8,128)S(1)}, f32[64,256]{0,1:T(8,128)S(1)}, u32[]{:S(2)}, u32[]{:S(2)}) collective-permute-start(f32[64,256]{0,1:T(8,128)S(1)} %add.89), channel_id=1, source_target_pairs={{0,32},{1,33},{2,34},{3,35},{4,36},{5,37},{6,38},{7,39},{8,40},{9,... | collective-permute-start | bytes 196616 | tf_op jit(solution)/shard_map/ppermute | solution.py:21
  84.9 8.3 %collective-permute-start.18 = (f32[64,256]{0,1:T(8,128)S(1)}, f32[64,256]{0,1:T(8,128)S(1)}, u32[]{:S(2)}, u32[]{:S(2)}) collective-permute-start(f32[64,256]{0,1:T(8,128)S(1)} %add.98), channel_id=1, source_target_pairs={{0,2},{1,3},{2,0},{3,1},{4,6},{5,7},{6,4},{7,5},{8,10},{9,11},{10,... | collective-permute-start | bytes 196616 | tf_op jit(solution)/shard_map/ppermute | solution.py:21
  88.8 8.3 %collective-permute-start.10 = (f32[64,256]{0,1:T(8,128)S(1)}, f32[64,256]{0,1:T(8,128)S(1)}, u32[]{:S(2)}, u32[]{:S(2)}) collective-permute-start(f32[64,256]{0,1:T(8,128)S(1)} %add.90), channel_id=1, source_target_pairs={{0,384},{1,385},{2,386},{3,387},{4,388},{5,389},{6,390},{7,391},{8... | collective-permute-start | bytes 196616 | tf_op jit(solution)/shard_map/ppermute | solution.py:21
  93.3 9.0 %collective-permute-start.19 = (f32[64,256]{0,1:T(8,128)S(1)}, f32[64,256]{0,1:T(8,128)S(1)}, u32[]{:S(2)}, u32[]{:S(2)}) collective-permute-start(f32[64,256]{0,1:T(8,128)S(1)} %add.99), channel_id=1, source_target_pairs={{0,112},{1,113},{2,114},{3,115},{4,116},{5,117},{6,118},{7,119},{8... | collective-permute-start | bytes 196616 | tf_op jit(solution)/shard_map/ppermute | solution.py:21
  97.2 9.9 %collective-permute-start.11 = (f32[64,256]{0,1:T(8,128)S(1)}, f32[64,256]{0,1:T(8,128)S(1)}, u32[]{:S(2)}, u32[]{:S(2)}) collective-permute-start(f32[64,256]{0,1:T(8,128)S(1)} %add.91), channel_id=1, source_target_pairs={{0,14},{1,15},{2,12},{3,13},{4,10},{5,11},{6,8},{7,9},{8,6},{9,7},... | collective-permute-start | bytes 196616 | tf_op jit(solution)/shard_map/ppermute | solution.py:21
  102.3 8.1 %collective-permute-start.20 = (f32[64,256]{0,1:T(8,128)S(1)}, f32[64,256]{0,1:T(8,128)S(1)}, u32[]{:S(2)}, u32[]{:S(2)}) collective-permute-start(f32[64,256]{0,1:T(8,128)S(1)} %add.100), channel_id=1, source_target_pairs={{0,14},{1,15},{2,12},{3,13},{4,10},{5,11},{6,8},{7,9},{8,6},{9,7},... | collective-permute-start | bytes 196616 | tf_op jit(solution)/shard_map/ppermute | solution.py:21
  107.1 8.3 %collective-permute-start.12 = (f32[64,256]{0,1:T(8,128)S(1)}, f32[64,256]{0,1:T(8,128)S(1)}, u32[]{:S(2)}, u32[]{:S(2)}) collective-permute-start(f32[64,256]{0,1:T(8,128)S(1)} %add.92), channel_id=1, source_target_pairs={{0,112},{1,113},{2,114},{3,115},{4,116},{5,117},{6,118},{7,119},{8... | collective-permute-start | bytes 196616 | tf_op jit(solution)/shard_map/ppermute | solution.py:21
  115.5 12.3 %collective-permute-start.21 = (f32[128,256]{0,1:T(8,128)S(1)}, f32[128,256]{0,1:T(8,128)S(1)}, u32[]{:S(2)}, u32[]{:S(2)}) collective-permute-start(f32[128,256]{0,1:T(8,128)S(1)} %pad_maximum_fusion), channel_id=1, source_target_pairs={{0,1},{1,0},{2,3},{3,2},{4,5},{5,4},{6,7},{7,6},{8,9},{9,8},{10,11... | collective-permute-start | bytes 393224 | tf_op jit(solution)/shard_map/ppermute | solution.py:48
  (4 other events, 48.6 us)
Sparse Core Ops, SparseCore 0:
  47.3 41.0 reduce-scatter.1

commit v7 on v1

--- a/solution.py
+++ b/solution.py
@@ -16,9 +16,6 @@
     local_weight = lax.dot_general(
         aggregated, grad_pre, (((0,), (0,)), ((), ())), preferred_element_type=jnp.float32
     )
-    raw_weight = lax.psum(local_weight, ("blk", "rep"))
-    norm_value = jnp.sqrt(jnp.sum(raw_weight * raw_weight) + 1e-06)
-    grad_weight = raw_weight * jnp.minimum(1.0, 128.0 / norm_value)
     inv_root = 1.0 / jnp.sqrt(degree.astype(jnp.float32))
     backward = lax.dot_general(
         grad_pre, weight, (((1,), (1,)), ((), ())), preferred_element_type=jnp.float32
@@ -54,6 +51,17 @@
         "tinc,tif->ncf", merged, rows, preferred_element_type=jnp.float32
     )
     owned = lax.psum_scatter(totals, "rep", scatter_dimension=0, tiled=True)
+    local_weight, totals = lax.optimization_barrier((local_weight, totals))
+    devices = lax.axis_size("blk") * lax.axis_size("rep")
+    pieces = lax.all_to_all(
+        local_weight.reshape(devices, -1), ("blk", "rep"), 0, 0, tiled=True
+    )
+    piece = jnp.sum(pieces, axis=0)
+    raw_weight = lax.all_to_all(
+        jnp.broadcast_to(piece, (devices,) + piece.shape), ("blk", "rep"), 0, 0, tiled=True
+    ).reshape(local_weight.shape)
+    norm_value = jnp.sqrt(jnp.sum(raw_weight * raw_weight) + 1e-06)
+    grad_weight = raw_weight * jnp.minimum(1.0, 128.0 / norm_value)
     grad_features = (owned[0] * inv_root[:, None]).astype(jnp.bfloat16)
     return (grad_features, grad_weight)
 

time: 315 us -> 115 us (0.37)
  waiting for transfers between devices: 256 us -> 0.03 us
  blocking collectives: 0 us -> 58.7 us
    psum x1 -> x0, waiting for transfers between devices: 256 us -> none  [on_device(): raw_weight = lax.psum(local_weight, ('blk', 'rep'))]
    all_to_all x0 -> x2, blocking collectives: none -> 58.7 us  [the longest x1 32.2 us: on_device(): lax.all_to_all(local_weight.reshape(devices, -1), ('blk', 'rep'), 0, 0, t...]
  transfers between devices with their start and end apart: 6 -> 5, of which waited for: 1 -> 0; matrix products, arithmetic and copies ran while one was open for 5% -> 12% of each run, Pallas kernels for 0% -> 0%
where the time goes in v7:
time: 115 us; the launch traced here: 114 us
  blocking collectives  58.7 us (51%)
  starting transfers between devices  21.9 us (19%)
  between operations  15 us (13%)
  other arithmetic  9.79 us (9%)
  matrix products  5.8 us (5%)
  local copies, waits for them, and re-layouts  2.98 us (3%)
    all_to_all x1, blocking collectives, on_device(): lax.all_to_all(local_weight.reshape(devices, -1), ('blk', 'rep'), 0, 0, t...  32.2 us
    all_to_all x1, blocking collectives, on_device(): lax.all_to_all(jnp.broadcast_to(piece, (devices,) + piece.shape), ('blk',...  26.5 us
    ppermute x4, starting transfers between devices, fetched_from(): lax.ppermute(x, axis, [(i, (i - offset) % size) for i in range(size)])  21.9 us
    reduce_sum x1, other arithmetic, on_device(): jnp.sum((listed[:, :, :, :, None] == positions[None, None, None, None, :]...  4.15 us
    dot_general x1, matrix products, on_device(): merged = jnp.einsum('tsn,tsic->tinc', chooser, counts).astype(jnp.bfloat16)  2.82 us
  transfers between devices with their start and end apart: 5, of which 0 were waited for; matrix products, arithmetic and copies ran while one was open for 12% of the time, Pallas kernels for 0%

profile of v7, /device:TPU:1, one launch (start us, length us, event | category | flops | bytes accessed | tf_op | source)
XLA Modules:
  0.0 114.2 jit_solution(12763210780142184754)
XLA Ops:
  7.2 0.7 convert_rsqrt_fusion
  8.0 1.2 %fusion.2 = bf16[128,256]{1,0:T(8,128)(2,1)S(1)} fusion(bf16[256,256]{1,0:T(8,128)(2,1)} %param.12, f32[128]{0:T(128)S(1)} %convert_rsqrt_fusion, bf16[128,256]{1,0:T(8,128)(2,1)} %param.9, bf16[128,256]{1,0:T(8,128)(2,1)} %param.10), kind=kOutput, calls=%fused_computation.11 | convolution fusion | flops 16908288 | bytes 328192 | tf_op jit(solution)/shard_map/dot_general | solution.py:20
  9.2 4.8 %collective-permute-start = (bf16[128,256]{1,0:T(8,128)(2,1)S(1)}, bf16[128,256]{1,0:T(8,128)(2,1)S(1)}, u32[]{:S(2)}, u32[]{:S(2)}) collective-permute-start(bf16[128,256]{1,0:T(8,128)(2,1)S(1)} %fusion.2), channel_id=1, source_target_pairs={{0,16},{8,24},{16,32},{24,40},{32,48},{40,56},{48,64},{56,72},{64,... | collective-permute-start | bytes 196616 | tf_op jit(solution)/shard_map/ppermute | solution.py:11
  14.0 3.2 %collective-permute-start.1 = (bf16[128,256]{1,0:T(8,128)(2,1)S(1)}, bf16[128,256]{1,0:T(8,128)(2,1)S(1)}, u32[]{:S(2)}, u32[]{:S(2)}) collective-permute-start(bf16[128,256]{1,0:T(8,128)(2,1)S(1)} %fusion.2), channel_id=1, source_target_pairs={{0,8},{8,16},{16,24},{24,32},{32,40},{40,48},{48,56},{56,64},{64,7... | collective-permute-start | bytes 196616 | tf_op jit(solution)/shard_map/ppermute | solution.py:11
  17.2 10.5 %collective-permute-start.2 = (bf16[128,256]{1,0:T(8,128)(2,1)S(1)}, bf16[128,256]{1,0:T(8,128)(2,1)S(1)}, u32[]{:S(2)}, u32[]{:S(2)}) collective-permute-start(bf16[128,256]{1,0:T(8,128)(2,1)S(1)} %fusion.2), channel_id=1, source_target_pairs={{0,504},{8,0},{16,8},{24,16},{32,24},{40,32},{48,40},{56,48},{64,5... | collective-permute-start | bytes 196616 | tf_op jit(solution)/shard_map/ppermute | solution.py:11
  27.7 3.4 %collective-permute-start.3 = (bf16[128,256]{1,0:T(8,128)(2,1)S(1)}, bf16[128,256]{1,0:T(8,128)(2,1)S(1)}, u32[]{:S(2)}, u32[]{:S(2)}) collective-permute-start(bf16[128,256]{1,0:T(8,128)(2,1)S(1)} %fusion.2), channel_id=1, source_target_pairs={{0,496},{8,504},{16,0},{24,8},{32,16},{40,24},{48,32},{56,40},{64,... | collective-permute-start | bytes 196616 | tf_op jit(solution)/shard_map/ppermute | solution.py:11
  31.1 0.7 compare_and_fusion
  31.8 0.6 gather_fusion
  32.4 4.2 %convert_reduce_fusion = s32[5,4,128,128]{3,2,1,0:T(8,128)S(1)} fusion(s32[5,4,8,128]{3,2,1,0:T(8,128)S(1)} %broadcast_select_fusion), kind=kLoop, calls=%fused_computation.3 | loop fusion | flops 7536640 | bytes 1392640 | tf_op jit(solution)/shard_map/reduce_sum | solution.py:41
  36.6 0.1 copy.18
  36.7 0.6 gather_fusion.1
  37.3 0.6 gather_fusion.2
  38.1 2.8 %convolution_bitcast_fusion = bf16[5,128,8,128]{3,2,1,0:T(8,128)(2,1)S(1)} fusion(s32[5,4,128,128]{3,2,1,0:T(8,128)S(1)} %convert_reduce_fusion, s32[5,4]{1,0:T(8,128)S(1)} %broadcast_select_fusion.1, pred[5,4]{1,0:T(8,128)(4,1)S(1)} %iota_compare_fusion.2), kind=kOutput, calls=%fused_computation.5 | convolution fusion | flops 5243200 | bytes 2621540 | tf_op jit(solution)/shard_map/tsn,tsic->tinc/dot_general | solution.py:49
  41.0 1.6 %convolution_bitcast_fusion.1 = f32[8,128,256]{2,1,0:T(8,128)} fusion(bf16[5,128,8,128]{3,2,1,0:T(8,128)(2,1)S(1)} %convolution_bitcast_fusion, bf16[5,128,256]{2,1,0:T(8,128)(2,1)S(1)} %bitcast_dynamic-update-slice_fusion), kind=kOutput, calls=%fused_computation.6 | convolution fusion | flops 335544320 | bytes 2686976 | tf_op jit(solution)/shard_map/tinc,tif->ncf/dot_general | solution.py:50
  42.7 0.2 convolution_bitcast_fusion.2
  42.9 0.1 copy.21
  43.1 32.2 %all_to_all.15 = f32[512,1,128]{2,1,0:T(1,128)S(1)} all-to-all(f32[512,1,128]{2,1,0:T(1,128)S(1)} %bitcast.37), channel_id=1, replica_groups=mesh['blk'=64,'rep'=8] {'blk','rep'}, dimensions={0} | all-to-all | bytes 524288 | tf_op jit(solution)/shard_map/all_to_all | solution.py:56
  75.2 0.6 reduce_sum.28
  75.8 0.1 broadcast_in_dim.36
  75.9 26.5 %all_to_all.16 = f32[512,1,128]{2,1,0:T(1,128)S(1)} all-to-all(f32[512,1,128]{2,1,0:T(1,128)S(1)} %broadcast_in_dim.36), channel_id=1, replica_groups=mesh['blk'=64,'rep'=8] {'blk','rep'}, dimensions={0} | all-to-all | bytes 524288 | tf_op jit(solution)/shard_map/all_to_all | solution.py:60
  102.5 1.1 multiply_reduce_fusion.1
  104.3 0.7 multiply_reduce_fusion
  105.0 0.8 mul.34
  105.7 1.6 %fusion.4 = bf16[128,256]{1,0:T(8,128)(2,1)} fusion(f32[1,128,256]{2,1,0:T(8,128)} %reduce-scatter.2.cloned.1.call-done, f32[128]{0:T(128)S(1)} %convert_rsqrt_fusion), kind=kLoop, calls=%fused_computation.16 | loop fusion | flops 65536 | bytes 197120 | tf_op jit(solution)/shard_map/convert_element_type | solution.py:65
  (30 shorter events, 0.4 us)
Async XLA Ops:
  7.2 24.6 %copy-start = (s32[1,1,64,4,8,128]{5,4,3,2,1,0:T(8,128)S(1)}, s32[1,1,64,4,8,128]{5,4,3,2,1,0:T(8,128)}, u32[]{:S(2)}) copy-start(s32[1,1,64,4,8,128]{5,4,3,2,1,0:T(8,128)} %param.14) | copy-start | bytes 3145732
  7.2 29.4 %copy-start.5 = (s32[1,1,64,4]{2,3,1,0:T(4,128)S(1)}, s32[1,1,64,4]{2,3,1,0:T(4,128)}, u32[]{:S(2)}) copy-start(s32[1,1,64,4]{2,3,1,0:T(4,128)} %param.15) | copy-start | bytes 3076
  7.2 30.1 %copy-start.1 = (s32[1,1,64]{2,1,0:T(1,128)S(1)}, s32[1,1,64]{2,1,0:T(1,128)}, u32[]{:S(2)}) copy-start(s32[1,1,64]{2,1,0:T(1,128)} %param.16) | copy-start | bytes 772
  7.2 98.5 %reduce-scatter.2.cloned.1.call-start = ((), (), s32[]{:S(2)}) async-start(), calls=%async_computation.3 | async-start | bytes 1179648 | tf_op jit(solution)/shard_map/reduce_scatter | solution.py:53
  9.2 31.7 %collective-permute-start = (bf16[128,256]{1,0:T(8,128)(2,1)S(1)}, bf16[128,256]{1,0:T(8,128)(2,1)S(1)}, u32[]{:S(2)}, u32[]{:S(2)}) collective-permute-start(bf16[128,256]{1,0:T(8,128)(2,1)S(1)} %fusion.2), channel_id=1, source_target_pairs={{0,16},{8,24},{16,32},{24,40},{32,48},{40,56},{48,64},{56,72},{64,... | collective-permute-start | bytes 196616 | tf_op jit(solution)/shard_map/ppermute | solution.py:11
  14.0 26.9 %collective-permute-start.1 = (bf16[128,256]{1,0:T(8,128)(2,1)S(1)}, bf16[128,256]{1,0:T(8,128)(2,1)S(1)}, u32[]{:S(2)}, u32[]{:S(2)}) collective-permute-start(bf16[128,256]{1,0:T(8,128)(2,1)S(1)} %fusion.2), channel_id=1, source_target_pairs={{0,8},{8,16},{16,24},{24,32},{32,40},{40,48},{48,56},{56,64},{64,7... | collective-permute-start | bytes 196616 | tf_op jit(solution)/shard_map/ppermute | solution.py:11
  17.2 23.7 %collective-permute-start.2 = (bf16[128,256]{1,0:T(8,128)(2,1)S(1)}, bf16[128,256]{1,0:T(8,128)(2,1)S(1)}, u32[]{:S(2)}, u32[]{:S(2)}) collective-permute-start(bf16[128,256]{1,0:T(8,128)(2,1)S(1)} %fusion.2), channel_id=1, source_target_pairs={{0,504},{8,0},{16,8},{24,16},{32,24},{40,32},{48,40},{56,48},{64,5... | collective-permute-start | bytes 196616 | tf_op jit(solution)/shard_map/ppermute | solution.py:11
  27.7 13.3 %collective-permute-start.3 = (bf16[128,256]{1,0:T(8,128)(2,1)S(1)}, bf16[128,256]{1,0:T(8,128)(2,1)S(1)}, u32[]{:S(2)}, u32[]{:S(2)}) collective-permute-start(bf16[128,256]{1,0:T(8,128)(2,1)S(1)} %fusion.2), channel_id=1, source_target_pairs={{0,496},{8,504},{16,0},{24,8},{32,16},{40,24},{48,32},{56,40},{64,... | collective-permute-start | bytes 196616 | tf_op jit(solution)/shard_map/ppermute | solution.py:11
  41.0 1.7 %copy-start.2 = (bf16[128,256]{1,0:T(8,128)(2,1)S(1)}, bf16[128,256]{1,0:T(8,128)(2,1)}, u32[]{:S(2)}) copy-start(bf16[128,256]{1,0:T(8,128)(2,1)} %param.9) | copy-start | bytes 196612
  41.0 1.7 %copy-start.3 = (bf16[128,256]{1,0:T(8,128)(2,1)S(1)}, bf16[128,256]{1,0:T(8,128)(2,1)}, u32[]{:S(2)}) copy-start(bf16[128,256]{1,0:T(8,128)(2,1)} %param.10) | copy-start | bytes 196612
  41.0 1.7 %copy-start.4 = (bf16[128,256]{1,0:T(8,128)(2,1)S(1)}, bf16[128,256]{1,0:T(8,128)(2,1)}, u32[]{:S(2)}) copy-start(bf16[128,256]{1,0:T(8,128)(2,1)} %param.11) | copy-start | bytes 196612
Sparse Core Ops, SparseCore 0:
  42.8 41.2 reduce-scatter.1

commit v8 on v7

--- a/solution.py
+++ b/solution.py
@@ -39,14 +39,16 @@
     positions = jnp.arange(tile_side, dtype=jnp.int32)
     slot_index = jnp.arange(slots_total, dtype=jnp.int32)
     counts = jnp.sum(
-        (listed[:, :, :, :, None] == positions[None, None, None, None, :]).astype(jnp.int32),
+        (listed[:, :, :, :, None] == positions[None, None, None, None, :]).astype(jnp.bfloat16),
         axis=2,
     )
     chooser = jnp.logical_and(
         column_ids[:, :, None] == jnp.arange(replicas, dtype=jnp.int32)[None, None, :],
         (slot_index[None, :] < present[:, None])[:, :, None],
-    ).astype(jnp.int32)
-    merged = jnp.einsum("tsn,tsic->tinc", chooser, counts).astype(jnp.bfloat16)
+    ).astype(jnp.bfloat16)
+    merged = jnp.sum(
+        chooser[:, :, None, :, None] * counts[:, :, :, None, :], axis=1
+    )
     totals = jnp.einsum(
         "tinc,tif->ncf", merged, rows, preferred_element_type=jnp.float32
     )

time: 115 us -> 114 us (level)
  matrix products: 5.8 us -> 2.98 us
  local copies, waits for them, and re-layouts: 2.98 us -> 4.31 us
  other arithmetic: 9.79 us -> 11.1 us
    dot_general x1 -> x0, matrix products: 2.82 us -> none  [on_device(): merged = jnp.einsum('tsn,tsic->tinc', chooser, counts).astype(jnp.bfloat16)]
where the time goes in v8:
time: 114 us
  blocking collectives  58.7 us (51%)
  starting transfers between devices  21.9 us (19%)
  between operations  15 us (13%)
  other arithmetic  11.1 us (10%)
  local copies, waits for them, and re-layouts  4.31 us (4%)
  matrix products  2.98 us (3%)
    all_to_all x1, blocking collectives, on_device(): lax.all_to_all(local_weight.reshape(devices, -1), ('blk', 'rep'), 0, 0, t...  32.2 us
    all_to_all x1, blocking collectives, on_device(): lax.all_to_all(jnp.broadcast_to(piece, (devices,) + piece.shape), ('blk',...  26.5 us
    ppermute x4, starting transfers between devices, fetched_from(): lax.ppermute(x, axis, [(i, (i - offset) % size) for i in range(size)])  21.9 us
    reduce_sum x1, other arithmetic, on_device(): jnp.sum((listed[:, :, :, :, None] == positions[None, None, None, None, :]...  4.21 us
  transfers between devices with their start and end apart: 5, of which 0 were waited for; matrix products, arithmetic and copies ran while one was open for 12% of the time, Pallas kernels for 0%

profile of v8, /device:TPU:1, one launch (start us, length us, event | category | flops | bytes accessed | tf_op | source)
XLA Modules:
  0.0 114.0 jit_solution(7978112820933680681)
XLA Ops:
  7.2 0.7 convert_rsqrt_fusion
  8.0 1.2 %fusion.3 = bf16[128,256]{1,0:T(8,128)(2,1)S(1)} fusion(bf16[256,256]{1,0:T(8,128)(2,1)} %param.12, f32[128]{0:T(128)S(1)} %convert_rsqrt_fusion, bf16[128,256]{1,0:T(8,128)(2,1)} %param.9, bf16[128,256]{1,0:T(8,128)(2,1)} %param.10), kind=kOutput, calls=%fused_computation.11 | convolution fusion | flops 16908288 | bytes 328192 | tf_op jit(solution)/shard_map/dot_general | solution.py:20
  9.1 4.8 %collective-permute-start = (bf16[128,256]{1,0:T(8,128)(2,1)S(1)}, bf16[128,256]{1,0:T(8,128)(2,1)S(1)}, u32[]{:S(2)}, u32[]{:S(2)}) collective-permute-start(bf16[128,256]{1,0:T(8,128)(2,1)S(1)} %fusion.3), channel_id=1, source_target_pairs={{0,16},{8,24},{16,32},{24,40},{32,48},{40,56},{48,64},{56,72},{64,... | collective-permute-start | bytes 196616 | tf_op jit(solution)/shard_map/ppermute | solution.py:11
  14.0 3.2 %collective-permute-start.1 = (bf16[128,256]{1,0:T(8,128)(2,1)S(1)}, bf16[128,256]{1,0:T(8,128)(2,1)S(1)}, u32[]{:S(2)}, u32[]{:S(2)}) collective-permute-start(bf16[128,256]{1,0:T(8,128)(2,1)S(1)} %fusion.3), channel_id=1, source_target_pairs={{0,8},{8,16},{16,24},{24,32},{32,40},{40,48},{48,56},{56,64},{64,7... | collective-permute-start | bytes 196616 | tf_op jit(solution)/shard_map/ppermute | solution.py:11
  17.2 10.5 %collective-permute-start.2 = (bf16[128,256]{1,0:T(8,128)(2,1)S(1)}, bf16[128,256]{1,0:T(8,128)(2,1)S(1)}, u32[]{:S(2)}, u32[]{:S(2)}) collective-permute-start(bf16[128,256]{1,0:T(8,128)(2,1)S(1)} %fusion.3), channel_id=1, source_target_pairs={{0,504},{8,0},{16,8},{24,16},{32,24},{40,32},{48,40},{56,48},{64,5... | collective-permute-start | bytes 196616 | tf_op jit(solution)/shard_map/ppermute | solution.py:11
  27.7 3.4 %collective-permute-start.3 = (bf16[128,256]{1,0:T(8,128)(2,1)S(1)}, bf16[128,256]{1,0:T(8,128)(2,1)S(1)}, u32[]{:S(2)}, u32[]{:S(2)}) collective-permute-start(bf16[128,256]{1,0:T(8,128)(2,1)S(1)} %fusion.3), channel_id=1, source_target_pairs={{0,496},{8,504},{16,0},{24,8},{32,16},{40,24},{48,32},{56,40},{64,... | collective-permute-start | bytes 196616 | tf_op jit(solution)/shard_map/ppermute | solution.py:11
  31.1 0.7 compare_and_fusion
  31.8 0.8 copy.17
  32.5 0.6 gather_fusion
  33.1 1.3 %gather_fusion.1 = s32[5]{0:T(128)S(1)} fusion(s32[64]{0:T(128)} %bitcast.29, s32[1024]{0:T(1024)S(1)} %pad_clamp_fusion), kind=kCustom, calls=%fused_computation.1 | custom fusion | bytes 60 | tf_op jit(solution)/shard_map/jit(_take)/gather | solution.py:35
  34.5 0.6 gather_fusion.2
  35.2 4.2 %fusion.1 = bf16[5,4,128,128]{3,2,1,0:T(8,128)(2,1)S(1)} fusion(s32[5,4,8,128]{3,2,1,0:T(8,128)S(1)} %broadcast_select_fusion), kind=kLoop, calls=%fused_computation.5 | loop fusion | flops 7536640 | bytes 737280 | tf_op jit(solution)/shard_map/reduce_sum | solution.py:41
  39.5 1.1 multiply_reduce_fusion
  40.8 1.6 %convolution_bitcast_fusion = f32[8,128,256]{2,1,0:T(8,128)} fusion(bf16[5,128,8,128]{3,2,1,0:T(8,128)(2,1)S(1)} %multiply_reduce_fusion, bf16[5,128,256]{2,1,0:T(8,128)(2,1)S(1)} %bitcast_dynamic-update-slice_fusion), kind=kOutput, calls=%fused_computation.7 | convolution fusion | flops 335544320 | bytes 2686976 | tf_op jit(solution)/shard_map/tinc,tif->ncf/dot_general | solution.py:52
  42.5 0.2 convolution_bitcast_fusion.1
  42.7 0.1 copy.19
  42.8 32.2 %all_to_all.15 = f32[512,1,128]{2,1,0:T(1,128)S(1)} all-to-all(f32[512,1,128]{2,1,0:T(1,128)S(1)} %bitcast.30), channel_id=1, replica_groups=mesh['blk'=64,'rep'=8] {'blk','rep'}, dimensions={0} | all-to-all | bytes 524288 | tf_op jit(solution)/shard_map/all_to_all | solution.py:58
  75.0 0.6 reduce_sum.44
  75.5 0.1 broadcast_in_dim.38
  75.7 26.5 %all_to_all.16 = f32[512,1,128]{2,1,0:T(1,128)S(1)} all-to-all(f32[512,1,128]{2,1,0:T(1,128)S(1)} %broadcast_in_dim.38), channel_id=1, replica_groups=mesh['blk'=64,'rep'=8] {'blk','rep'}, dimensions={0} | all-to-all | bytes 524288 | tf_op jit(solution)/shard_map/all_to_all | solution.py:62
  102.2 1.1 multiply_reduce_fusion.2
  104.0 0.7 multiply_reduce_fusion.1
  104.7 0.8 mul.50
  105.5 1.6 %fusion.5 = bf16[128,256]{1,0:T(8,128)(2,1)} fusion(f32[1,128,256]{2,1,0:T(8,128)} %reduce-scatter.2.cloned.1.call-done, f32[128]{0:T(128)S(1)} %convert_rsqrt_fusion), kind=kLoop, calls=%fused_computation.16 | loop fusion | flops 65536 | bytes 197120 | tf_op jit(solution)/shard_map/convert_element_type | solution.py:67
  (27 shorter events, 0.5 us)
Async XLA Ops:
  7.2 27.3 %copy-start = (s32[1,1,64,4,8,128]{5,4,3,2,1,0:T(8,128)S(1)}, s32[1,1,64,4,8,128]{5,4,3,2,1,0:T(8,128)}, u32[]{:S(2)}) copy-start(s32[1,1,64,4,8,128]{5,4,3,2,1,0:T(8,128)} %param.14) | copy-start | bytes 3145732
  7.2 98.3 %reduce-scatter.2.cloned.1.call-start = ((), (), s32[]{:S(2)}) async-start(), calls=%async_computation.3 | async-start | bytes 1179648 | tf_op jit(solution)/shard_map/reduce_scatter | solution.py:55
  9.1 31.5 %collective-permute-start = (bf16[128,256]{1,0:T(8,128)(2,1)S(1)}, bf16[128,256]{1,0:T(8,128)(2,1)S(1)}, u32[]{:S(2)}, u32[]{:S(2)}) collective-permute-start(bf16[128,256]{1,0:T(8,128)(2,1)S(1)} %fusion.3), channel_id=1, source_target_pairs={{0,16},{8,24},{16,32},{24,40},{32,48},{40,56},{48,64},{56,72},{64,... | collective-permute-start | bytes 196616 | tf_op jit(solution)/shard_map/ppermute | solution.py:11
  14.0 26.7 %collective-permute-start.1 = (bf16[128,256]{1,0:T(8,128)(2,1)S(1)}, bf16[128,256]{1,0:T(8,128)(2,1)S(1)}, u32[]{:S(2)}, u32[]{:S(2)}) collective-permute-start(bf16[128,256]{1,0:T(8,128)(2,1)S(1)} %fusion.3), channel_id=1, source_target_pairs={{0,8},{8,16},{16,24},{24,32},{32,40},{40,48},{48,56},{56,64},{64,7... | collective-permute-start | bytes 196616 | tf_op jit(solution)/shard_map/ppermute | solution.py:11
  17.2 23.5 %collective-permute-start.2 = (bf16[128,256]{1,0:T(8,128)(2,1)S(1)}, bf16[128,256]{1,0:T(8,128)(2,1)S(1)}, u32[]{:S(2)}, u32[]{:S(2)}) collective-permute-start(bf16[128,256]{1,0:T(8,128)(2,1)S(1)} %fusion.3), channel_id=1, source_target_pairs={{0,504},{8,0},{16,8},{24,16},{32,24},{40,32},{48,40},{56,48},{64,5... | collective-permute-start | bytes 196616 | tf_op jit(solution)/shard_map/ppermute | solution.py:11
  27.7 13.0 %collective-permute-start.3 = (bf16[128,256]{1,0:T(8,128)(2,1)S(1)}, bf16[128,256]{1,0:T(8,128)(2,1)S(1)}, u32[]{:S(2)}, u32[]{:S(2)}) collective-permute-start(bf16[128,256]{1,0:T(8,128)(2,1)S(1)} %fusion.3), channel_id=1, source_target_pairs={{0,496},{8,504},{16,0},{24,8},{32,16},{40,24},{48,32},{56,40},{64,... | collective-permute-start | bytes 196616 | tf_op jit(solution)/shard_map/ppermute | solution.py:11
  40.8 1.7 %copy-start.1 = (bf16[128,256]{1,0:T(8,128)(2,1)S(1)}, bf16[128,256]{1,0:T(8,128)(2,1)}, u32[]{:S(2)}) copy-start(bf16[128,256]{1,0:T(8,128)(2,1)} %param.9) | copy-start | bytes 196612
  40.8 1.7 %copy-start.2 = (bf16[128,256]{1,0:T(8,128)(2,1)S(1)}, bf16[128,256]{1,0:T(8,128)(2,1)}, u32[]{:S(2)}) copy-start(bf16[128,256]{1,0:T(8,128)(2,1)} %param.10) | copy-start | bytes 196612
  40.8 1.7 %copy-start.3 = (bf16[128,256]{1,0:T(8,128)(2,1)S(1)}, bf16[128,256]{1,0:T(8,128)(2,1)}, u32[]{:S(2)}) copy-start(bf16[128,256]{1,0:T(8,128)(2,1)} %param.11) | copy-start | bytes 196612
Sparse Core Ops, SparseCore 0:
  42.5 41.3 reduce-scatter.1

commit v9 on v8

--- a/solution.py
+++ b/solution.py
@@ -26,9 +26,6 @@
     replicas = lax.axis_size("rep")
     own_block = lax.axis_index("blk")
     offsets = list(range(-REACH, REACH + 1))
-    rows = jnp.stack(
-        [scaled if d == 0 else fetched_from(scaled, "blk", d) for d in offsets]
-    )
     sources = (own_block + jnp.array(offsets, jnp.int32)) % blocks
     listed = jnp.take(neighbors[0, 0], sources, axis=0)
     column_ids = jnp.take(tile_col[0, 0], sources, axis=0)
@@ -49,6 +46,10 @@
     merged = jnp.sum(
         chooser[:, :, None, :, None] * counts[:, :, :, None, :], axis=1
     )
+    early = {d: fetched_from(scaled, "blk", d) for d in offsets if d < 0}
+    later_source, merged = lax.optimization_barrier((scaled, merged))
+    late = {d: fetched_from(later_source, "blk", d) for d in offsets if d > 0}
+    rows = jnp.stack([scaled if d == 0 else {**early, **late}[d] for d in offsets])
     totals = jnp.einsum(
         "tinc,tif->ncf", merged, rows, preferred_element_type=jnp.float32
     )

time: 114 us -> 118 us (1.035)
  blocking collectives: 58.7 us -> 61.1 us
  waiting for transfers between devices: 0.03 us -> 1.58 us
    all_to_all x1, blocking collectives: 32.2 us -> 34.6 us  [on_device(): lax.all_to_all(local_weight.reshape(devices, -1), ('blk', 'rep'), 0, 0, t...]
    ppermute x4, waiting for transfers between devices: 0.01 us -> 1.56 us  [fetched_from(): lax.ppermute(x, axis, [(i, (i - offset) % size) for i in range(size)])]
  transfers between devices with their start and end apart: 5 -> 5, of which waited for: 0 -> 1; matrix products, arithmetic and copies ran while one was open for 12% -> 11% of each run, Pallas kernels for 0% -> 0%
where the time goes in v9:
time: 118 us
  blocking collectives  61.1 us (52%)
  starting transfers between devices  21.9 us (19%)
  between operations  14.9 us (13%)
  other arithmetic  11.1 us (9%)
  local copies, waits for them, and re-layouts  4.31 us (4%)
  matrix products  2.98 us (3%)
  waiting for transfers between devices  1.58 us (1%)
    all_to_all x1, blocking collectives, on_device(): lax.all_to_all(local_weight.reshape(devices, -1), ('blk', 'rep'), 0, 0, t...  34.6 us
    all_to_all x1, blocking collectives, on_device(): lax.all_to_all(jnp.broadcast_to(piece, (devices,) + piece.shape), ('blk',...  26.5 us
    ppermute x4, starting transfers between devices, fetched_from(): lax.ppermute(x, axis, [(i, (i - offset) % size) for i in range(size)])  21.9 us
    reduce_sum x1, other arithmetic, on_device(): jnp.sum((listed[:, :, :, :, None] == positions[None, None, None, None, :]...  4.21 us
  transfers between devices with their start and end apart: 5, of which 1 were waited for; matrix products, arithmetic and copies ran while one was open for 11% of the time, Pallas kernels for 0%

profile of v9, /device:TPU:1, one launch (start us, length us, event | category | flops | bytes accessed | tf_op | source)
XLA Modules:
  0.0 117.9 jit_solution(8200772377116381780)
XLA Ops:
  7.2 0.7 convert_rsqrt_fusion
  8.0 1.2 fusion.3
  9.1 4.8 %collective-permute-start = (bf16[128,256]{1,0:T(8,128)(2,1)S(1)}, bf16[128,256]{1,0:T(8,128)(2,1)S(1)}, u32[]{:S(2)}, u32[]{:S(2)}) collective-permute-start(bf16[128,256]{1,0:T(8,128)(2,1)S(1)} %fusion.3), channel_id=1, source_target_pairs={{0,16},{8,24},{16,32},{24,40},{32,48},{40,56},{48,64},{56,72},{64,... | collective-permute-start | bytes 196616 | tf_op jit(solution)/shard_map/ppermute | solution.py:11
  14.0 3.2 %collective-permute-start.1 = (bf16[128,256]{1,0:T(8,128)(2,1)S(1)}, bf16[128,256]{1,0:T(8,128)(2,1)S(1)}, u32[]{:S(2)}, u32[]{:S(2)}) collective-permute-start(bf16[128,256]{1,0:T(8,128)(2,1)S(1)} %fusion.3), channel_id=1, source_target_pairs={{0,8},{8,16},{16,24},{24,32},{32,40},{40,48},{48,56},{56,64},{64,7... | collective-permute-start | bytes 196616 | tf_op jit(solution)/shard_map/ppermute | solution.py:11
  17.2 0.7 compare_and_fusion
  17.9 0.8 copy.17
  18.7 0.6 gather_fusion
  19.2 1.3 %gather_fusion.1 = s32[5]{0:T(128)S(1)} fusion(s32[64]{0:T(128)} %bitcast.29, s32[1024]{0:T(1024)S(1)} %pad_clamp_fusion), kind=kCustom, calls=%fused_computation.1 | custom fusion | bytes 60 | tf_op jit(solution)/shard_map/jit(_take)/gather | solution.py:32
  20.6 0.6 gather_fusion.2
  21.3 4.2 %fusion.1 = bf16[5,4,128,128]{3,2,1,0:T(8,128)(2,1)S(1)} fusion(s32[5,4,8,128]{3,2,1,0:T(8,128)S(1)} %broadcast_select_fusion), kind=kLoop, calls=%fused_computation.5 | loop fusion | flops 7536640 | bytes 737280 | tf_op jit(solution)/shard_map/reduce_sum | solution.py:38
  25.6 1.1 multiply_reduce_fusion
  26.8 10.5 %collective-permute-start.2 = (bf16[128,256]{1,0:T(8,128)(2,1)S(1)}, bf16[128,256]{1,0:T(8,128)(2,1)S(1)}, u32[]{:S(2)}, u32[]{:S(2)}) collective-permute-start(bf16[128,256]{1,0:T(8,128)(2,1)S(1)} %fusion.3), channel_id=1, source_target_pairs={{0,504},{8,0},{16,8},{24,16},{32,24},{40,32},{48,40},{56,48},{64,5... | collective-permute-start | bytes 196616 | tf_op jit(solution)/shard_map/ppermute | solution.py:11
  37.3 3.4 %collective-permute-start.3 = (bf16[128,256]{1,0:T(8,128)(2,1)S(1)}, bf16[128,256]{1,0:T(8,128)(2,1)S(1)}, u32[]{:S(2)}, u32[]{:S(2)}) collective-permute-start(bf16[128,256]{1,0:T(8,128)(2,1)S(1)} %fusion.3), channel_id=1, source_target_pairs={{0,496},{8,504},{16,0},{24,8},{32,16},{40,24},{48,32},{56,40},{64,... | collective-permute-start | bytes 196616 | tf_op jit(solution)/shard_map/ppermute | solution.py:11
  40.7 1.6 %collective-permute-done.3 = bf16[128,256]{1,0:T(8,128)(2,1)S(1)} collective-permute-done((bf16[128,256]{1,0:T(8,128)(2,1)S(1)}, bf16[128,256]{1,0:T(8,128)(2,1)S(1)}, u32[]{:S(2)}, u32[]{:S(2)}) %collective-permute-start.3) | collective-permute-done | bytes 65568 | tf_op jit(solution)/shard_map/ppermute | solution.py:11
  42.3 1.6 %convolution_bitcast_fusion = f32[8,128,256]{2,1,0:T(8,128)} fusion(bf16[5,128,8,128]{3,2,1,0:T(8,128)(2,1)S(1)} %multiply_reduce_fusion, bf16[5,128,256]{2,1,0:T(8,128)(2,1)S(1)} %bitcast_dynamic-update-slice_fusion), kind=kOutput, calls=%fused_computation.7 | convolution fusion | flops 335544320 | bytes 2686976 | tf_op jit(solution)/shard_map/tinc,tif->ncf/dot_general | solution.py:53
  44.0 0.2 convolution_bitcast_fusion.1
  44.4 34.6 %all_to_all.15 = f32[512,1,128]{2,1,0:T(1,128)S(1)} all-to-all(f32[512,1,128]{2,1,0:T(1,128)S(1)} %bitcast.30), channel_id=1, replica_groups=mesh['blk'=64,'rep'=8] {'blk','rep'}, dimensions={0} | all-to-all | bytes 524288 | tf_op jit(solution)/shard_map/all_to_all | solution.py:59
  79.0 0.6 reduce_sum.44
  79.5 0.1 broadcast_in_dim.38
  79.7 26.5 %all_to_all.16 = f32[512,1,128]{2,1,0:T(1,128)S(1)} all-to-all(f32[512,1,128]{2,1,0:T(1,128)S(1)} %broadcast_in_dim.38), channel_id=1, replica_groups=mesh['blk'=64,'rep'=8] {'blk','rep'}, dimensions={0} | all-to-all | bytes 524288 | tf_op jit(solution)/shard_map/all_to_all | solution.py:63
  106.2 1.1 multiply_reduce_fusion.2
  108.0 0.7 multiply_reduce_fusion.1
  108.7 0.8 mul.50
  109.5 1.6 %fusion.5 = bf16[128,256]{1,0:T(8,128)(2,1)} fusion(f32[1,128,256]{2,1,0:T(8,128)} %reduce-scatter.2.cloned.1.call-done, f32[128]{0:T(128)S(1)} %convert_rsqrt_fusion), kind=kLoop, calls=%fused_computation.16 | loop fusion | flops 65536 | bytes 197120 | tf_op jit(solution)/shard_map/convert_element_type | solution.py:68
  (27 shorter events, 0.6 us)
Async XLA Ops:
  7.2 13.4 %copy-start = (s32[1,1,64,4,8,128]{5,4,3,2,1,0:T(8,128)S(1)}, s32[1,1,64,4,8,128]{5,4,3,2,1,0:T(8,128)}, u32[]{:S(2)}) copy-start(s32[1,1,64,4,8,128]{5,4,3,2,1,0:T(8,128)} %param.14) | copy-start | bytes 3145732
  7.2 102.3 %reduce-scatter.2.cloned.1.call-start = ((), (), s32[]{:S(2)}) async-start(), calls=%async_computation.3 | async-start | bytes 1179648 | tf_op jit(solution)/shard_map/reduce_scatter | solution.py:56
  9.1 31.5 %collective-permute-start = (bf16[128,256]{1,0:T(8,128)(2,1)S(1)}, bf16[128,256]{1,0:T(8,128)(2,1)S(1)}, u32[]{:S(2)}, u32[]{:S(2)}) collective-permute-start(bf16[128,256]{1,0:T(8,128)(2,1)S(1)} %fusion.3), channel_id=1, source_target_pairs={{0,16},{8,24},{16,32},{24,40},{32,48},{40,56},{48,64},{56,72},{64,... | collective-permute-start | bytes 196616 | tf_op jit(solution)/shard_map/ppermute | solution.py:11
  14.0 26.7 %collective-permute-start.1 = (bf16[128,256]{1,0:T(8,128)(2,1)S(1)}, bf16[128,256]{1,0:T(8,128)(2,1)S(1)}, u32[]{:S(2)}, u32[]{:S(2)}) collective-permute-start(bf16[128,256]{1,0:T(8,128)(2,1)S(1)} %fusion.3), channel_id=1, source_target_pairs={{0,8},{8,16},{16,24},{24,32},{32,40},{40,48},{48,56},{56,64},{64,7... | collective-permute-start | bytes 196616 | tf_op jit(solution)/shard_map/ppermute | solution.py:11
  26.8 14.0 %collective-permute-start.2 = (bf16[128,256]{1,0:T(8,128)(2,1)S(1)}, bf16[128,256]{1,0:T(8,128)(2,1)S(1)}, u32[]{:S(2)}, u32[]{:S(2)}) collective-permute-start(bf16[128,256]{1,0:T(8,128)(2,1)S(1)} %fusion.3), channel_id=1, source_target_pairs={{0,504},{8,0},{16,8},{24,16},{32,24},{40,32},{48,40},{56,48},{64,5... | collective-permute-start | bytes 196616 | tf_op jit(solution)/shard_map/ppermute | solution.py:11
  37.3 5.0 %collective-permute-start.3 = (bf16[128,256]{1,0:T(8,128)(2,1)S(1)}, bf16[128,256]{1,0:T(8,128)(2,1)S(1)}, u32[]{:S(2)}, u32[]{:S(2)}) collective-permute-start(bf16[128,256]{1,0:T(8,128)(2,1)S(1)} %fusion.3), channel_id=1, source_target_pairs={{0,496},{8,504},{16,0},{24,8},{32,16},{40,24},{48,32},{56,40},{64,... | collective-permute-start | bytes 196616 | tf_op jit(solution)/shard_map/ppermute | solution.py:11
  42.3 1.7 %copy-start.1 = (bf16[128,256]{1,0:T(8,128)(2,1)S(1)}, bf16[128,256]{1,0:T(8,128)(2,1)}, u32[]{:S(2)}) copy-start(bf16[128,256]{1,0:T(8,128)(2,1)} %param.9) | copy-start | bytes 196612
  42.3 1.7 %copy-start.2 = (bf16[128,256]{1,0:T(8,128)(2,1)S(1)}, bf16[128,256]{1,0:T(8,128)(2,1)}, u32[]{:S(2)}) copy-start(bf16[128,256]{1,0:T(8,128)(2,1)} %param.10) | copy-start | bytes 196612
  42.3 1.7 %copy-start.3 = (bf16[128,256]{1,0:T(8,128)(2,1)S(1)}, bf16[128,256]{1,0:T(8,128)(2,1)}, u32[]{:S(2)}) copy-start(bf16[128,256]{1,0:T(8,128)(2,1)} %param.11) | copy-start | bytes 196612
Sparse Core Ops, SparseCore 0:
  44.1 43.7 reduce-scatter.1

commit v10 on v7

--- a/solution.py
+++ b/solution.py
@@ -50,7 +50,17 @@
     totals = jnp.einsum(
         "tinc,tif->ncf", merged, rows, preferred_element_type=jnp.float32
     )
-    owned = lax.psum_scatter(totals, "rep", scatter_dimension=0, tiled=True)
+    rep_index = lax.axis_index("rep")
+
+    def halved(parts, lower, upper, bit, mask):
+        mine = (rep_index >> bit) & 1
+        kept = jnp.where(mine == 0, lower, upper)
+        given = jnp.where(mine == 0, upper, lower)
+        return kept + lax.ppermute(given, "rep", [(i, i ^ mask) for i in range(replicas)])
+
+    by_core = halved(totals, totals[0::2], totals[1::2], 0, 1)
+    by_far = halved(by_core, by_core[:2], by_core[2:], 2, 6)
+    owned = halved(by_far, by_far[0:1], by_far[1:2], 1, 2)
     local_weight, totals = lax.optimization_barrier((local_weight, totals))
     devices = lax.axis_size("blk") * lax.axis_size("rep")
     pieces = lax.all_to_all(

time: 115 us -> 103 us (0.90)
  blocking collectives: 58.7 us -> 0 us
  starting transfers between devices: 21.9 us -> 56.8 us
  waiting for transfers between devices: 0.03 us -> 22.9 us
  between operations: 15 us -> 1.69 us
  local copies, waits for them, and re-layouts: 2.98 us -> 4.38 us
  other arithmetic: 9.79 us -> 11 us
    all_to_all x2 -> x0, blocking collectives: 58.7 us -> none  [the longest x1 32.2 us: on_device(): lax.all_to_all(local_weight.reshape(devices, -1), ('blk', 'rep'), 0, 0, t...]
    all_to_all x0 -> x2, starting transfers between devices: none -> 21.5 us  [the longest x1 12.6 us: on_device(): lax.all_to_all(local_weight.reshape(devices, -1), ('blk', 'rep'), 0, 0, t...]
    all_to_all x0 -> x2, waiting for transfers between devices: none -> 16.6 us  [the longest x1 11 us: on_device(): lax.all_to_all(local_weight.reshape(devices, -1), ('blk', 'rep'), 0, 0, t...]
    ppermute x0 -> x3, starting transfers between devices: none -> 13.4 us  [halved(): lax.ppermute(given, 'rep', [(i, i ^ mask) for i in range(replicas)])]
    ppermute x0 -> x3, waiting for transfers between devices: none -> 6.25 us  [halved(): lax.ppermute(given, 'rep', [(i, i ^ mask) for i in range(replicas)])]
    dot_general x1, matrix products: 2.82 us -> 4.09 us  [on_device(): merged = jnp.einsum('tsn,tsic->tinc', chooser, counts).astype(jnp.bfloat16)]
  transfers between devices with their start and end apart: 5 -> 9, of which waited for: 0 -> 3; matrix products, arithmetic and copies ran while one was open for 12% -> 14% of each run, Pallas kernels for 0% -> 0%
where the time goes in v10:
time: 103 us
  starting transfers between devices  56.8 us (55%)
  waiting for transfers between devices  22.9 us (22%)
  other arithmetic  11 us (11%)
  matrix products  6.07 us (6%)
  local copies, waits for them, and re-layouts  4.38 us (4%)
  between operations  1.69 us (2%)
    ppermute x4, starting transfers between devices, fetched_from(): lax.ppermute(x, axis, [(i, (i - offset) % size) for i in range(size)])  21.9 us
    ppermute x3, starting transfers between devices, halved(): lax.ppermute(given, 'rep', [(i, i ^ mask) for i in range(replicas)])  13.4 us
    all_to_all x1, starting transfers between devices, on_device(): lax.all_to_all(local_weight.reshape(devices, -1), ('blk', 'rep'), 0, 0, t...  12.6 us
    all_to_all x1, waiting for transfers between devices, on_device(): lax.all_to_all(local_weight.reshape(devices, -1), ('blk', 'rep'), 0, 0, t...  11 us
    all_to_all x1, starting transfers between devices, on_device(): lax.all_to_all(jnp.broadcast_to(piece, (devices,) + piece.shape), ('blk',...  8.89 us
    ppermute x3, waiting for transfers between devices, halved(): lax.ppermute(given, 'rep', [(i, i ^ mask) for i in range(replicas)])  6.25 us
    all_to_all x1, waiting for transfers between devices, on_device(): lax.all_to_all(jnp.broadcast_to(piece, (devices,) + piece.shape), ('blk',...  5.59 us
    reduce_sum x1, other arithmetic, on_device(): jnp.sum((listed[:, :, :, :, None] == positions[None, None, None, None, :]...  5.23 us
  transfers between devices with their start and end apart: 9, of which 3 were waited for; matrix products, arithmetic and copies ran while one was open for 14% of the time, Pallas kernels for 0%

profile of v10, /device:TPU:1, one launch (start us, length us, event | category | flops | bytes accessed | tf_op | source)
XLA Modules:
  0.0 102.9 jit_solution(9952033536340681641)
XLA Ops:
  0.7 0.7 convert_rsqrt_fusion
  1.4 1.2 %fusion.2 = bf16[128,256]{1,0:T(8,128)(2,1)S(1)} fusion(bf16[256,256]{1,0:T(8,128)(2,1)} %param.12, f32[128]{0:T(128)S(1)} %convert_rsqrt_fusion, bf16[128,256]{1,0:T(8,128)(2,1)} %param.9, bf16[128,256]{1,0:T(8,128)(2,1)} %param.10), kind=kOutput, calls=%fused_computation.11 | convolution fusion | flops 16908288 | bytes 328192 | tf_op jit(solution)/shard_map/dot_general | solution.py:20
  2.6 4.8 %collective-permute-start = (bf16[128,256]{1,0:T(8,128)(2,1)S(1)}, bf16[128,256]{1,0:T(8,128)(2,1)S(1)}, u32[]{:S(2)}, u32[]{:S(2)}) collective-permute-start(bf16[128,256]{1,0:T(8,128)(2,1)S(1)} %fusion.2), channel_id=1, source_target_pairs={{0,16},{8,24},{16,32},{24,40},{32,48},{40,56},{48,64},{56,72},{64,... | collective-permute-start | bytes 196616 | tf_op jit(solution)/shard_map/ppermute | solution.py:11
  7.4 3.2 %collective-permute-start.1 = (bf16[128,256]{1,0:T(8,128)(2,1)S(1)}, bf16[128,256]{1,0:T(8,128)(2,1)S(1)}, u32[]{:S(2)}, u32[]{:S(2)}) collective-permute-start(bf16[128,256]{1,0:T(8,128)(2,1)S(1)} %fusion.2), channel_id=1, source_target_pairs={{0,8},{8,16},{16,24},{24,32},{32,40},{40,48},{48,56},{56,64},{64,7... | collective-permute-start | bytes 196616 | tf_op jit(solution)/shard_map/ppermute | solution.py:11
  10.6 10.5 %collective-permute-start.2 = (bf16[128,256]{1,0:T(8,128)(2,1)S(1)}, bf16[128,256]{1,0:T(8,128)(2,1)S(1)}, u32[]{:S(2)}, u32[]{:S(2)}) collective-permute-start(bf16[128,256]{1,0:T(8,128)(2,1)S(1)} %fusion.2), channel_id=1, source_target_pairs={{0,504},{8,0},{16,8},{24,16},{32,24},{40,32},{48,40},{56,48},{64,5... | collective-permute-start | bytes 196616 | tf_op jit(solution)/shard_map/ppermute | solution.py:11
  21.2 3.4 %collective-permute-start.3 = (bf16[128,256]{1,0:T(8,128)(2,1)S(1)}, bf16[128,256]{1,0:T(8,128)(2,1)S(1)}, u32[]{:S(2)}, u32[]{:S(2)}) collective-permute-start(bf16[128,256]{1,0:T(8,128)(2,1)S(1)} %fusion.2), channel_id=1, source_target_pairs={{0,496},{8,504},{16,0},{24,8},{32,16},{40,24},{48,32},{56,40},{64,... | collective-permute-start | bytes 196616 | tf_op jit(solution)/shard_map/ppermute | solution.py:11
  24.5 0.7 compare_and_fusion
  25.9 5.2 %convert_reduce_fusion = s32[5,4,128,128]{3,2,1,0:T(8,128)} fusion(s32[5,4,8,128]{3,2,1,0:T(8,128)S(1)} %broadcast_select_fusion), kind=kLoop, calls=%fused_computation.3 | loop fusion | flops 7536640 | bytes 1392640 | tf_op jit(solution)/shard_map/reduce_sum | solution.py:41
  32.6 4.1 %convolution_bitcast_fusion = bf16[5,128,8,128]{3,2,1,0:T(8,128)(2,1)S(1)} fusion(s32[5,4,128,128]{3,2,1,0:T(8,128)} %convert_reduce_fusion, s32[5,4]{1,0:T(8,128)S(1)} %broadcast_select_fusion.1, pred[5,4]{1,0:T(8,128)(4,1)S(1)} %iota_compare_fusion.2), kind=kOutput, calls=%fused_computation.5 | convolution fusion | flops 5243200 | bytes 2621540 | tf_op jit(solution)/shard_map/tsn,tsic->tinc/dot_general | solution.py:49
  37.4 0.9 slice_select_fusion
  38.3 3.4 %collective-permute-start.4 = (f32[4,128,256]{2,1,0:T(8,128)}, f32[4,128,256]{2,1,0:T(8,128)S(1)}, u32[]{:S(2)}, u32[]{:S(2)}) collective-permute-start(f32[4,128,256]{2,1,0:T(8,128)} %slice_select_fusion), channel_id=1, source_target_pairs={{0,1},{1,0},{2,3},{3,2},{4,5},{5,4},{6,7},{7,6},{8,9},{9,8},{10,11... | collective-permute-start | bytes 1572872 | tf_op jit(solution)/shard_map/ppermute | solution.py:59
  42.1 0.7 all_to_all.10
  42.8 12.6 %all-to-all-start = ((f32[512,1,128]{2,1,0:T(1,128)}), f32[512,1,128]{2,1,0:T(1,128)S(1)}, u32[]{:S(2)}, u32[]{:S(2)}) async-start(f32[512,1,128]{2,1,0:T(1,128)} %bitcast.16), calls=%async_computation | async-start | bytes 524288 | tf_op jit(solution)/shard_map/all_to_all | solution.py:66
  55.6 5.7 %collective-permute-start.5 = (f32[2,128,256]{2,1,0:T(8,128)S(1)}, f32[2,128,256]{2,1,0:T(8,128)S(1)}, u32[]{:S(2)}, u32[]{:S(2)}) collective-permute-start(f32[2,128,256]{2,1,0:T(8,128)S(1)} %slice_select_fusion.1), channel_id=1, source_target_pairs={{0,6},{1,7},{2,4},{3,5},{4,2},{5,3},{6,0},{7,1},{8,14},{9,15},{10,... | collective-permute-start | bytes 786440 | tf_op jit(solution)/shard_map/ppermute | solution.py:59
  61.3 11.0 %all-to-all-done = f32[512,1,128]{2,1,0:T(1,128)S(1)} async-done(((f32[512,1,128]{2,1,0:T(1,128)}), f32[512,1,128]{2,1,0:T(1,128)S(1)}, u32[]{:S(2)}, u32[]{:S(2)}) %all-to-all-start) | async-done | bytes 262176 | tf_op jit(solution)/shard_map/all_to_all | solution.py:66
  72.8 0.8 broadcast_in_dim.36
  73.7 8.9 %all-to-all-start.1 = ((f32[512,1,128]{2,1,0:T(1,128)}), f32[512,1,128]{2,1,0:T(1,128)S(1)}, u32[]{:S(2)}, u32[]{:S(2)}) async-start(f32[512,1,128]{2,1,0:T(1,128)} %broadcast_in_dim.36), calls=%async_computation.1 | async-start | bytes 524288 | tf_op jit(solution)/shard_map/all_to_all | solution.py:70
  82.7 4.3 %collective-permute-start.6 = (f32[1,128,256]{2,1,0:T(8,128)S(1)}, f32[1,128,256]{2,1,0:T(8,128)S(1)}, u32[]{:S(2)}, u32[]{:S(2)}) collective-permute-start(f32[1,128,256]{2,1,0:T(8,128)S(1)} %slice_select_fusion.2), channel_id=1, source_target_pairs={{0,2},{1,3},{2,0},{3,1},{4,6},{5,7},{6,4},{7,5},{8,10},{9,11},{10,... | collective-permute-start | bytes 393224 | tf_op jit(solution)/shard_map/ppermute | solution.py:59
  87.0 6.2 %collective-permute-done.6 = f32[1,128,256]{2,1,0:T(8,128)S(1)} collective-permute-done((f32[1,128,256]{2,1,0:T(8,128)S(1)}, f32[1,128,256]{2,1,0:T(8,128)S(1)}, u32[]{:S(2)}, u32[]{:S(2)}) %collective-permute-start.6) | collective-permute-done | bytes 131104 | tf_op jit(solution)/shard_map/ppermute | solution.py:59
  93.2 0.7 fusion.4
  94.0 5.6 %all-to-all-done.1 = f32[512,1,128]{2,1,0:T(1,128)S(1)} async-done(((f32[512,1,128]{2,1,0:T(1,128)}), f32[512,1,128]{2,1,0:T(1,128)S(1)}, u32[]{:S(2)}, u32[]{:S(2)}) %all-to-all-start.1) | async-done | bytes 262176 | tf_op jit(solution)/shard_map/all_to_all | solution.py:70
  99.6 1.1 %multiply_reduce_fusion.1 = f32[]{:T(128)} fusion(f32[512,1,128]{2,1,0:T(1,128)S(1)} %all-to-all-done.1), kind=kLoop, calls=%fused_computation.16 | loop fusion | flops 131071 | bytes 262148 | tf_op jit(solution)/shard_map/reduce_sum | solution.py:73
  101.4 0.7 multiply_reduce_fusion
  102.1 0.8 mul.34
  (40 shorter events, 3.9 us)
Async XLA Ops:
  0.6 24.6 %copy-start = (s32[1,1,64,4,8,128]{5,4,3,2,1,0:T(8,128)S(1)}, s32[1,1,64,4,8,128]{5,4,3,2,1,0:T(8,128)}, u32[]{:S(2)}) copy-start(s32[1,1,64,4,8,128]{5,4,3,2,1,0:T(8,128)} %param.14) | copy-start | bytes 3145732
  0.6 30.5 %copy-start.5 = (s32[1,1,64,4]{2,3,1,0:T(4,128)S(1)}, s32[1,1,64,4]{2,3,1,0:T(4,128)}, u32[]{:S(2)}) copy-start(s32[1,1,64,4]{2,3,1,0:T(4,128)} %param.15) | copy-start | bytes 3076
  0.7 31.2 %copy-start.1 = (s32[1,1,64]{2,1,0:T(1,128)S(1)}, s32[1,1,64]{2,1,0:T(1,128)}, u32[]{:S(2)}) copy-start(s32[1,1,64]{2,1,0:T(1,128)} %param.16) | copy-start | bytes 772
  2.6 34.1 %collective-permute-start = (bf16[128,256]{1,0:T(8,128)(2,1)S(1)}, bf16[128,256]{1,0:T(8,128)(2,1)S(1)}, u32[]{:S(2)}, u32[]{:S(2)}) collective-permute-start(bf16[128,256]{1,0:T(8,128)(2,1)S(1)} %fusion.2), channel_id=1, source_target_pairs={{0,16},{8,24},{16,32},{24,40},{32,48},{40,56},{48,64},{56,72},{64,... | collective-permute-start | bytes 196616 | tf_op jit(solution)/shard_map/ppermute | solution.py:11
  7.4 29.3 %collective-permute-start.1 = (bf16[128,256]{1,0:T(8,128)(2,1)S(1)}, bf16[128,256]{1,0:T(8,128)(2,1)S(1)}, u32[]{:S(2)}, u32[]{:S(2)}) collective-permute-start(bf16[128,256]{1,0:T(8,128)(2,1)S(1)} %fusion.2), channel_id=1, source_target_pairs={{0,8},{8,16},{16,24},{24,32},{32,40},{40,48},{48,56},{56,64},{64,7... | collective-permute-start | bytes 196616 | tf_op jit(solution)/shard_map/ppermute | solution.py:11
  10.6 26.1 %collective-permute-start.2 = (bf16[128,256]{1,0:T(8,128)(2,1)S(1)}, bf16[128,256]{1,0:T(8,128)(2,1)S(1)}, u32[]{:S(2)}, u32[]{:S(2)}) collective-permute-start(bf16[128,256]{1,0:T(8,128)(2,1)S(1)} %fusion.2), channel_id=1, source_target_pairs={{0,504},{8,0},{16,8},{24,16},{32,24},{40,32},{48,40},{56,48},{64,5... | collective-permute-start | bytes 196616 | tf_op jit(solution)/shard_map/ppermute | solution.py:11
  21.2 15.6 %collective-permute-start.3 = (bf16[128,256]{1,0:T(8,128)(2,1)S(1)}, bf16[128,256]{1,0:T(8,128)(2,1)S(1)}, u32[]{:S(2)}, u32[]{:S(2)}) collective-permute-start(bf16[128,256]{1,0:T(8,128)(2,1)S(1)} %fusion.2), channel_id=1, source_target_pairs={{0,496},{8,504},{16,0},{24,8},{32,16},{40,24},{48,32},{56,40},{64,... | collective-permute-start | bytes 196616 | tf_op jit(solution)/shard_map/ppermute | solution.py:11
  37.4 4.3 %copy-start.2 = (bf16[128,256]{1,0:T(8,128)(2,1)S(1)}, bf16[128,256]{1,0:T(8,128)(2,1)}, u32[]{:S(2)}) copy-start(bf16[128,256]{1,0:T(8,128)(2,1)} %param.9) | copy-start | bytes 196612
  37.4 4.3 %copy-start.3 = (bf16[128,256]{1,0:T(8,128)(2,1)S(1)}, bf16[128,256]{1,0:T(8,128)(2,1)}, u32[]{:S(2)}) copy-start(bf16[128,256]{1,0:T(8,128)(2,1)} %param.10) | copy-start | bytes 196612
  37.4 4.3 %copy-start.4 = (bf16[128,256]{1,0:T(8,128)(2,1)S(1)}, bf16[128,256]{1,0:T(8,128)(2,1)}, u32[]{:S(2)}) copy-start(bf16[128,256]{1,0:T(8,128)(2,1)} %param.11) | copy-start | bytes 196612
  38.3 17.2 %collective-permute-start.4 = (f32[4,128,256]{2,1,0:T(8,128)}, f32[4,128,256]{2,1,0:T(8,128)S(1)}, u32[]{:S(2)}, u32[]{:S(2)}) collective-permute-start(f32[4,128,256]{2,1,0:T(8,128)} %slice_select_fusion), channel_id=1, source_target_pairs={{0,1},{1,0},{2,3},{3,2},{4,5},{5,4},{6,7},{7,6},{8,9},{9,8},{10,11... | collective-permute-start | bytes 1572872 | tf_op jit(solution)/shard_map/ppermute | solution.py:59
  42.8 29.5 %all-to-all-start = ((f32[512,1,128]{2,1,0:T(1,128)}), f32[512,1,128]{2,1,0:T(1,128)S(1)}, u32[]{:S(2)}, u32[]{:S(2)}) async-start(f32[512,1,128]{2,1,0:T(1,128)} %bitcast.16), calls=%async_computation | async-start | bytes 524288 | tf_op jit(solution)/shard_map/all_to_all | solution.py:66
  55.6 27.0 %collective-permute-start.5 = (f32[2,128,256]{2,1,0:T(8,128)S(1)}, f32[2,128,256]{2,1,0:T(8,128)S(1)}, u32[]{:S(2)}, u32[]{:S(2)}) collective-permute-start(f32[2,128,256]{2,1,0:T(8,128)S(1)} %slice_select_fusion.1), channel_id=1, source_target_pairs={{0,6},{1,7},{2,4},{3,5},{4,2},{5,3},{6,0},{7,1},{8,14},{9,15},{10,... | collective-permute-start | bytes 786440 | tf_op jit(solution)/shard_map/ppermute | solution.py:59
  73.7 25.9 %all-to-all-start.1 = ((f32[512,1,128]{2,1,0:T(1,128)}), f32[512,1,128]{2,1,0:T(1,128)S(1)}, u32[]{:S(2)}, u32[]{:S(2)}) async-start(f32[512,1,128]{2,1,0:T(1,128)} %broadcast_in_dim.36), calls=%async_computation.1 | async-start | bytes 524288 | tf_op jit(solution)/shard_map/all_to_all | solution.py:70
  82.7 10.6 %collective-permute-start.6 = (f32[1,128,256]{2,1,0:T(8,128)S(1)}, f32[1,128,256]{2,1,0:T(8,128)S(1)}, u32[]{:S(2)}, u32[]{:S(2)}) collective-permute-start(f32[1,128,256]{2,1,0:T(8,128)S(1)} %slice_select_fusion.2), channel_id=1, source_target_pairs={{0,2},{1,3},{2,0},{3,1},{4,6},{5,7},{6,4},{7,5},{8,10},{9,11},{10,... | collective-permute-start | bytes 393224 | tf_op jit(solution)/shard_map/ppermute | solution.py:59

commit v11 on v10

--- a/solution.py
+++ b/solution.py
@@ -39,14 +39,16 @@
     positions = jnp.arange(tile_side, dtype=jnp.int32)
     slot_index = jnp.arange(slots_total, dtype=jnp.int32)
     counts = jnp.sum(
-        (listed[:, :, :, :, None] == positions[None, None, None, None, :]).astype(jnp.int32),
+        (listed[:, :, :, :, None] == positions[None, None, None, None, :]).astype(jnp.bfloat16),
         axis=2,
     )
     chooser = jnp.logical_and(
         column_ids[:, :, None] == jnp.arange(replicas, dtype=jnp.int32)[None, None, :],
         (slot_index[None, :] < present[:, None])[:, :, None],
-    ).astype(jnp.int32)
-    merged = jnp.einsum("tsn,tsic->tinc", chooser, counts).astype(jnp.bfloat16)
+    ).astype(jnp.bfloat16)
+    merged = jnp.sum(
+        chooser[:, :, None, :, None] * counts[:, :, :, None, :], axis=1
+    )
     totals = jnp.einsum(
         "tinc,tif->ncf", merged, rows, preferred_element_type=jnp.float32
     )

time: 103 us -> 101 us (0.981)
  matrix products: 6.07 us -> 1.98 us
  local copies, waits for them, and re-layouts: 4.38 us -> 5.71 us
    dot_general x1 -> x0, matrix products: 4.09 us -> none  [on_device(): merged = jnp.einsum('tsn,tsic->tinc', chooser, counts).astype(jnp.bfloat16)]
    reduce_sum x0 -> x1, other arithmetic: none -> 1.13 us  [on_device(): jnp.sum(chooser[:, :, None, :, None] * counts[:, :, :, None, :], axis=1)]
  transfers between devices with their start and end apart: 9 -> 9, of which waited for: 3 -> 3; matrix products, arithmetic and copies ran while one was open for 14% -> 12% of each run, Pallas kernels for 0% -> 0%
where the time goes in v11:
time: 101 us; the launch traced here: 100 us
  starting transfers between devices  56.8 us (56%)
  waiting for transfers between devices  22.9 us (23%)
  other arithmetic  11.2 us (11%)
  local copies, waits for them, and re-layouts  5.71 us (6%)
  matrix products  1.98 us (2%)
  between operations  1.67 us (2%)
    ppermute x4, starting transfers between devices, fetched_from(): lax.ppermute(x, axis, [(i, (i - offset) % size) for i in range(size)])  21.9 us
    ppermute x3, starting transfers between devices, halved(): lax.ppermute(given, 'rep', [(i, i ^ mask) for i in range(replicas)])  13.4 us
    all_to_all x1, starting transfers between devices, on_device(): lax.all_to_all(local_weight.reshape(devices, -1), ('blk', 'rep'), 0, 0, t...  12.6 us
    all_to_all x1, waiting for transfers between devices, on_device(): lax.all_to_all(local_weight.reshape(devices, -1), ('blk', 'rep'), 0, 0, t...  11 us
    all_to_all x1, starting transfers between devices, on_device(): lax.all_to_all(jnp.broadcast_to(piece, (devices,) + piece.shape), ('blk',...  8.89 us
    ppermute x3, waiting for transfers between devices, halved(): lax.ppermute(given, 'rep', [(i, i ^ mask) for i in range(replicas)])  6.25 us
    all_to_all x1, waiting for transfers between devices, on_device(): lax.all_to_all(jnp.broadcast_to(piece, (devices,) + piece.shape), ('blk',...  5.59 us
    reduce_sum x1, other arithmetic, on_device(): jnp.sum((listed[:, :, :, :, None] == positions[None, None, None, None, :]...  4.21 us
  transfers between devices with their start and end apart: 9, of which 3 were waited for; matrix products, arithmetic and copies ran while one was open for 12% of the time, Pallas kernels for 0%

profile of v11, /device:TPU:1, one launch (start us, length us, event | category | flops | bytes accessed | tf_op | source)
XLA Modules:
  0.0 100.3 jit_solution(9820418263514301017)
XLA Ops:
  0.6 0.7 convert_rsqrt_fusion
  1.4 1.2 %fusion.3 = bf16[128,256]{1,0:T(8,128)(2,1)S(1)} fusion(bf16[256,256]{1,0:T(8,128)(2,1)} %param.12, f32[128]{0:T(128)S(1)} %convert_rsqrt_fusion, bf16[128,256]{1,0:T(8,128)(2,1)} %param.9, bf16[128,256]{1,0:T(8,128)(2,1)} %param.10), kind=kOutput, calls=%fused_computation.11 | convolution fusion | flops 16908288 | bytes 328192 | tf_op jit(solution)/shard_map/dot_general | solution.py:20
  2.6 4.8 %collective-permute-start = (bf16[128,256]{1,0:T(8,128)(2,1)S(1)}, bf16[128,256]{1,0:T(8,128)(2,1)S(1)}, u32[]{:S(2)}, u32[]{:S(2)}) collective-permute-start(bf16[128,256]{1,0:T(8,128)(2,1)S(1)} %fusion.3), channel_id=1, source_target_pairs={{0,16},{8,24},{16,32},{24,40},{32,48},{40,56},{48,64},{56,72},{64,... | collective-permute-start | bytes 196616 | tf_op jit(solution)/shard_map/ppermute | solution.py:11
  7.4 3.2 %collective-permute-start.1 = (bf16[128,256]{1,0:T(8,128)(2,1)S(1)}, bf16[128,256]{1,0:T(8,128)(2,1)S(1)}, u32[]{:S(2)}, u32[]{:S(2)}) collective-permute-start(bf16[128,256]{1,0:T(8,128)(2,1)S(1)} %fusion.3), channel_id=1, source_target_pairs={{0,8},{8,16},{16,24},{24,32},{32,40},{40,48},{48,56},{56,64},{64,7... | collective-permute-start | bytes 196616 | tf_op jit(solution)/shard_map/ppermute | solution.py:11
  10.6 10.5 %collective-permute-start.2 = (bf16[128,256]{1,0:T(8,128)(2,1)S(1)}, bf16[128,256]{1,0:T(8,128)(2,1)S(1)}, u32[]{:S(2)}, u32[]{:S(2)}) collective-permute-start(bf16[128,256]{1,0:T(8,128)(2,1)S(1)} %fusion.3), channel_id=1, source_target_pairs={{0,504},{8,0},{16,8},{24,16},{32,24},{40,32},{48,40},{56,48},{64,5... | collective-permute-start | bytes 196616 | tf_op jit(solution)/shard_map/ppermute | solution.py:11
  21.1 3.4 %collective-permute-start.3 = (bf16[128,256]{1,0:T(8,128)(2,1)S(1)}, bf16[128,256]{1,0:T(8,128)(2,1)S(1)}, u32[]{:S(2)}, u32[]{:S(2)}) collective-permute-start(bf16[128,256]{1,0:T(8,128)(2,1)S(1)} %fusion.3), channel_id=1, source_target_pairs={{0,496},{8,504},{16,0},{24,8},{32,16},{40,24},{48,32},{56,40},{64,... | collective-permute-start | bytes 196616 | tf_op jit(solution)/shard_map/ppermute | solution.py:11
  25.2 0.8 copy.17
  26.5 1.3 %gather_fusion.1 = s32[5]{0:T(128)S(1)} fusion(s32[64]{0:T(128)} %bitcast.29, s32[1024]{0:T(1024)S(1)} %pad_clamp_fusion), kind=kCustom, calls=%fused_computation.1 | custom fusion | bytes 60 | tf_op jit(solution)/shard_map/jit(_take)/gather | solution.py:35
  28.6 4.2 %fusion.1 = bf16[5,4,128,128]{3,2,1,0:T(8,128)(2,1)S(1)} fusion(s32[5,4,8,128]{3,2,1,0:T(8,128)S(1)} %broadcast_select_fusion), kind=kLoop, calls=%fused_computation.5 | loop fusion | flops 7536640 | bytes 737280 | tf_op jit(solution)/shard_map/reduce_sum | solution.py:41
  32.9 1.1 %multiply_reduce_fusion = bf16[5,128,8,128]{3,2,1,0:T(8,128)(2,1)S(1)} fusion(bf16[5,4,128,128]{3,2,1,0:T(8,128)(2,1)S(1)} %fusion.1, bf16[5,4,8]{2,1,0:T(4,128)(2,1)S(1)} %fusion.7), kind=kLoop, calls=%fused_computation.6 | loop fusion | flops 4587520 | bytes 1966400 | tf_op jit(solution)/shard_map/reduce_sum | solution.py:49
  34.8 0.8 slice_select_fusion
  35.7 3.4 %collective-permute-start.4 = (f32[4,128,256]{2,1,0:T(8,128)}, f32[4,128,256]{2,1,0:T(8,128)S(1)}, u32[]{:S(2)}, u32[]{:S(2)}) collective-permute-start(f32[4,128,256]{2,1,0:T(8,128)} %slice_select_fusion), channel_id=1, source_target_pairs={{0,1},{1,0},{2,3},{3,2},{4,5},{5,4},{6,7},{7,6},{8,9},{9,8},{10,11... | collective-permute-start | bytes 1572872 | tf_op jit(solution)/shard_map/ppermute | solution.py:61
  39.5 0.7 all_to_all.10
  40.2 12.6 %all-to-all-start = ((f32[512,1,128]{2,1,0:T(1,128)}), f32[512,1,128]{2,1,0:T(1,128)S(1)}, u32[]{:S(2)}, u32[]{:S(2)}) async-start(f32[512,1,128]{2,1,0:T(1,128)} %bitcast.13), calls=%async_computation | async-start | bytes 524288 | tf_op jit(solution)/shard_map/all_to_all | solution.py:68
  53.0 5.7 %collective-permute-start.5 = (f32[2,128,256]{2,1,0:T(8,128)S(1)}, f32[2,128,256]{2,1,0:T(8,128)S(1)}, u32[]{:S(2)}, u32[]{:S(2)}) collective-permute-start(f32[2,128,256]{2,1,0:T(8,128)S(1)} %slice_select_fusion.1), channel_id=1, source_target_pairs={{0,6},{1,7},{2,4},{3,5},{4,2},{5,3},{6,0},{7,1},{8,14},{9,15},{10,... | collective-permute-start | bytes 786440 | tf_op jit(solution)/shard_map/ppermute | solution.py:61
  58.7 11.0 %all-to-all-done = f32[512,1,128]{2,1,0:T(1,128)S(1)} async-done(((f32[512,1,128]{2,1,0:T(1,128)}), f32[512,1,128]{2,1,0:T(1,128)S(1)}, u32[]{:S(2)}, u32[]{:S(2)}) %all-to-all-start) | async-done | bytes 262176 | tf_op jit(solution)/shard_map/all_to_all | solution.py:68
  70.3 0.8 broadcast_in_dim.38
  71.1 8.9 %all-to-all-start.1 = ((f32[512,1,128]{2,1,0:T(1,128)}), f32[512,1,128]{2,1,0:T(1,128)S(1)}, u32[]{:S(2)}, u32[]{:S(2)}) async-start(f32[512,1,128]{2,1,0:T(1,128)} %broadcast_in_dim.38), calls=%async_computation.1 | async-start | bytes 524288 | tf_op jit(solution)/shard_map/all_to_all | solution.py:72
  80.1 4.3 %collective-permute-start.6 = (f32[1,128,256]{2,1,0:T(8,128)S(1)}, f32[1,128,256]{2,1,0:T(8,128)S(1)}, u32[]{:S(2)}, u32[]{:S(2)}) collective-permute-start(f32[1,128,256]{2,1,0:T(8,128)S(1)} %slice_select_fusion.2), channel_id=1, source_target_pairs={{0,2},{1,3},{2,0},{3,1},{4,6},{5,7},{6,4},{7,5},{8,10},{9,11},{10,... | collective-permute-start | bytes 393224 | tf_op jit(solution)/shard_map/ppermute | solution.py:61
  84.4 6.2 %collective-permute-done.6 = f32[1,128,256]{2,1,0:T(8,128)S(1)} collective-permute-done((f32[1,128,256]{2,1,0:T(8,128)S(1)}, f32[1,128,256]{2,1,0:T(8,128)S(1)}, u32[]{:S(2)}, u32[]{:S(2)}) %collective-permute-start.6) | collective-permute-done | bytes 131104 | tf_op jit(solution)/shard_map/ppermute | solution.py:61
  90.7 0.7 fusion.5
  91.4 5.6 %all-to-all-done.1 = f32[512,1,128]{2,1,0:T(1,128)S(1)} async-done(((f32[512,1,128]{2,1,0:T(1,128)}), f32[512,1,128]{2,1,0:T(1,128)S(1)}, u32[]{:S(2)}, u32[]{:S(2)}) %all-to-all-start.1) | async-done | bytes 262176 | tf_op jit(solution)/shard_map/all_to_all | solution.py:72
  97.0 1.1 %multiply_reduce_fusion.2 = f32[]{:T(128)} fusion(f32[512,1,128]{2,1,0:T(1,128)S(1)} %all-to-all-done.1), kind=kLoop, calls=%fused_computation.16 | loop fusion | flops 131071 | bytes 262148 | tf_op jit(solution)/shard_map/reduce_sum | solution.py:75
  99.5 0.8 mul.50
  (37 shorter events, 4.6 us)
Async XLA Ops:
  0.6 27.3 %copy-start = (s32[1,1,64,4,8,128]{5,4,3,2,1,0:T(8,128)S(1)}, s32[1,1,64,4,8,128]{5,4,3,2,1,0:T(8,128)}, u32[]{:S(2)}) copy-start(s32[1,1,64,4,8,128]{5,4,3,2,1,0:T(8,128)} %param.14) | copy-start | bytes 3145732
  2.6 31.5 %collective-permute-start = (bf16[128,256]{1,0:T(8,128)(2,1)S(1)}, bf16[128,256]{1,0:T(8,128)(2,1)S(1)}, u32[]{:S(2)}, u32[]{:S(2)}) collective-permute-start(bf16[128,256]{1,0:T(8,128)(2,1)S(1)} %fusion.3), channel_id=1, source_target_pairs={{0,16},{8,24},{16,32},{24,40},{32,48},{40,56},{48,64},{56,72},{64,... | collective-permute-start | bytes 196616 | tf_op jit(solution)/shard_map/ppermute | solution.py:11
  7.4 26.7 %collective-permute-start.1 = (bf16[128,256]{1,0:T(8,128)(2,1)S(1)}, bf16[128,256]{1,0:T(8,128)(2,1)S(1)}, u32[]{:S(2)}, u32[]{:S(2)}) collective-permute-start(bf16[128,256]{1,0:T(8,128)(2,1)S(1)} %fusion.3), channel_id=1, source_target_pairs={{0,8},{8,16},{16,24},{24,32},{32,40},{40,48},{48,56},{56,64},{64,7... | collective-permute-start | bytes 196616 | tf_op jit(solution)/shard_map/ppermute | solution.py:11
  10.6 23.5 %collective-permute-start.2 = (bf16[128,256]{1,0:T(8,128)(2,1)S(1)}, bf16[128,256]{1,0:T(8,128)(2,1)S(1)}, u32[]{:S(2)}, u32[]{:S(2)}) collective-permute-start(bf16[128,256]{1,0:T(8,128)(2,1)S(1)} %fusion.3), channel_id=1, source_target_pairs={{0,504},{8,0},{16,8},{24,16},{32,24},{40,32},{48,40},{56,48},{64,5... | collective-permute-start | bytes 196616 | tf_op jit(solution)/shard_map/ppermute | solution.py:11
  21.1 13.0 %collective-permute-start.3 = (bf16[128,256]{1,0:T(8,128)(2,1)S(1)}, bf16[128,256]{1,0:T(8,128)(2,1)S(1)}, u32[]{:S(2)}, u32[]{:S(2)}) collective-permute-start(bf16[128,256]{1,0:T(8,128)(2,1)S(1)} %fusion.3), channel_id=1, source_target_pairs={{0,496},{8,504},{16,0},{24,8},{32,16},{40,24},{48,32},{56,40},{64,... | collective-permute-start | bytes 196616 | tf_op jit(solution)/shard_map/ppermute | solution.py:11
  34.8 4.3 %copy-start.1 = (bf16[128,256]{1,0:T(8,128)(2,1)S(1)}, bf16[128,256]{1,0:T(8,128)(2,1)}, u32[]{:S(2)}) copy-start(bf16[128,256]{1,0:T(8,128)(2,1)} %param.9) | copy-start | bytes 196612
  34.8 4.3 %copy-start.2 = (bf16[128,256]{1,0:T(8,128)(2,1)S(1)}, bf16[128,256]{1,0:T(8,128)(2,1)}, u32[]{:S(2)}) copy-start(bf16[128,256]{1,0:T(8,128)(2,1)} %param.10) | copy-start | bytes 196612
  34.8 4.3 %copy-start.3 = (bf16[128,256]{1,0:T(8,128)(2,1)S(1)}, bf16[128,256]{1,0:T(8,128)(2,1)}, u32[]{:S(2)}) copy-start(bf16[128,256]{1,0:T(8,128)(2,1)} %param.11) | copy-start | bytes 196612
  35.7 17.2 %collective-permute-start.4 = (f32[4,128,256]{2,1,0:T(8,128)}, f32[4,128,256]{2,1,0:T(8,128)S(1)}, u32[]{:S(2)}, u32[]{:S(2)}) collective-permute-start(f32[4,128,256]{2,1,0:T(8,128)} %slice_select_fusion), channel_id=1, source_target_pairs={{0,1},{1,0},{2,3},{3,2},{4,5},{5,4},{6,7},{7,6},{8,9},{9,8},{10,11... | collective-permute-start | bytes 1572872 | tf_op jit(solution)/shard_map/ppermute | solution.py:61
  40.2 29.5 %all-to-all-start = ((f32[512,1,128]{2,1,0:T(1,128)}), f32[512,1,128]{2,1,0:T(1,128)S(1)}, u32[]{:S(2)}, u32[]{:S(2)}) async-start(f32[512,1,128]{2,1,0:T(1,128)} %bitcast.13), calls=%async_computation | async-start | bytes 524288 | tf_op jit(solution)/shard_map/all_to_all | solution.py:68
  53.0 27.0 %collective-permute-start.5 = (f32[2,128,256]{2,1,0:T(8,128)S(1)}, f32[2,128,256]{2,1,0:T(8,128)S(1)}, u32[]{:S(2)}, u32[]{:S(2)}) collective-permute-start(f32[2,128,256]{2,1,0:T(8,128)S(1)} %slice_select_fusion.1), channel_id=1, source_target_pairs={{0,6},{1,7},{2,4},{3,5},{4,2},{5,3},{6,0},{7,1},{8,14},{9,15},{10,... | collective-permute-start | bytes 786440 | tf_op jit(solution)/shard_map/ppermute | solution.py:61
  71.1 25.9 %all-to-all-start.1 = ((f32[512,1,128]{2,1,0:T(1,128)}), f32[512,1,128]{2,1,0:T(1,128)S(1)}, u32[]{:S(2)}, u32[]{:S(2)}) async-start(f32[512,1,128]{2,1,0:T(1,128)} %broadcast_in_dim.38), calls=%async_computation.1 | async-start | bytes 524288 | tf_op jit(solution)/shard_map/all_to_all | solution.py:72
  80.1 10.6 %collective-permute-start.6 = (f32[1,128,256]{2,1,0:T(8,128)S(1)}, f32[1,128,256]{2,1,0:T(8,128)S(1)}, u32[]{:S(2)}, u32[]{:S(2)}) collective-permute-start(f32[1,128,256]{2,1,0:T(8,128)S(1)} %slice_select_fusion.2), channel_id=1, source_target_pairs={{0,2},{1,3},{2,0},{3,1},{4,6},{5,7},{6,4},{7,5},{8,10},{9,11},{10,... | collective-permute-start | bytes 393224 | tf_op jit(solution)/shard_map/ppermute | solution.py:61

commit v12 on v11

--- a/solution.py
+++ b/solution.py
@@ -63,7 +63,6 @@
     by_core = halved(totals, totals[0::2], totals[1::2], 0, 1)
     by_far = halved(by_core, by_core[:2], by_core[2:], 2, 6)
     owned = halved(by_far, by_far[0:1], by_far[1:2], 1, 2)
-    local_weight, totals = lax.optimization_barrier((local_weight, totals))
     devices = lax.axis_size("blk") * lax.axis_size("rep")
     pieces = lax.all_to_all(
         local_weight.reshape(devices, -1), ("blk", "rep"), 0, 0, tiled=True

time: 101 us -> 101 us (level)
  no operation moved by 1% of the time
where the time goes in v12:
time: 101 us; the launch traced here: 100 us
  starting transfers between devices  56.8 us (56%)
  waiting for transfers between devices  22.8 us (23%)
  other arithmetic  11.2 us (11%)
  local copies, waits for them, and re-layouts  5.71 us (6%)
  matrix products  1.99 us (2%)
  between operations  1.67 us (2%)
    ppermute x4, starting transfers between devices, fetched_from(): lax.ppermute(x, axis, [(i, (i - offset) % size) for i in range(size)])  21.9 us
    ppermute x3, starting transfers between devices, halved(): lax.ppermute(given, 'rep', [(i, i ^ mask) for i in range(replicas)])  13.4 us
    all_to_all x1, starting transfers between devices, on_device(): lax.all_to_all(local_weight.reshape(devices, -1), ('blk', 'rep'), 0, 0, t...  12.6 us
    all_to_all x1, waiting for transfers between devices, on_device(): lax.all_to_all(local_weight.reshape(devices, -1), ('blk', 'rep'), 0, 0, t...  11 us
    all_to_all x1, starting transfers between devices, on_device(): lax.all_to_all(jnp.broadcast_to(piece, (devices,) + piece.shape), ('blk',...  8.89 us
    ppermute x3, waiting for transfers between devices, halved(): lax.ppermute(given, 'rep', [(i, i ^ mask) for i in range(replicas)])  6.25 us
    all_to_all x1, waiting for transfers between devices, on_device(): lax.all_to_all(jnp.broadcast_to(piece, (devices,) + piece.shape), ('blk',...  5.59 us
    reduce_sum x1, other arithmetic, on_device(): jnp.sum((listed[:, :, :, :, None] == positions[None, None, None, None, :]...  4.21 us
  transfers between devices with their start and end apart: 9, of which 3 were waited for; matrix products, arithmetic and copies ran while one was open for 12% of the time, Pallas kernels for 0%

profile of v12, /device:TPU:1, one launch (start us, length us, event | category | flops | bytes accessed | tf_op | source)
XLA Modules:
  0.0 100.3 jit_solution(18178909804167219)
XLA Ops:
  0.6 0.7 convert_rsqrt_fusion
  1.4 1.2 %fusion.3 = bf16[128,256]{1,0:T(8,128)(2,1)S(1)} fusion(bf16[256,256]{1,0:T(8,128)(2,1)} %param.12, f32[128]{0:T(128)S(1)} %convert_rsqrt_fusion, bf16[128,256]{1,0:T(8,128)(2,1)} %param.9, bf16[128,256]{1,0:T(8,128)(2,1)} %param.10), kind=kOutput, calls=%fused_computation.11 | convolution fusion | flops 16908288 | bytes 328192 | tf_op jit(solution)/shard_map/dot_general | solution.py:20
  2.6 4.8 %collective-permute-start = (bf16[128,256]{1,0:T(8,128)(2,1)S(1)}, bf16[128,256]{1,0:T(8,128)(2,1)S(1)}, u32[]{:S(2)}, u32[]{:S(2)}) collective-permute-start(bf16[128,256]{1,0:T(8,128)(2,1)S(1)} %fusion.3), channel_id=1, source_target_pairs={{0,16},{8,24},{16,32},{24,40},{32,48},{40,56},{48,64},{56,72},{64,... | collective-permute-start | bytes 196616 | tf_op jit(solution)/shard_map/ppermute | solution.py:11
  7.4 3.2 %collective-permute-start.1 = (bf16[128,256]{1,0:T(8,128)(2,1)S(1)}, bf16[128,256]{1,0:T(8,128)(2,1)S(1)}, u32[]{:S(2)}, u32[]{:S(2)}) collective-permute-start(bf16[128,256]{1,0:T(8,128)(2,1)S(1)} %fusion.3), channel_id=1, source_target_pairs={{0,8},{8,16},{16,24},{24,32},{32,40},{40,48},{48,56},{56,64},{64,7... | collective-permute-start | bytes 196616 | tf_op jit(solution)/shard_map/ppermute | solution.py:11
  10.6 10.5 %collective-permute-start.2 = (bf16[128,256]{1,0:T(8,128)(2,1)S(1)}, bf16[128,256]{1,0:T(8,128)(2,1)S(1)}, u32[]{:S(2)}, u32[]{:S(2)}) collective-permute-start(bf16[128,256]{1,0:T(8,128)(2,1)S(1)} %fusion.3), channel_id=1, source_target_pairs={{0,504},{8,0},{16,8},{24,16},{32,24},{40,32},{48,40},{56,48},{64,5... | collective-permute-start | bytes 196616 | tf_op jit(solution)/shard_map/ppermute | solution.py:11
  21.1 3.4 %collective-permute-start.3 = (bf16[128,256]{1,0:T(8,128)(2,1)S(1)}, bf16[128,256]{1,0:T(8,128)(2,1)S(1)}, u32[]{:S(2)}, u32[]{:S(2)}) collective-permute-start(bf16[128,256]{1,0:T(8,128)(2,1)S(1)} %fusion.3), channel_id=1, source_target_pairs={{0,496},{8,504},{16,0},{24,8},{32,16},{40,24},{48,32},{56,40},{64,... | collective-permute-start | bytes 196616 | tf_op jit(solution)/shard_map/ppermute | solution.py:11
  25.2 0.8 copy.17
  26.5 1.3 %gather_fusion.1 = s32[5]{0:T(128)S(1)} fusion(s32[64]{0:T(128)} %bitcast.29, s32[1024]{0:T(1024)S(1)} %pad_clamp_fusion), kind=kCustom, calls=%fused_computation.1 | custom fusion | bytes 60 | tf_op jit(solution)/shard_map/jit(_take)/gather | solution.py:35
  28.6 4.2 %fusion.1 = bf16[5,4,128,128]{3,2,1,0:T(8,128)(2,1)S(1)} fusion(s32[5,4,8,128]{3,2,1,0:T(8,128)S(1)} %broadcast_select_fusion), kind=kLoop, calls=%fused_computation.5 | loop fusion | flops 7536640 | bytes 737280 | tf_op jit(solution)/shard_map/reduce_sum | solution.py:41
  32.9 1.1 %multiply_reduce_fusion = bf16[5,128,8,128]{3,2,1,0:T(8,128)(2,1)S(1)} fusion(bf16[5,4,128,128]{3,2,1,0:T(8,128)(2,1)S(1)} %fusion.1, bf16[5,4,8]{2,1,0:T(4,128)(2,1)S(1)} %fusion.7), kind=kLoop, calls=%fused_computation.6 | loop fusion | flops 4587520 | bytes 1966400 | tf_op jit(solution)/shard_map/reduce_sum | solution.py:49
  34.8 0.8 slice_select_fusion
  35.7 3.4 %collective-permute-start.4 = (f32[4,128,256]{2,1,0:T(8,128)}, f32[4,128,256]{2,1,0:T(8,128)S(1)}, u32[]{:S(2)}, u32[]{:S(2)}) collective-permute-start(f32[4,128,256]{2,1,0:T(8,128)} %slice_select_fusion), channel_id=1, source_target_pairs={{0,1},{1,0},{2,3},{3,2},{4,5},{5,4},{6,7},{7,6},{8,9},{9,8},{10,11... | collective-permute-start | bytes 1572872 | tf_op jit(solution)/shard_map/ppermute | solution.py:61
  39.5 0.7 all_to_all.10
  40.2 12.6 %all-to-all-start = ((f32[512,1,128]{2,1,0:T(1,128)}), f32[512,1,128]{2,1,0:T(1,128)S(1)}, u32[]{:S(2)}, u32[]{:S(2)}) async-start(f32[512,1,128]{2,1,0:T(1,128)} %bitcast.13), calls=%async_computation | async-start | bytes 524288 | tf_op jit(solution)/shard_map/all_to_all | solution.py:67
  53.0 5.7 %collective-permute-start.5 = (f32[2,128,256]{2,1,0:T(8,128)S(1)}, f32[2,128,256]{2,1,0:T(8,128)S(1)}, u32[]{:S(2)}, u32[]{:S(2)}) collective-permute-start(f32[2,128,256]{2,1,0:T(8,128)S(1)} %slice_select_fusion.1), channel_id=1, source_target_pairs={{0,6},{1,7},{2,4},{3,5},{4,2},{5,3},{6,0},{7,1},{8,14},{9,15},{10,... | collective-permute-start | bytes 786440 | tf_op jit(solution)/shard_map/ppermute | solution.py:61
  58.7 11.0 %all-to-all-done = f32[512,1,128]{2,1,0:T(1,128)S(1)} async-done(((f32[512,1,128]{2,1,0:T(1,128)}), f32[512,1,128]{2,1,0:T(1,128)S(1)}, u32[]{:S(2)}, u32[]{:S(2)}) %all-to-all-start) | async-done | bytes 262176 | tf_op jit(solution)/shard_map/all_to_all | solution.py:67
  70.2 0.8 broadcast_in_dim.38
  71.1 8.9 %all-to-all-start.1 = ((f32[512,1,128]{2,1,0:T(1,128)}), f32[512,1,128]{2,1,0:T(1,128)S(1)}, u32[]{:S(2)}, u32[]{:S(2)}) async-start(f32[512,1,128]{2,1,0:T(1,128)} %broadcast_in_dim.38), calls=%async_computation.1 | async-start | bytes 524288 | tf_op jit(solution)/shard_map/all_to_all | solution.py:71
  80.1 4.3 %collective-permute-start.6 = (f32[1,128,256]{2,1,0:T(8,128)S(1)}, f32[1,128,256]{2,1,0:T(8,128)S(1)}, u32[]{:S(2)}, u32[]{:S(2)}) collective-permute-start(f32[1,128,256]{2,1,0:T(8,128)S(1)} %slice_select_fusion.2), channel_id=1, source_target_pairs={{0,2},{1,3},{2,0},{3,1},{4,6},{5,7},{6,4},{7,5},{8,10},{9,11},{10,... | collective-permute-start | bytes 393224 | tf_op jit(solution)/shard_map/ppermute | solution.py:61
  84.4 6.2 %collective-permute-done.6 = f32[1,128,256]{2,1,0:T(8,128)S(1)} collective-permute-done((f32[1,128,256]{2,1,0:T(8,128)S(1)}, f32[1,128,256]{2,1,0:T(8,128)S(1)}, u32[]{:S(2)}, u32[]{:S(2)}) %collective-permute-start.6) | collective-permute-done | bytes 131104 | tf_op jit(solution)/shard_map/ppermute | solution.py:61
  90.7 0.7 fusion.5
  91.4 5.6 %all-to-all-done.1 = f32[512,1,128]{2,1,0:T(1,128)S(1)} async-done(((f32[512,1,128]{2,1,0:T(1,128)}), f32[512,1,128]{2,1,0:T(1,128)S(1)}, u32[]{:S(2)}, u32[]{:S(2)}) %all-to-all-start.1) | async-done | bytes 262176 | tf_op jit(solution)/shard_map/all_to_all | solution.py:71
  97.0 1.1 %multiply_reduce_fusion.2 = f32[]{:T(128)} fusion(f32[512,1,128]{2,1,0:T(1,128)S(1)} %all-to-all-done.1), kind=kLoop, calls=%fused_computation.16 | loop fusion | flops 131071 | bytes 262148 | tf_op jit(solution)/shard_map/reduce_sum | solution.py:74
  99.5 0.8 mul.50
  (37 shorter events, 4.6 us)
Async XLA Ops:
  0.6 27.3 %copy-start = (s32[1,1,64,4,8,128]{5,4,3,2,1,0:T(8,128)S(1)}, s32[1,1,64,4,8,128]{5,4,3,2,1,0:T(8,128)}, u32[]{:S(2)}) copy-start(s32[1,1,64,4,8,128]{5,4,3,2,1,0:T(8,128)} %param.14) | copy-start | bytes 3145732
  2.6 31.5 %collective-permute-start = (bf16[128,256]{1,0:T(8,128)(2,1)S(1)}, bf16[128,256]{1,0:T(8,128)(2,1)S(1)}, u32[]{:S(2)}, u32[]{:S(2)}) collective-permute-start(bf16[128,256]{1,0:T(8,128)(2,1)S(1)} %fusion.3), channel_id=1, source_target_pairs={{0,16},{8,24},{16,32},{24,40},{32,48},{40,56},{48,64},{56,72},{64,... | collective-permute-start | bytes 196616 | tf_op jit(solution)/shard_map/ppermute | solution.py:11
  7.4 26.7 %collective-permute-start.1 = (bf16[128,256]{1,0:T(8,128)(2,1)S(1)}, bf16[128,256]{1,0:T(8,128)(2,1)S(1)}, u32[]{:S(2)}, u32[]{:S(2)}) collective-permute-start(bf16[128,256]{1,0:T(8,128)(2,1)S(1)} %fusion.3), channel_id=1, source_target_pairs={{0,8},{8,16},{16,24},{24,32},{32,40},{40,48},{48,56},{56,64},{64,7... | collective-permute-start | bytes 196616 | tf_op jit(solution)/shard_map/ppermute | solution.py:11
  10.6 23.5 %collective-permute-start.2 = (bf16[128,256]{1,0:T(8,128)(2,1)S(1)}, bf16[128,256]{1,0:T(8,128)(2,1)S(1)}, u32[]{:S(2)}, u32[]{:S(2)}) collective-permute-start(bf16[128,256]{1,0:T(8,128)(2,1)S(1)} %fusion.3), channel_id=1, source_target_pairs={{0,504},{8,0},{16,8},{24,16},{32,24},{40,32},{48,40},{56,48},{64,5... | collective-permute-start | bytes 196616 | tf_op jit(solution)/shard_map/ppermute | solution.py:11
  21.1 13.0 %collective-permute-start.3 = (bf16[128,256]{1,0:T(8,128)(2,1)S(1)}, bf16[128,256]{1,0:T(8,128)(2,1)S(1)}, u32[]{:S(2)}, u32[]{:S(2)}) collective-permute-start(bf16[128,256]{1,0:T(8,128)(2,1)S(1)} %fusion.3), channel_id=1, source_target_pairs={{0,496},{8,504},{16,0},{24,8},{32,16},{40,24},{48,32},{56,40},{64,... | collective-permute-start | bytes 196616 | tf_op jit(solution)/shard_map/ppermute | solution.py:11
  34.8 4.3 %copy-start.1 = (bf16[128,256]{1,0:T(8,128)(2,1)S(1)}, bf16[128,256]{1,0:T(8,128)(2,1)}, u32[]{:S(2)}) copy-start(bf16[128,256]{1,0:T(8,128)(2,1)} %param.9) | copy-start | bytes 196612
  34.8 4.3 %copy-start.2 = (bf16[128,256]{1,0:T(8,128)(2,1)S(1)}, bf16[128,256]{1,0:T(8,128)(2,1)}, u32[]{:S(2)}) copy-start(bf16[128,256]{1,0:T(8,128)(2,1)} %param.10) | copy-start | bytes 196612
  34.8 4.3 %copy-start.3 = (bf16[128,256]{1,0:T(8,128)(2,1)S(1)}, bf16[128,256]{1,0:T(8,128)(2,1)}, u32[]{:S(2)}) copy-start(bf16[128,256]{1,0:T(8,128)(2,1)} %param.11) | copy-start | bytes 196612
  35.7 17.2 %collective-permute-start.4 = (f32[4,128,256]{2,1,0:T(8,128)}, f32[4,128,256]{2,1,0:T(8,128)S(1)}, u32[]{:S(2)}, u32[]{:S(2)}) collective-permute-start(f32[4,128,256]{2,1,0:T(8,128)} %slice_select_fusion), channel_id=1, source_target_pairs={{0,1},{1,0},{2,3},{3,2},{4,5},{5,4},{6,7},{7,6},{8,9},{9,8},{10,11... | collective-permute-start | bytes 1572872 | tf_op jit(solution)/shard_map/ppermute | solution.py:61
  40.2 29.5 %all-to-all-start = ((f32[512,1,128]{2,1,0:T(1,128)}), f32[512,1,128]{2,1,0:T(1,128)S(1)}, u32[]{:S(2)}, u32[]{:S(2)}) async-start(f32[512,1,128]{2,1,0:T(1,128)} %bitcast.13), calls=%async_computation | async-start | bytes 524288 | tf_op jit(solution)/shard_map/all_to_all | solution.py:67
  53.0 27.0 %collective-permute-start.5 = (f32[2,128,256]{2,1,0:T(8,128)S(1)}, f32[2,128,256]{2,1,0:T(8,128)S(1)}, u32[]{:S(2)}, u32[]{:S(2)}) collective-permute-start(f32[2,128,256]{2,1,0:T(8,128)S(1)} %slice_select_fusion.1), channel_id=1, source_target_pairs={{0,6},{1,7},{2,4},{3,5},{4,2},{5,3},{6,0},{7,1},{8,14},{9,15},{10,... | collective-permute-start | bytes 786440 | tf_op jit(solution)/shard_map/ppermute | solution.py:61
  71.1 25.9 %all-to-all-start.1 = ((f32[512,1,128]{2,1,0:T(1,128)}), f32[512,1,128]{2,1,0:T(1,128)S(1)}, u32[]{:S(2)}, u32[]{:S(2)}) async-start(f32[512,1,128]{2,1,0:T(1,128)} %broadcast_in_dim.38), calls=%async_computation.1 | async-start | bytes 524288 | tf_op jit(solution)/shard_map/all_to_all | solution.py:71
  80.1 10.6 %collective-permute-start.6 = (f32[1,128,256]{2,1,0:T(8,128)S(1)}, f32[1,128,256]{2,1,0:T(8,128)S(1)}, u32[]{:S(2)}, u32[]{:S(2)}) collective-permute-start(f32[1,128,256]{2,1,0:T(8,128)S(1)} %slice_select_fusion.2), channel_id=1, source_target_pairs={{0,2},{1,3},{2,0},{3,1},{4,6},{5,7},{6,4},{7,5},{8,10},{9,11},{10,... | collective-permute-start | bytes 393224 | tf_op jit(solution)/shard_map/ppermute | solution.py:61

commit v13 on v12

--- a/solution.py
+++ b/solution.py
@@ -21,6 +21,11 @@
         grad_pre, weight, (((1,), (1,)), ((), ())), preferred_element_type=jnp.float32
     )
     scaled = (backward * inv_root[:, None]).astype(jnp.bfloat16)
+    devices = lax.axis_size("blk") * lax.axis_size("rep")
+    pieces = lax.all_to_all(
+        local_weight.reshape(devices, -1), ("blk", "rep"), 0, 0, tiled=True
+    )
+    scaled, pieces = lax.optimization_barrier((scaled, pieces))
 
     blocks = lax.axis_size("blk")
     replicas = lax.axis_size("rep")
@@ -63,11 +68,7 @@
     by_core = halved(totals, totals[0::2], totals[1::2], 0, 1)
     by_far = halved(by_core, by_core[:2], by_core[2:], 2, 6)
     owned = halved(by_far, by_far[0:1], by_far[1:2], 1, 2)
-    devices = lax.axis_size("blk") * lax.axis_size("rep")
-    pieces = lax.all_to_all(
-        local_weight.reshape(devices, -1), ("blk", "rep"), 0, 0, tiled=True
-    )
-    piece = jnp.sum(pieces, axis=0)
+    piece, totals = lax.optimization_barrier((jnp.sum(pieces, axis=0), totals))
     raw_weight = lax.all_to_all(
         jnp.broadcast_to(piece, (devices,) + piece.shape), ("blk", "rep"), 0, 0, tiled=True
     ).reshape(local_weight.shape)

time: 101 us -> 108 us (1.069)
  waiting for transfers between devices: 22.8 us -> 33.4 us
  other arithmetic: 11.2 us -> 9.35 us
  local copies, waits for them, and re-layouts: 5.71 us -> 4.41 us
    all_to_all x1, starting transfers between devices: 12.6 us -> 22.2 us  [on_device(): lax.all_to_all(local_weight.reshape(devices, -1), ('blk', 'rep'), 0, 0, t...]
    ppermute x4, starting transfers between devices: 21.9 us -> 13.9 us  [fetched_from(): lax.ppermute(x, axis, [(i, (i - offset) % size) for i in range(size)])]
    ppermute x4, waiting for transfers between devices: 0.01 us -> 6.05 us  [fetched_from(): lax.ppermute(x, axis, [(i, (i - offset) % size) for i in range(size)])]
    all_to_all x1, waiting for transfers between devices: 5.59 us -> 11 us  [on_device(): lax.all_to_all(jnp.broadcast_to(piece, (devices,) + piece.shape), ('blk',...]
  transfers between devices with their start and end apart: 9 -> 9, of which waited for: 3 -> 4; matrix products, arithmetic and copies ran while one was open for 12% -> 11% of each run, Pallas kernels for 0% -> 0%
where the time goes in v13:
time: 108 us
  starting transfers between devices  57.1 us (53%)
  waiting for transfers between devices  33.4 us (31%)
  other arithmetic  9.35 us (9%)
  local copies, waits for them, and re-layouts  4.41 us (4%)
  matrix products  1.99 us (2%)
  between operations  1.75 us (2%)
    all_to_all x1, starting transfers between devices, on_device(): lax.all_to_all(local_weight.reshape(devices, -1), ('blk', 'rep'), 0, 0, t...  22.2 us
    ppermute x4, starting transfers between devices, fetched_from(): lax.ppermute(x, axis, [(i, (i - offset) % size) for i in range(size)])  13.9 us
    ppermute x3, starting transfers between devices, halved(): lax.ppermute(given, 'rep', [(i, i ^ mask) for i in range(replicas)])  12.7 us
    all_to_all x1, waiting for transfers between devices, on_device(): lax.all_to_all(jnp.broadcast_to(piece, (devices,) + piece.shape), ('blk',...  11 us
    all_to_all x1, waiting for transfers between devices, on_device(): lax.all_to_all(local_weight.reshape(devices, -1), ('blk', 'rep'), 0, 0, t...  10.1 us
    all_to_all x1, starting transfers between devices, on_device(): lax.all_to_all(jnp.broadcast_to(piece, (devices,) + piece.shape), ('blk',...  8.35 us
    ppermute x3, waiting for transfers between devices, halved(): lax.ppermute(given, 'rep', [(i, i ^ mask) for i in range(replicas)])  6.21 us
    ppermute x4, waiting for transfers between devices, fetched_from(): lax.ppermute(x, axis, [(i, (i - offset) % size) for i in range(size)])  6.05 us
  transfers between devices with their start and end apart: 9, of which 4 were waited for; matrix products, arithmetic and copies ran while one was open for 11% of the time, Pallas kernels for 0%

profile of v13, /device:TPU:1, one launch (start us, length us, event | category | flops | bytes accessed | tf_op | source)
XLA Modules:
  0.0 108.0 jit_solution(8633465880491996161)
XLA Ops:
  0.7 1.2 %convolution_bitcast_fusion.1 = f32[256,256]{0,1:T(8,128)S(1)} fusion(bf16[128,256]{1,0:T(8,128)(2,1)} %param.11, bf16[128,256]{1,0:T(8,128)(2,1)} %param.9, bf16[128,256]{1,0:T(8,128)(2,1)} %param.10), kind=kOutput, calls=%fused_computation.9 | convolution fusion | flops 16842752 | bytes 458752 | tf_op jit(solution)/shard_map/dot_general | solution.py:16
  2.1 0.7 all_to_all.12
  2.8 22.2 %all-to-all-start = ((f32[512,1,128]{2,1,0:T(1,128)}), f32[512,1,128]{2,1,0:T(1,128)S(1)}, u32[]{:S(2)}, u32[]{:S(2)}) async-start(f32[512,1,128]{2,1,0:T(1,128)} %bitcast.4), calls=%async_computation | async-start | bytes 524288 | tf_op jit(solution)/shard_map/all_to_all | solution.py:25
  25.0 0.6 gather_fusion.1
  27.4 4.2 %fusion.1 = bf16[5,4,128,128]{3,2,1,0:T(8,128)(2,1)S(1)} fusion(s32[5,4,8,128]{3,2,1,0:T(8,128)S(1)} %broadcast_select_fusion), kind=kLoop, calls=%fused_computation.5 | loop fusion | flops 7536640 | bytes 737280 | tf_op jit(solution)/shard_map/reduce_sum | solution.py:46
  31.7 10.1 %all-to-all-done = f32[512,1,128]{2,1,0:T(1,128)S(1)} async-done(((f32[512,1,128]{2,1,0:T(1,128)}), f32[512,1,128]{2,1,0:T(1,128)S(1)}, u32[]{:S(2)}, u32[]{:S(2)}) %all-to-all-start) | async-done | bytes 262176 | tf_op jit(solution)/shard_map/all_to_all | solution.py:25
  41.8 2.7 %collective-permute-start = (bf16[128,256]{1,0:T(8,128)(2,1)S(1)}, bf16[128,256]{1,0:T(8,128)(2,1)S(1)}, u32[]{:S(2)}, u32[]{:S(2)}) collective-permute-start(bf16[128,256]{1,0:T(8,128)(2,1)S(1)} %fusion.3), channel_id=1, source_target_pairs={{0,16},{8,24},{16,32},{24,40},{32,48},{40,56},{48,64},{56,72},{64,... | collective-permute-start | bytes 196616 | tf_op jit(solution)/shard_map/ppermute | solution.py:11
  44.5 1.1 %multiply_reduce_fusion = bf16[5,128,8,128]{3,2,1,0:T(8,128)(2,1)S(1)} fusion(bf16[5,4,128,128]{3,2,1,0:T(8,128)(2,1)S(1)} %fusion.1, bf16[5,4,8]{2,1,0:T(4,128)(2,1)S(1)} %fusion.7), kind=kLoop, calls=%fused_computation.6 | loop fusion | flops 4587520 | bytes 1966400 | tf_op jit(solution)/shard_map/reduce_sum | solution.py:54
  45.7 5.9 %collective-permute-start.3 = (bf16[128,256]{1,0:T(8,128)(2,1)S(1)}, bf16[128,256]{1,0:T(8,128)(2,1)S(1)}, u32[]{:S(2)}, u32[]{:S(2)}) collective-permute-start(bf16[128,256]{1,0:T(8,128)(2,1)S(1)} %fusion.3), channel_id=1, source_target_pairs={{0,496},{8,504},{16,0},{24,8},{32,16},{40,24},{48,32},{56,40},{64,... | collective-permute-start | bytes 196616 | tf_op jit(solution)/shard_map/ppermute | solution.py:11
  51.5 2.1 %collective-permute-start.2 = (bf16[128,256]{1,0:T(8,128)(2,1)S(1)}, bf16[128,256]{1,0:T(8,128)(2,1)S(1)}, u32[]{:S(2)}, u32[]{:S(2)}) collective-permute-start(bf16[128,256]{1,0:T(8,128)(2,1)S(1)} %fusion.3), channel_id=1, source_target_pairs={{0,504},{8,0},{16,8},{24,16},{32,24},{40,32},{48,40},{56,48},{64,5... | collective-permute-start | bytes 196616 | tf_op jit(solution)/shard_map/ppermute | solution.py:11
  53.7 3.2 %collective-permute-start.1 = (bf16[128,256]{1,0:T(8,128)(2,1)S(1)}, bf16[128,256]{1,0:T(8,128)(2,1)S(1)}, u32[]{:S(2)}, u32[]{:S(2)}) collective-permute-start(bf16[128,256]{1,0:T(8,128)(2,1)S(1)} %fusion.3), channel_id=1, source_target_pairs={{0,8},{8,16},{16,24},{24,32},{32,40},{40,48},{48,56},{56,64},{64,7... | collective-permute-start | bytes 196616 | tf_op jit(solution)/shard_map/ppermute | solution.py:11
  56.9 6.0 %collective-permute-done.1 = bf16[128,256]{1,0:T(8,128)(2,1)S(1)} collective-permute-done((bf16[128,256]{1,0:T(8,128)(2,1)S(1)}, bf16[128,256]{1,0:T(8,128)(2,1)S(1)}, u32[]{:S(2)}, u32[]{:S(2)}) %collective-permute-start.1) | collective-permute-done | bytes 65568 | tf_op jit(solution)/shard_map/ppermute | solution.py:11
  63.6 0.9 slice_select_fusion
  64.5 4.2 %collective-permute-start.4 = (f32[4,128,256]{2,1,0:T(8,128)}, f32[4,128,256]{2,1,0:T(8,128)S(1)}, u32[]{:S(2)}, u32[]{:S(2)}) collective-permute-start(f32[4,128,256]{2,1,0:T(8,128)} %slice_select_fusion), channel_id=1, source_target_pairs={{0,1},{1,0},{2,3},{3,2},{4,5},{5,4},{6,7},{7,6},{8,9},{9,8},{10,11... | collective-permute-start | bytes 1572872 | tf_op jit(solution)/shard_map/ppermute | solution.py:66
  68.8 0.8 broadcast_in_dim.38
  69.6 8.3 %all-to-all-start.1 = ((f32[512,1,128]{2,1,0:T(1,128)}), f32[512,1,128]{2,1,0:T(1,128)S(1)}, u32[]{:S(2)}, u32[]{:S(2)}) async-start(f32[512,1,128]{2,1,0:T(1,128)} %broadcast_in_dim.38), calls=%async_computation.1 | async-start | bytes 524288 | tf_op jit(solution)/shard_map/all_to_all | solution.py:72
  78.2 5.7 %collective-permute-start.5 = (f32[2,128,256]{2,1,0:T(8,128)S(1)}, f32[2,128,256]{2,1,0:T(8,128)S(1)}, u32[]{:S(2)}, u32[]{:S(2)}) collective-permute-start(f32[2,128,256]{2,1,0:T(8,128)S(1)} %slice_select_fusion.1), channel_id=1, source_target_pairs={{0,6},{1,7},{2,4},{3,5},{4,2},{5,3},{6,0},{7,1},{8,14},{9,15},{10,... | collective-permute-start | bytes 786440 | tf_op jit(solution)/shard_map/ppermute | solution.py:66
  83.8 11.0 %all-to-all-done.1 = f32[512,1,128]{2,1,0:T(1,128)S(1)} async-done(((f32[512,1,128]{2,1,0:T(1,128)}), f32[512,1,128]{2,1,0:T(1,128)S(1)}, u32[]{:S(2)}, u32[]{:S(2)}) %all-to-all-start.1) | async-done | bytes 262176 | tf_op jit(solution)/shard_map/all_to_all | solution.py:72
  94.8 1.1 %multiply_reduce_fusion.2 = f32[]{:T(128)} fusion(f32[512,1,128]{2,1,0:T(1,128)S(1)} %all-to-all-done.1), kind=kLoop, calls=%fused_computation.16 | loop fusion | flops 131071 | bytes 262148 | tf_op jit(solution)/shard_map/reduce_sum | solution.py:75
  96.8 2.8 %collective-permute-start.6 = (f32[1,128,256]{2,1,0:T(8,128)S(1)}, f32[1,128,256]{2,1,0:T(8,128)S(1)}, u32[]{:S(2)}, u32[]{:S(2)}) collective-permute-start(f32[1,128,256]{2,1,0:T(8,128)S(1)} %slice_select_fusion.2), channel_id=1, source_target_pairs={{0,2},{1,3},{2,0},{3,1},{4,6},{5,7},{6,4},{7,5},{8,10},{9,11},{10,... | collective-permute-start | bytes 393224 | tf_op jit(solution)/shard_map/ppermute | solution.py:66
  99.6 0.7 multiply_reduce_fusion.1
  100.3 0.8 mul.50
  101.0 6.2 %collective-permute-done.6 = f32[1,128,256]{2,1,0:T(8,128)S(1)} collective-permute-done((f32[1,128,256]{2,1,0:T(8,128)S(1)}, f32[1,128,256]{2,1,0:T(8,128)S(1)}, u32[]{:S(2)}, u32[]{:S(2)}) %collective-permute-start.6) | collective-permute-done | bytes 131104 | tf_op jit(solution)/shard_map/ppermute | solution.py:66
  107.2 0.7 fusion.5
  (49 shorter events, 2.9 us)
Async XLA Ops:
  0.6 25.8 %copy-start = (s32[1,1,64,4,8,128]{5,4,3,2,1,0:T(8,128)S(1)}, s32[1,1,64,4,8,128]{5,4,3,2,1,0:T(8,128)}, u32[]{:S(2)}) copy-start(s32[1,1,64,4,8,128]{5,4,3,2,1,0:T(8,128)} %param.14) | copy-start | bytes 3145732
  0.6 24.3 %copy-start.8 = (s32[5]{0:T(128)S(1)}, s32[5]{0:T(128)}, u32[]{:S(2)}) copy-start(s32[5]{0:T(128)} %constant.81.clone) | copy-start | bytes 64
  0.7 24.3 %copy-start.1 = (s32[1,1,64]{2,1,0:T(1,128)S(1)}, s32[1,1,64]{2,1,0:T(1,128)}, u32[]{:S(2)}) copy-start(s32[1,1,64]{2,1,0:T(1,128)} %param.16) | copy-start | bytes 772
  0.7 25.1 %copy-start.7 = (s32[1,1,64,4]{2,3,1,0:T(4,128)S(1)}, s32[1,1,64,4]{2,3,1,0:T(4,128)}, u32[]{:S(2)}) copy-start(s32[1,1,64,4]{2,3,1,0:T(4,128)} %param.15) | copy-start | bytes 3076
  1.9 25.3 %copy-start.9 = (s32[128]{0:T(128)S(1)}, s32[128]{0:T(128)}, u32[]{:S(2)}) copy-start(s32[128]{0:T(128)} %param.13) | copy-start | bytes 1540
  1.9 25.3 %copy-start.4 = (bf16[128,256]{1,0:T(8,128)(2,1)S(1)}, bf16[128,256]{1,0:T(8,128)(2,1)}, u32[]{:S(2)}) copy-start(bf16[128,256]{1,0:T(8,128)(2,1)} %param.9) | copy-start | bytes 196612
  1.9 25.3 %copy-start.5 = (bf16[128,256]{1,0:T(8,128)(2,1)S(1)}, bf16[128,256]{1,0:T(8,128)(2,1)}, u32[]{:S(2)}) copy-start(bf16[128,256]{1,0:T(8,128)(2,1)} %param.10) | copy-start | bytes 196612
  1.9 25.3 %copy-start.6 = (bf16[256,256]{1,0:T(8,128)(2,1)S(1)}, bf16[256,256]{1,0:T(8,128)(2,1)}, u32[]{:S(2)}) copy-start(bf16[256,256]{1,0:T(8,128)(2,1)} %param.12) | copy-start | bytes 393220
  2.8 39.0 %all-to-all-start = ((f32[512,1,128]{2,1,0:T(1,128)}), f32[512,1,128]{2,1,0:T(1,128)S(1)}, u32[]{:S(2)}, u32[]{:S(2)}) async-start(f32[512,1,128]{2,1,0:T(1,128)} %bitcast.4), calls=%async_computation | async-start | bytes 524288 | tf_op jit(solution)/shard_map/all_to_all | solution.py:25
  41.8 21.2 %copy-start.2 = (f32[512,1,128]{2,1,0:T(1,128)}, f32[512,1,128]{2,1,0:T(1,128)S(1)}, u32[]{:S(2)}) copy-start(f32[512,1,128]{2,1,0:T(1,128)S(1)} %all-to-all-done) | copy-start | bytes 786436
  41.8 15.0 %collective-permute-start = (bf16[128,256]{1,0:T(8,128)(2,1)S(1)}, bf16[128,256]{1,0:T(8,128)(2,1)S(1)}, u32[]{:S(2)}, u32[]{:S(2)}) collective-permute-start(bf16[128,256]{1,0:T(8,128)(2,1)S(1)} %fusion.3), channel_id=1, source_target_pairs={{0,16},{8,24},{16,32},{24,40},{32,48},{40,56},{48,64},{56,72},{64,... | collective-permute-start | bytes 196616 | tf_op jit(solution)/shard_map/ppermute | solution.py:11
  45.7 17.3 %collective-permute-start.3 = (bf16[128,256]{1,0:T(8,128)(2,1)S(1)}, bf16[128,256]{1,0:T(8,128)(2,1)S(1)}, u32[]{:S(2)}, u32[]{:S(2)}) collective-permute-start(bf16[128,256]{1,0:T(8,128)(2,1)S(1)} %fusion.3), channel_id=1, source_target_pairs={{0,496},{8,504},{16,0},{24,8},{32,16},{40,24},{48,32},{56,40},{64,... | collective-permute-start | bytes 196616 | tf_op jit(solution)/shard_map/ppermute | solution.py:11
  51.5 11.4 %collective-permute-start.2 = (bf16[128,256]{1,0:T(8,128)(2,1)S(1)}, bf16[128,256]{1,0:T(8,128)(2,1)S(1)}, u32[]{:S(2)}, u32[]{:S(2)}) collective-permute-start(bf16[128,256]{1,0:T(8,128)(2,1)S(1)} %fusion.3), channel_id=1, source_target_pairs={{0,504},{8,0},{16,8},{24,16},{32,24},{40,32},{48,40},{56,48},{64,5... | collective-permute-start | bytes 196616 | tf_op jit(solution)/shard_map/ppermute | solution.py:11
  53.7 9.2 %collective-permute-start.1 = (bf16[128,256]{1,0:T(8,128)(2,1)S(1)}, bf16[128,256]{1,0:T(8,128)(2,1)S(1)}, u32[]{:S(2)}, u32[]{:S(2)}) collective-permute-start(bf16[128,256]{1,0:T(8,128)(2,1)S(1)} %fusion.3), channel_id=1, source_target_pairs={{0,8},{8,16},{16,24},{24,32},{32,40},{40,48},{48,56},{56,64},{64,7... | collective-permute-start | bytes 196616 | tf_op jit(solution)/shard_map/ppermute | solution.py:11
  63.6 5.1 %copy-start.3 = (f32[512,1,128]{2,1,0:T(1,128)S(1)}, f32[512,1,128]{2,1,0:T(1,128)}, u32[]{:S(2)}) copy-start(f32[512,1,128]{2,1,0:T(1,128)} %copy-done.2) | copy-start | bytes 786436
  64.5 13.5 %collective-permute-start.4 = (f32[4,128,256]{2,1,0:T(8,128)}, f32[4,128,256]{2,1,0:T(8,128)S(1)}, u32[]{:S(2)}, u32[]{:S(2)}) collective-permute-start(f32[4,128,256]{2,1,0:T(8,128)} %slice_select_fusion), channel_id=1, source_target_pairs={{0,1},{1,0},{2,3},{3,2},{4,5},{5,4},{6,7},{7,6},{8,9},{9,8},{10,11... | collective-permute-start | bytes 1572872 | tf_op jit(solution)/shard_map/ppermute | solution.py:66
  69.6 25.2 %all-to-all-start.1 = ((f32[512,1,128]{2,1,0:T(1,128)}), f32[512,1,128]{2,1,0:T(1,128)S(1)}, u32[]{:S(2)}, u32[]{:S(2)}) async-start(f32[512,1,128]{2,1,0:T(1,128)} %broadcast_in_dim.38), calls=%async_computation.1 | async-start | bytes 524288 | tf_op jit(solution)/shard_map/all_to_all | solution.py:72
  78.2 18.5 %collective-permute-start.5 = (f32[2,128,256]{2,1,0:T(8,128)S(1)}, f32[2,128,256]{2,1,0:T(8,128)S(1)}, u32[]{:S(2)}, u32[]{:S(2)}) collective-permute-start(f32[2,128,256]{2,1,0:T(8,128)S(1)} %slice_select_fusion.1), channel_id=1, source_target_pairs={{0,6},{1,7},{2,4},{3,5},{4,2},{5,3},{6,0},{7,1},{8,14},{9,15},{10,... | collective-permute-start | bytes 786440 | tf_op jit(solution)/shard_map/ppermute | solution.py:66
  96.8 10.5 %collective-permute-start.6 = (f32[1,128,256]{2,1,0:T(8,128)S(1)}, f32[1,128,256]{2,1,0:T(8,128)S(1)}, u32[]{:S(2)}, u32[]{:S(2)}) collective-permute-start(f32[1,128,256]{2,1,0:T(8,128)S(1)} %slice_select_fusion.2), channel_id=1, source_target_pairs={{0,2},{1,3},{2,0},{3,1},{4,6},{5,7},{6,4},{7,5},{8,10},{9,11},{10,... | collective-permute-start | bytes 393224 | tf_op jit(solution)/shard_map/ppermute | solution.py:66

commit v14 on v11

--- a/solution.py
+++ b/solution.py
@@ -69,10 +69,13 @@
         local_weight.reshape(devices, -1), ("blk", "rep"), 0, 0, tiled=True
     )
     piece = jnp.sum(pieces, axis=0)
-    raw_weight = lax.all_to_all(
-        jnp.broadcast_to(piece, (devices,) + piece.shape), ("blk", "rep"), 0, 0, tiled=True
-    ).reshape(local_weight.shape)
-    norm_value = jnp.sqrt(jnp.sum(raw_weight * raw_weight) + 1e-06)
+    squares = jnp.zeros_like(piece).at[0].set(jnp.sum(piece * piece))
+    sent = jnp.stack([piece, squares])
+    gathered = lax.all_to_all(
+        jnp.broadcast_to(sent, (devices,) + sent.shape), ("blk", "rep"), 0, 0, tiled=True
+    )
+    raw_weight = gathered[:, 0].reshape(local_weight.shape)
+    norm_value = jnp.sqrt(jnp.sum(gathered[:, 1, 0]) + 1e-06)
     grad_weight = raw_weight * jnp.minimum(1.0, 128.0 / norm_value)
     grad_features = (owned[0] * inv_root[:, None]).astype(jnp.bfloat16)
     return (grad_features, grad_weight)

time: 101 us -> 112 us (1.11)
  starting transfers between devices: 56.8 us -> 60.7 us
  waiting for transfers between devices: 22.9 us -> 26.8 us
  other arithmetic: 11.2 us -> 12.7 us
    ppermute x3, waiting for transfers between devices: 6.25 us -> 9.68 us  [halved(): lax.ppermute(given, 'rep', [(i, i ^ mask) for i in range(replicas)])]
    all_to_all x1, starting transfers between devices: 8.89 us -> 11.5 us  [on_device(): lax.all_to_all(jnp.broadcast_to(sent, (devices,) + sent.shape), ('blk', '...]
    all_to_all x1, starting transfers between devices: 12.6 us -> 14 us  [on_device(): lax.all_to_all(local_weight.reshape(devices, -1), ('blk', 'rep'), 0, 0, t...]
  transfers between devices with their start and end apart: 9 -> 9, of which waited for: 3 -> 3; matrix products, arithmetic and copies ran while one was open for 12% -> 13% of each run, Pallas kernels for 0% -> 0%
where the time goes in v14:
time: 112 us; the launch traced here: 111 us
  starting transfers between devices  60.7 us (54%)
  waiting for transfers between devices  26.8 us (24%)
  other arithmetic  12.7 us (11%)
  local copies, waits for them, and re-layouts  6.74 us (6%)
  matrix products  2.7 us (2%)
  between operations  1.64 us (1%)
    ppermute x4, starting transfers between devices, fetched_from(): lax.ppermute(x, axis, [(i, (i - offset) % size) for i in range(size)])  21.9 us
    all_to_all x1, starting transfers between devices, on_device(): lax.all_to_all(local_weight.reshape(devices, -1), ('blk', 'rep'), 0, 0, t...  14 us
    ppermute x3, starting transfers between devices, halved(): lax.ppermute(given, 'rep', [(i, i ^ mask) for i in range(replicas)])  13.3 us
    all_to_all x1, starting transfers between devices, on_device(): lax.all_to_all(jnp.broadcast_to(sent, (devices,) + sent.shape), ('blk', '...  11.5 us
    all_to_all x1, waiting for transfers between devices, on_device(): lax.all_to_all(local_weight.reshape(devices, -1), ('blk', 'rep'), 0, 0, t...  10.5 us
    ppermute x3, waiting for transfers between devices, halved(): lax.ppermute(given, 'rep', [(i, i ^ mask) for i in range(replicas)])  9.68 us
    all_to_all x1, waiting for transfers between devices, on_device(): lax.all_to_all(jnp.broadcast_to(sent, (devices,) + sent.shape), ('blk', '...  6.57 us
    reduce_sum x1, other arithmetic, on_device(): jnp.sum((listed[:, :, :, :, None] == positions[None, None, None, None, :]...  4.22 us
  transfers between devices with their start and end apart: 9, of which 3 were waited for; matrix products, arithmetic and copies ran while one was open for 13% of the time, Pallas kernels for 0%

profile of v14, /device:TPU:1, one launch (start us, length us, event | category | flops | bytes accessed | tf_op | source)
XLA Modules:
  0.0 111.3 jit_solution(12013847140555424025)
XLA Ops:
  0.6 0.7 convert_rsqrt_fusion
  1.4 1.2 %fusion.3 = bf16[128,256]{1,0:T(8,128)(2,1)S(1)} fusion(bf16[256,256]{1,0:T(8,128)(2,1)} %param.14, f32[128]{0:T(128)S(1)} %convert_rsqrt_fusion, bf16[128,256]{1,0:T(8,128)(2,1)} %param.11, bf16[128,256]{1,0:T(8,128)(2,1)} %param.12), kind=kOutput, calls=%fused_computation.11 | convolution fusion | flops 16908288 | bytes 328192 | tf_op jit(solution)/shard_map/dot_general | solution.py:20
  2.6 4.8 %collective-permute-start = (bf16[128,256]{1,0:T(8,128)(2,1)S(1)}, bf16[128,256]{1,0:T(8,128)(2,1)S(1)}, u32[]{:S(2)}, u32[]{:S(2)}) collective-permute-start(bf16[128,256]{1,0:T(8,128)(2,1)S(1)} %fusion.3), channel_id=1, source_target_pairs={{0,16},{8,24},{16,32},{24,40},{32,48},{40,56},{48,64},{56,72},{64,... | collective-permute-start | bytes 196616 | tf_op jit(solution)/shard_map/ppermute | solution.py:11
  7.4 3.2 %collective-permute-start.1 = (bf16[128,256]{1,0:T(8,128)(2,1)S(1)}, bf16[128,256]{1,0:T(8,128)(2,1)S(1)}, u32[]{:S(2)}, u32[]{:S(2)}) collective-permute-start(bf16[128,256]{1,0:T(8,128)(2,1)S(1)} %fusion.3), channel_id=1, source_target_pairs={{0,8},{8,16},{16,24},{24,32},{32,40},{40,48},{48,56},{56,64},{64,7... | collective-permute-start | bytes 196616 | tf_op jit(solution)/shard_map/ppermute | solution.py:11
  10.6 10.5 %collective-permute-start.2 = (bf16[128,256]{1,0:T(8,128)(2,1)S(1)}, bf16[128,256]{1,0:T(8,128)(2,1)S(1)}, u32[]{:S(2)}, u32[]{:S(2)}) collective-permute-start(bf16[128,256]{1,0:T(8,128)(2,1)S(1)} %fusion.3), channel_id=1, source_target_pairs={{0,504},{8,0},{16,8},{24,16},{32,24},{40,32},{48,40},{56,48},{64,5... | collective-permute-start | bytes 196616 | tf_op jit(solution)/shard_map/ppermute | solution.py:11
  21.1 3.4 %collective-permute-start.3 = (bf16[128,256]{1,0:T(8,128)(2,1)S(1)}, bf16[128,256]{1,0:T(8,128)(2,1)S(1)}, u32[]{:S(2)}, u32[]{:S(2)}) collective-permute-start(bf16[128,256]{1,0:T(8,128)(2,1)S(1)} %fusion.3), channel_id=1, source_target_pairs={{0,496},{8,504},{16,0},{24,8},{32,16},{40,24},{48,32},{56,40},{64,... | collective-permute-start | bytes 196616 | tf_op jit(solution)/shard_map/ppermute | solution.py:11
  25.2 0.8 copy.17
  26.5 1.3 %gather_fusion.1 = s32[5]{0:T(128)S(1)} fusion(s32[64]{0:T(128)} %bitcast.31, s32[1024]{0:T(1024)S(1)} %pad_clamp_fusion), kind=kCustom, calls=%fused_computation.1 | custom fusion | bytes 60 | tf_op jit(solution)/shard_map/jit(_take)/gather | solution.py:35
  28.7 4.2 %fusion.1 = bf16[5,4,128,128]{3,2,1,0:T(8,128)(2,1)S(1)} fusion(s32[5,4,8,128]{3,2,1,0:T(8,128)S(1)} %broadcast_select_fusion), kind=kLoop, calls=%fused_computation.5 | loop fusion | flops 7536640 | bytes 737280 | tf_op jit(solution)/shard_map/reduce_sum | solution.py:41
  33.0 1.1 %multiply_reduce_fusion = bf16[5,128,8,128]{3,2,1,0:T(8,128)(2,1)S(1)} fusion(bf16[5,4,128,128]{3,2,1,0:T(8,128)(2,1)S(1)} %fusion.1, bf16[5,4,8]{2,1,0:T(4,128)(2,1)S(1)} %fusion.8), kind=kLoop, calls=%fused_computation.6 | loop fusion | flops 4587520 | bytes 1966400 | tf_op jit(solution)/shard_map/reduce_sum | solution.py:49
  34.1 0.9 convolution_bitcast_fusion.1
  35.8 1.1 copy.19
  37.6 14.0 %all-to-all-start = ((f32[512,1,128]{2,1,0:T(1,128)}), f32[512,1,128]{2,1,0:T(1,128)S(1)}, u32[]{:S(2)}, u32[]{:S(2)}) async-start(f32[512,1,128]{2,1,0:T(1,128)} %bitcast.13), calls=%async_computation | async-start | bytes 524288 | tf_op jit(solution)/shard_map/all_to_all | solution.py:68
  51.7 6.2 %collective-permute-start.4 = (f32[4,128,256]{2,1,0:T(8,128)S(1)}, f32[4,128,256]{2,1,0:T(8,128)}, u32[]{:S(2)}, u32[]{:S(2)}) collective-permute-start(f32[4,128,256]{2,1,0:T(8,128)S(1)} %slice_select_fusion), channel_id=1, source_target_pairs={{0,1},{1,0},{2,3},{3,2},{4,5},{5,4},{6,7},{7,6},{8,9},{9,8},{10,11... | collective-permute-start | bytes 1572872 | tf_op jit(solution)/shard_map/ppermute | solution.py:61
  57.9 10.5 %all-to-all-done = f32[512,1,128]{2,1,0:T(1,128)S(1)} async-done(((f32[512,1,128]{2,1,0:T(1,128)}), f32[512,1,128]{2,1,0:T(1,128)S(1)}, u32[]{:S(2)}, u32[]{:S(2)}) %all-to-all-start) | async-done | bytes 262176 | tf_op jit(solution)/shard_map/all_to_all | solution.py:68
  69.6 1.1 %select_add_fusion = f32[4,128,256]{2,1,0:T(8,128)S(1)} fusion(f32[4,128,256]{2,1,0:T(8,128)} %collective-permute-done.4, f32[8,128,256]{2,1,0:T(8,128)S(1)} %convolution_bitcast_fusion, pred[]{:T(512)S(6)} %eq.46), kind=kLoop, calls=%fused_computation.12 | loop fusion | flops 262144 | bytes 2097153 | tf_op jit(solution)/shard_map/add | solution.py:61
  70.8 2.3 %collective-permute-start.5 = (f32[2,128,256]{2,1,0:T(8,128)S(1)}, f32[2,128,256]{2,1,0:T(8,128)S(1)}, u32[]{:S(2)}, u32[]{:S(2)}) collective-permute-start(f32[2,128,256]{2,1,0:T(8,128)S(1)} %slice_select_fusion.1), channel_id=1, source_target_pairs={{0,6},{1,7},{2,4},{3,5},{4,2},{5,3},{6,0},{7,1},{8,14},{9,15},{10,... | collective-permute-start | bytes 786440 | tf_op jit(solution)/shard_map/ppermute | solution.py:61
  73.7 0.9 broadcast_in_dim.39
  74.6 11.5 %all-to-all-start.1 = ((f32[512,2,128]{2,1,0:T(2,128)}), f32[512,2,128]{2,1,0:T(2,128)S(1)}, u32[]{:S(2)}, u32[]{:S(2)}) async-start(f32[512,2,128]{2,1,0:T(2,128)} %broadcast_in_dim.39), calls=%async_computation.1 | async-start | bytes 1048576 | tf_op jit(solution)/shard_map/all_to_all | solution.py:74
  86.2 4.8 %collective-permute-start.6 = (f32[1,128,256]{2,1,0:T(8,128)S(1)}, f32[1,128,256]{2,1,0:T(8,128)S(1)}, u32[]{:S(2)}, u32[]{:S(2)}) collective-permute-start(f32[1,128,256]{2,1,0:T(8,128)S(1)} %slice_select_fusion.2), channel_id=1, source_target_pairs={{0,2},{1,3},{2,0},{3,1},{4,6},{5,7},{6,4},{7,5},{8,10},{9,11},{10,... | collective-permute-start | bytes 393224 | tf_op jit(solution)/shard_map/ppermute | solution.py:61
  91.1 9.7 %collective-permute-done.6 = f32[1,128,256]{2,1,0:T(8,128)S(1)} collective-permute-done((f32[1,128,256]{2,1,0:T(8,128)S(1)}, f32[1,128,256]{2,1,0:T(8,128)S(1)}, u32[]{:S(2)}, u32[]{:S(2)}) %collective-permute-start.6) | collective-permute-done | bytes 131104 | tf_op jit(solution)/shard_map/ppermute | solution.py:61
  101.5 6.6 %all-to-all-done.1 = f32[512,2,128]{2,1,0:T(2,128)S(1)} async-done(((f32[512,2,128]{2,1,0:T(2,128)}), f32[512,2,128]{2,1,0:T(2,128)S(1)}, u32[]{:S(2)}, u32[]{:S(2)}) %all-to-all-start.1) | async-done | bytes 524320 | tf_op jit(solution)/shard_map/all_to_all | solution.py:74
  108.0 1.1 %slice_reduce_fusion = f32[]{:T(128)} fusion(f32[512,2,128]{2,1,0:T(2,128)S(1)} %all-to-all-done.1), kind=kLoop, calls=%fused_computation.15 | loop fusion | flops 511 | bytes 2052 | tf_op jit(solution)/shard_map/reduce_sum | solution.py:78
  110.6 0.8 mul.48
  (39 shorter events, 6.9 us)
Async XLA Ops:
  0.6 27.3 %copy-start = (s32[1,1,64,4,8,128]{5,4,3,2,1,0:T(8,128)S(1)}, s32[1,1,64,4,8,128]{5,4,3,2,1,0:T(8,128)}, u32[]{:S(2)}) copy-start(s32[1,1,64,4,8,128]{5,4,3,2,1,0:T(8,128)} %param.16) | copy-start | bytes 3145732
  2.6 32.5 %collective-permute-start = (bf16[128,256]{1,0:T(8,128)(2,1)S(1)}, bf16[128,256]{1,0:T(8,128)(2,1)S(1)}, u32[]{:S(2)}, u32[]{:S(2)}) collective-permute-start(bf16[128,256]{1,0:T(8,128)(2,1)S(1)} %fusion.3), channel_id=1, source_target_pairs={{0,16},{8,24},{16,32},{24,40},{32,48},{40,56},{48,64},{56,72},{64,... | collective-permute-start | bytes 196616 | tf_op jit(solution)/shard_map/ppermute | solution.py:11
  7.4 27.6 %collective-permute-start.1 = (bf16[128,256]{1,0:T(8,128)(2,1)S(1)}, bf16[128,256]{1,0:T(8,128)(2,1)S(1)}, u32[]{:S(2)}, u32[]{:S(2)}) collective-permute-start(bf16[128,256]{1,0:T(8,128)(2,1)S(1)} %fusion.3), channel_id=1, source_target_pairs={{0,8},{8,16},{16,24},{24,32},{32,40},{40,48},{48,56},{56,64},{64,7... | collective-permute-start | bytes 196616 | tf_op jit(solution)/shard_map/ppermute | solution.py:11
  10.6 24.5 %collective-permute-start.2 = (bf16[128,256]{1,0:T(8,128)(2,1)S(1)}, bf16[128,256]{1,0:T(8,128)(2,1)S(1)}, u32[]{:S(2)}, u32[]{:S(2)}) collective-permute-start(bf16[128,256]{1,0:T(8,128)(2,1)S(1)} %fusion.3), channel_id=1, source_target_pairs={{0,504},{8,0},{16,8},{24,16},{32,24},{40,32},{48,40},{56,48},{64,5... | collective-permute-start | bytes 196616 | tf_op jit(solution)/shard_map/ppermute | solution.py:11
  21.1 14.0 %collective-permute-start.3 = (bf16[128,256]{1,0:T(8,128)(2,1)S(1)}, bf16[128,256]{1,0:T(8,128)(2,1)S(1)}, u32[]{:S(2)}, u32[]{:S(2)}) collective-permute-start(bf16[128,256]{1,0:T(8,128)(2,1)S(1)} %fusion.3), channel_id=1, source_target_pairs={{0,496},{8,504},{16,0},{24,8},{32,16},{40,24},{48,32},{56,40},{64,... | collective-permute-start | bytes 196616 | tf_op jit(solution)/shard_map/ppermute | solution.py:11
  28.6 5.5 %copy-start.1 = (bf16[128,256]{1,0:T(8,128)(2,1)S(1)}, bf16[128,256]{1,0:T(8,128)(2,1)}, u32[]{:S(2)}) copy-start(bf16[128,256]{1,0:T(8,128)(2,1)} %param.11) | copy-start | bytes 196612
  28.6 5.5 %copy-start.2 = (bf16[128,256]{1,0:T(8,128)(2,1)S(1)}, bf16[128,256]{1,0:T(8,128)(2,1)}, u32[]{:S(2)}) copy-start(bf16[128,256]{1,0:T(8,128)(2,1)} %param.12) | copy-start | bytes 196612
  28.6 5.5 %copy-start.3 = (bf16[128,256]{1,0:T(8,128)(2,1)S(1)}, bf16[128,256]{1,0:T(8,128)(2,1)}, u32[]{:S(2)}) copy-start(bf16[128,256]{1,0:T(8,128)(2,1)} %param.13) | copy-start | bytes 196612
  37.6 30.9 %all-to-all-start = ((f32[512,1,128]{2,1,0:T(1,128)}), f32[512,1,128]{2,1,0:T(1,128)S(1)}, u32[]{:S(2)}, u32[]{:S(2)}) async-start(f32[512,1,128]{2,1,0:T(1,128)} %bitcast.13), calls=%async_computation | async-start | bytes 524288 | tf_op jit(solution)/shard_map/all_to_all | solution.py:68
  51.7 17.9 %collective-permute-start.4 = (f32[4,128,256]{2,1,0:T(8,128)S(1)}, f32[4,128,256]{2,1,0:T(8,128)}, u32[]{:S(2)}, u32[]{:S(2)}) collective-permute-start(f32[4,128,256]{2,1,0:T(8,128)S(1)} %slice_select_fusion), channel_id=1, source_target_pairs={{0,1},{1,0},{2,3},{3,2},{4,5},{5,4},{6,7},{7,6},{8,9},{9,8},{10,11... | collective-permute-start | bytes 1572872 | tf_op jit(solution)/shard_map/ppermute | solution.py:61
  70.8 15.3 %collective-permute-start.5 = (f32[2,128,256]{2,1,0:T(8,128)S(1)}, f32[2,128,256]{2,1,0:T(8,128)S(1)}, u32[]{:S(2)}, u32[]{:S(2)}) collective-permute-start(f32[2,128,256]{2,1,0:T(8,128)S(1)} %slice_select_fusion.1), channel_id=1, source_target_pairs={{0,6},{1,7},{2,4},{3,5},{4,2},{5,3},{6,0},{7,1},{8,14},{9,15},{10,... | collective-permute-start | bytes 786440 | tf_op jit(solution)/shard_map/ppermute | solution.py:61
  74.6 33.4 %all-to-all-start.1 = ((f32[512,2,128]{2,1,0:T(2,128)}), f32[512,2,128]{2,1,0:T(2,128)S(1)}, u32[]{:S(2)}, u32[]{:S(2)}) async-start(f32[512,2,128]{2,1,0:T(2,128)} %broadcast_in_dim.39), calls=%async_computation.1 | async-start | bytes 1048576 | tf_op jit(solution)/shard_map/all_to_all | solution.py:74
  86.2 14.5 %collective-permute-start.6 = (f32[1,128,256]{2,1,0:T(8,128)S(1)}, f32[1,128,256]{2,1,0:T(8,128)S(1)}, u32[]{:S(2)}, u32[]{:S(2)}) collective-permute-start(f32[1,128,256]{2,1,0:T(8,128)S(1)} %slice_select_fusion.2), channel_id=1, source_target_pairs={{0,2},{1,3},{2,0},{3,1},{4,6},{5,7},{6,4},{7,5},{8,10},{9,11},{10,... | collective-permute-start | bytes 393224 | tf_op jit(solution)/shard_map/ppermute | solution.py:61

commit v15 on v11

--- a/solution.py
+++ b/solution.py
@@ -31,8 +31,10 @@
     )
     sources = (own_block + jnp.array(offsets, jnp.int32)) % blocks
     listed = jnp.take(neighbors[0, 0], sources, axis=0)
-    column_ids = jnp.take(tile_col[0, 0], sources, axis=0)
-    present = jnp.take(tile_count[0, 0], sources, axis=0)
+    slot_table = jnp.take(
+        jnp.concatenate([tile_col[0, 0], tile_count[0, 0][:, None]], axis=1), sources, axis=0
+    )
+    column_ids, present = slot_table[:, :-1], slot_table[:, -1]
     slots_total = listed.shape[1]
     tile_side = listed.shape[3]
     hidden = scaled.shape[1]

time: 101 us -> 99.6 us (0.986)
  local copies, waits for them, and re-layouts: 5.71 us -> 3.92 us
    gather x2 -> x1, local copies, waits for them, and re-layouts: 1.85 us -> 0.55 us  [on_device(): jnp.take(jnp.concatenate([tile_col[0, 0], tile_count[0, 0][:, None]], axi...]
  transfers between devices with their start and end apart: 9 -> 9, of which waited for: 3 -> 3; matrix products, arithmetic and copies ran while one was open for 12% -> 11% of each run, Pallas kernels for 0% -> 0%
where the time goes in v15:
time: 99.6 us; the launch traced here: 99.2 us
  starting transfers between devices  56.8 us (57%)
  waiting for transfers between devices  22.9 us (23%)
  other arithmetic  11.9 us (12%)
  local copies, waits for them, and re-layouts  3.92 us (4%)
  matrix products  1.98 us (2%)
  between operations  1.67 us (2%)
    ppermute x4, starting transfers between devices, fetched_from(): lax.ppermute(x, axis, [(i, (i - offset) % size) for i in range(size)])  21.9 us
    ppermute x3, starting transfers between devices, halved(): lax.ppermute(given, 'rep', [(i, i ^ mask) for i in range(replicas)])  13.4 us
    all_to_all x1, starting transfers between devices, on_device(): lax.all_to_all(local_weight.reshape(devices, -1), ('blk', 'rep'), 0, 0, t...  12.6 us
    all_to_all x1, waiting for transfers between devices, on_device(): lax.all_to_all(local_weight.reshape(devices, -1), ('blk', 'rep'), 0, 0, t...  11 us
    all_to_all x1, starting transfers between devices, on_device(): lax.all_to_all(jnp.broadcast_to(piece, (devices,) + piece.shape), ('blk',...  8.89 us
    ppermute x3, waiting for transfers between devices, halved(): lax.ppermute(given, 'rep', [(i, i ^ mask) for i in range(replicas)])  6.25 us
    all_to_all x1, waiting for transfers between devices, on_device(): lax.all_to_all(jnp.broadcast_to(piece, (devices,) + piece.shape), ('blk',...  5.59 us
    reduce_sum x1, other arithmetic, on_device(): jnp.sum((listed[:, :, :, :, None] == positions[None, None, None, None, :]...  4.21 us
  transfers between devices with their start and end apart: 9, of which 3 were waited for; matrix products, arithmetic and copies ran while one was open for 11% of the time, Pallas kernels for 0%

profile of v15, /device:TPU:1, one launch (start us, length us, event | category | flops | bytes accessed | tf_op | source)
XLA Modules:
  0.0 99.2 jit_solution(6286582055891933797)
XLA Ops:
  0.6 0.7 convert_rsqrt_fusion
  1.4 1.2 %fusion.3 = bf16[128,256]{1,0:T(8,128)(2,1)S(1)} fusion(bf16[256,256]{1,0:T(8,128)(2,1)} %param.12, f32[128]{0:T(128)S(1)} %convert_rsqrt_fusion, bf16[128,256]{1,0:T(8,128)(2,1)} %param.9, bf16[128,256]{1,0:T(8,128)(2,1)} %param.10), kind=kOutput, calls=%fused_computation.10 | convolution fusion | flops 16908288 | bytes 328192 | tf_op jit(solution)/shard_map/dot_general | solution.py:20
  2.6 4.8 %collective-permute-start = (bf16[128,256]{1,0:T(8,128)(2,1)S(1)}, bf16[128,256]{1,0:T(8,128)(2,1)S(1)}, u32[]{:S(2)}, u32[]{:S(2)}) collective-permute-start(bf16[128,256]{1,0:T(8,128)(2,1)S(1)} %fusion.3), channel_id=1, source_target_pairs={{0,16},{8,24},{16,32},{24,40},{32,48},{40,56},{48,64},{56,72},{64,... | collective-permute-start | bytes 196616 | tf_op jit(solution)/shard_map/ppermute | solution.py:11
  7.4 3.2 %collective-permute-start.1 = (bf16[128,256]{1,0:T(8,128)(2,1)S(1)}, bf16[128,256]{1,0:T(8,128)(2,1)S(1)}, u32[]{:S(2)}, u32[]{:S(2)}) collective-permute-start(bf16[128,256]{1,0:T(8,128)(2,1)S(1)} %fusion.3), channel_id=1, source_target_pairs={{0,8},{8,16},{16,24},{24,32},{32,40},{40,48},{48,56},{56,64},{64,7... | collective-permute-start | bytes 196616 | tf_op jit(solution)/shard_map/ppermute | solution.py:11
  10.6 10.5 %collective-permute-start.2 = (bf16[128,256]{1,0:T(8,128)(2,1)S(1)}, bf16[128,256]{1,0:T(8,128)(2,1)S(1)}, u32[]{:S(2)}, u32[]{:S(2)}) collective-permute-start(bf16[128,256]{1,0:T(8,128)(2,1)S(1)} %fusion.3), channel_id=1, source_target_pairs={{0,504},{8,0},{16,8},{24,16},{32,24},{40,32},{48,40},{56,48},{64,5... | collective-permute-start | bytes 196616 | tf_op jit(solution)/shard_map/ppermute | solution.py:11
  21.1 3.4 %collective-permute-start.3 = (bf16[128,256]{1,0:T(8,128)(2,1)S(1)}, bf16[128,256]{1,0:T(8,128)(2,1)S(1)}, u32[]{:S(2)}, u32[]{:S(2)}) collective-permute-start(bf16[128,256]{1,0:T(8,128)(2,1)S(1)} %fusion.3), channel_id=1, source_target_pairs={{0,496},{8,504},{16,0},{24,8},{32,16},{40,24},{48,32},{56,40},{64,... | collective-permute-start | bytes 196616 | tf_op jit(solution)/shard_map/ppermute | solution.py:11
  25.2 0.7 pad_add_fusion
  27.5 4.2 %fusion.1 = bf16[5,4,128,128]{3,2,1,0:T(8,128)(2,1)S(1)} fusion(s32[5,4,8,128]{3,2,1,0:T(8,128)S(1)} %broadcast_select_fusion), kind=kLoop, calls=%fused_computation.4 | loop fusion | flops 7536640 | bytes 737280 | tf_op jit(solution)/shard_map/reduce_sum | solution.py:43
  31.8 1.1 %multiply_reduce_fusion = bf16[5,128,8,128]{3,2,1,0:T(8,128)(2,1)S(1)} fusion(bf16[5,4,128,128]{3,2,1,0:T(8,128)(2,1)S(1)} %fusion.1, bf16[5,4,8]{2,1,0:T(4,128)(2,1)S(1)} %fusion.7), kind=kLoop, calls=%fused_computation.5 | loop fusion | flops 4587520 | bytes 1966400 | tf_op jit(solution)/shard_map/reduce_sum | solution.py:51
  33.8 0.9 slice_select_fusion
  34.6 3.4 %collective-permute-start.4 = (f32[4,128,256]{2,1,0:T(8,128)}, f32[4,128,256]{2,1,0:T(8,128)S(1)}, u32[]{:S(2)}, u32[]{:S(2)}) collective-permute-start(f32[4,128,256]{2,1,0:T(8,128)} %slice_select_fusion), channel_id=1, source_target_pairs={{0,1},{1,0},{2,3},{3,2},{4,5},{5,4},{6,7},{7,6},{8,9},{9,8},{10,11... | collective-permute-start | bytes 1572872 | tf_op jit(solution)/shard_map/ppermute | solution.py:63
  38.4 0.7 all_to_all.10
  39.1 12.6 %all-to-all-start = ((f32[512,1,128]{2,1,0:T(1,128)}), f32[512,1,128]{2,1,0:T(1,128)S(1)}, u32[]{:S(2)}, u32[]{:S(2)}) async-start(f32[512,1,128]{2,1,0:T(1,128)} %bitcast.13), calls=%async_computation | async-start | bytes 524288 | tf_op jit(solution)/shard_map/all_to_all | solution.py:70
  51.9 5.7 %collective-permute-start.5 = (f32[2,128,256]{2,1,0:T(8,128)S(1)}, f32[2,128,256]{2,1,0:T(8,128)S(1)}, u32[]{:S(2)}, u32[]{:S(2)}) collective-permute-start(f32[2,128,256]{2,1,0:T(8,128)S(1)} %slice_select_fusion.1), channel_id=1, source_target_pairs={{0,6},{1,7},{2,4},{3,5},{4,2},{5,3},{6,0},{7,1},{8,14},{9,15},{10,... | collective-permute-start | bytes 786440 | tf_op jit(solution)/shard_map/ppermute | solution.py:63
  57.6 11.0 %all-to-all-done = f32[512,1,128]{2,1,0:T(1,128)S(1)} async-done(((f32[512,1,128]{2,1,0:T(1,128)}), f32[512,1,128]{2,1,0:T(1,128)S(1)}, u32[]{:S(2)}, u32[]{:S(2)}) %all-to-all-start) | async-done | bytes 262176 | tf_op jit(solution)/shard_map/all_to_all | solution.py:70
  69.2 0.8 broadcast_in_dim.35
  70.0 8.9 %all-to-all-start.1 = ((f32[512,1,128]{2,1,0:T(1,128)}), f32[512,1,128]{2,1,0:T(1,128)S(1)}, u32[]{:S(2)}, u32[]{:S(2)}) async-start(f32[512,1,128]{2,1,0:T(1,128)} %broadcast_in_dim.35), calls=%async_computation.1 | async-start | bytes 524288 | tf_op jit(solution)/shard_map/all_to_all | solution.py:74
  79.0 4.3 %collective-permute-start.6 = (f32[1,128,256]{2,1,0:T(8,128)S(1)}, f32[1,128,256]{2,1,0:T(8,128)S(1)}, u32[]{:S(2)}, u32[]{:S(2)}) collective-permute-start(f32[1,128,256]{2,1,0:T(8,128)S(1)} %slice_select_fusion.2), channel_id=1, source_target_pairs={{0,2},{1,3},{2,0},{3,1},{4,6},{5,7},{6,4},{7,5},{8,10},{9,11},{10,... | collective-permute-start | bytes 393224 | tf_op jit(solution)/shard_map/ppermute | solution.py:63
  83.3 6.2 %collective-permute-done.6 = f32[1,128,256]{2,1,0:T(8,128)S(1)} collective-permute-done((f32[1,128,256]{2,1,0:T(8,128)S(1)}, f32[1,128,256]{2,1,0:T(8,128)S(1)}, u32[]{:S(2)}, u32[]{:S(2)}) %collective-permute-start.6) | collective-permute-done | bytes 131104 | tf_op jit(solution)/shard_map/ppermute | solution.py:63
  89.6 0.7 fusion.5
  90.3 5.6 %all-to-all-done.1 = f32[512,1,128]{2,1,0:T(1,128)S(1)} async-done(((f32[512,1,128]{2,1,0:T(1,128)}), f32[512,1,128]{2,1,0:T(1,128)S(1)}, u32[]{:S(2)}, u32[]{:S(2)}) %all-to-all-start.1) | async-done | bytes 262176 | tf_op jit(solution)/shard_map/all_to_all | solution.py:74
  95.9 1.1 %multiply_reduce_fusion.2 = f32[]{:T(128)} fusion(f32[512,1,128]{2,1,0:T(1,128)S(1)} %all-to-all-done.1), kind=kLoop, calls=%fused_computation.15 | loop fusion | flops 131071 | bytes 262148 | tf_op jit(solution)/shard_map/reduce_sum | solution.py:77
  97.7 0.7 multiply_reduce_fusion.1
  98.4 0.8 mul.50
  (37 shorter events, 4.2 us)
Async XLA Ops:
  0.6 26.3 %copy-start = (s32[1,1,64,4,8,128]{5,4,3,2,1,0:T(8,128)S(1)}, s32[1,1,64,4,8,128]{5,4,3,2,1,0:T(8,128)}, u32[]{:S(2)}) copy-start(s32[1,1,64,4,8,128]{5,4,3,2,1,0:T(8,128)} %param.14) | copy-start | bytes 3145732
  2.6 30.4 %collective-permute-start = (bf16[128,256]{1,0:T(8,128)(2,1)S(1)}, bf16[128,256]{1,0:T(8,128)(2,1)S(1)}, u32[]{:S(2)}, u32[]{:S(2)}) collective-permute-start(bf16[128,256]{1,0:T(8,128)(2,1)S(1)} %fusion.3), channel_id=1, source_target_pairs={{0,16},{8,24},{16,32},{24,40},{32,48},{40,56},{48,64},{56,72},{64,... | collective-permute-start | bytes 196616 | tf_op jit(solution)/shard_map/ppermute | solution.py:11
  7.4 25.6 %collective-permute-start.1 = (bf16[128,256]{1,0:T(8,128)(2,1)S(1)}, bf16[128,256]{1,0:T(8,128)(2,1)S(1)}, u32[]{:S(2)}, u32[]{:S(2)}) collective-permute-start(bf16[128,256]{1,0:T(8,128)(2,1)S(1)} %fusion.3), channel_id=1, source_target_pairs={{0,8},{8,16},{16,24},{24,32},{32,40},{40,48},{48,56},{56,64},{64,7... | collective-permute-start | bytes 196616 | tf_op jit(solution)/shard_map/ppermute | solution.py:11
  10.6 22.4 %collective-permute-start.2 = (bf16[128,256]{1,0:T(8,128)(2,1)S(1)}, bf16[128,256]{1,0:T(8,128)(2,1)S(1)}, u32[]{:S(2)}, u32[]{:S(2)}) collective-permute-start(bf16[128,256]{1,0:T(8,128)(2,1)S(1)} %fusion.3), channel_id=1, source_target_pairs={{0,504},{8,0},{16,8},{24,16},{32,24},{40,32},{48,40},{56,48},{64,5... | collective-permute-start | bytes 196616 | tf_op jit(solution)/shard_map/ppermute | solution.py:11
  21.1 11.9 %collective-permute-start.3 = (bf16[128,256]{1,0:T(8,128)(2,1)S(1)}, bf16[128,256]{1,0:T(8,128)(2,1)S(1)}, u32[]{:S(2)}, u32[]{:S(2)}) collective-permute-start(bf16[128,256]{1,0:T(8,128)(2,1)S(1)} %fusion.3), channel_id=1, source_target_pairs={{0,496},{8,504},{16,0},{24,8},{32,16},{40,24},{48,32},{56,40},{64,... | collective-permute-start | bytes 196616 | tf_op jit(solution)/shard_map/ppermute | solution.py:11
  33.7 4.3 %copy-start.1 = (bf16[128,256]{1,0:T(8,128)(2,1)S(1)}, bf16[128,256]{1,0:T(8,128)(2,1)}, u32[]{:S(2)}) copy-start(bf16[128,256]{1,0:T(8,128)(2,1)} %param.9) | copy-start | bytes 196612
  33.7 4.3 %copy-start.2 = (bf16[128,256]{1,0:T(8,128)(2,1)S(1)}, bf16[128,256]{1,0:T(8,128)(2,1)}, u32[]{:S(2)}) copy-start(bf16[128,256]{1,0:T(8,128)(2,1)} %param.10) | copy-start | bytes 196612
  33.7 4.3 %copy-start.3 = (bf16[128,256]{1,0:T(8,128)(2,1)S(1)}, bf16[128,256]{1,0:T(8,128)(2,1)}, u32[]{:S(2)}) copy-start(bf16[128,256]{1,0:T(8,128)(2,1)} %param.11) | copy-start | bytes 196612
  34.6 17.2 %collective-permute-start.4 = (f32[4,128,256]{2,1,0:T(8,128)}, f32[4,128,256]{2,1,0:T(8,128)S(1)}, u32[]{:S(2)}, u32[]{:S(2)}) collective-permute-start(f32[4,128,256]{2,1,0:T(8,128)} %slice_select_fusion), channel_id=1, source_target_pairs={{0,1},{1,0},{2,3},{3,2},{4,5},{5,4},{6,7},{7,6},{8,9},{9,8},{10,11... | collective-permute-start | bytes 1572872 | tf_op jit(solution)/shard_map/ppermute | solution.py:63
  39.1 29.5 %all-to-all-start = ((f32[512,1,128]{2,1,0:T(1,128)}), f32[512,1,128]{2,1,0:T(1,128)S(1)}, u32[]{:S(2)}, u32[]{:S(2)}) async-start(f32[512,1,128]{2,1,0:T(1,128)} %bitcast.13), calls=%async_computation | async-start | bytes 524288 | tf_op jit(solution)/shard_map/all_to_all | solution.py:70
  51.9 27.0 %collective-permute-start.5 = (f32[2,128,256]{2,1,0:T(8,128)S(1)}, f32[2,128,256]{2,1,0:T(8,128)S(1)}, u32[]{:S(2)}, u32[]{:S(2)}) collective-permute-start(f32[2,128,256]{2,1,0:T(8,128)S(1)} %slice_select_fusion.1), channel_id=1, source_target_pairs={{0,6},{1,7},{2,4},{3,5},{4,2},{5,3},{6,0},{7,1},{8,14},{9,15},{10,... | collective-permute-start | bytes 786440 | tf_op jit(solution)/shard_map/ppermute | solution.py:63
  70.0 25.9 %all-to-all-start.1 = ((f32[512,1,128]{2,1,0:T(1,128)}), f32[512,1,128]{2,1,0:T(1,128)S(1)}, u32[]{:S(2)}, u32[]{:S(2)}) async-start(f32[512,1,128]{2,1,0:T(1,128)} %broadcast_in_dim.35), calls=%async_computation.1 | async-start | bytes 524288 | tf_op jit(solution)/shard_map/all_to_all | solution.py:74
  79.0 10.6 %collective-permute-start.6 = (f32[1,128,256]{2,1,0:T(8,128)S(1)}, f32[1,128,256]{2,1,0:T(8,128)S(1)}, u32[]{:S(2)}, u32[]{:S(2)}) collective-permute-start(f32[1,128,256]{2,1,0:T(8,128)S(1)} %slice_select_fusion.2), channel_id=1, source_target_pairs={{0,2},{1,3},{2,0},{3,1},{4,6},{5,7},{6,4},{7,5},{8,10},{9,11},{10,... | collective-permute-start | bytes 393224 | tf_op jit(solution)/shard_map/ppermute | solution.py:63
